TPU v7x, 256 devices: a whole 4x4x8 slice. The times are simulated.
256 devices in a mesh: lon: 32 (over y_hi, z, core), lat: 8 (over x, y_lo).
Axes of the slice: x: 4, y: 4 (y_hi: 2, y_lo: 2; y = y_hi * 2 + y_lo), z: 8, core: 2. Of those that a mesh axis runs over, the one named last changes fastest.
Arguments:
- trajectory: float32 [2, 512, 512, 128], P(None, 'lon', 'lat'), may hold values from -4 to 4
- cotangent: float32 [8, 512, 512, 128], P(None, 'lon', 'lat'), may hold values from -6 to 6
- courant: float32 [2, 512, 512, 128], P(None, 'lon', 'lat'), may hold values from -0.5 to 0.5
- branch: int32 [512, 512, 128], P('lon', 'lat'), may hold values from 0 to 3
- cloud_list: int32 [32, 8, 768], P('lon', 'lat'), may hold values from 0 to 1023, as said below
- cloud_count: int32 [32, 8], P('lon', 'lat'), may hold values from 0 to 768, as said below
Outputs:
- adjoint_state: float32 [8, 512, 512, 128], P(None, 'lon', 'lat')
Inputs may be any that keep to these rules, and one draw needn't show every extreme that they name: `cloud_count`: for every lat index, the counts of the 32 devices of that lon cycle add up to 8192. `cloud_list`: each device's entries are distinct local column numbers.
All inputs are finite; a program needn't handle non-finite values.
Results may differ from a plain program's by a relative error of at most 0.0003.
Values sent between devices are 32-bit elements; how exact they have to be, the bound alone decides.
No kernel may reach another device: no remote copies, remote signals or barrier semaphores. Data moves between devices by JAX's collectives and lax.ppermute only.
A program may use at most 64 MiB of HBM per device.

v0:
```python
import jax
import jax.numpy as jnp
from jax import lax
from jax.sharding import PartitionSpec as P

NEWT = 4
BLOCK = 256


growth = 0.5
latent_liquid = 1.0
latent_ice = 1.3


def with_halo(block, sides, width, periodic):
    for axis, dim in sides:
        count = lax.axis_size(axis)
        forward = [(i, i + 1) for i in range(count - 1)]
        if periodic:
            forward.append((count - 1, 0))
        backward = [(target, source) for source, target in forward]
        low = lax.ppermute(
            lax.slice_in_dim(block, block.shape[dim] - width, None, axis=dim), axis, forward
        )
        high = lax.ppermute(lax.slice_in_dim(block, 0, width, axis=dim), axis, backward)
        block = jnp.concatenate([low, block, high], axis=dim)
    return block


def increments(warmth, vapour, kinds):
    mixed = jax.nn.sigmoid(2.0 * warmth)
    liquid_share = jnp.where(kinds == 1, 1.0, jnp.where(kinds == 2, 0.0, mixed))
    latent = latent_liquid * liquid_share + latent_ice * (1.0 - liquid_share)
    active = (kinds > 0).astype(warmth.dtype)
    amount = jnp.zeros_like(warmth)
    for newton_step in range(NEWT):
        saturated = jnp.exp(growth * (warmth + latent * amount))
        excess = vapour - amount - saturated
        amount = amount + excess / (1.0 + growth * latent * saturated)
    amount = active * amount
    return (latent * amount, -amount, liquid_share * amount, (1.0 - liquid_share) * amount)


def sat_adjoint(warmth, vapour, kinds, cot_heat, cot_vapour, cot_liquid, cot_ice):

    def forward(first_in, second_in):
        return increments(first_in, second_in, kinds)

    unused, pullback = jax.vjp(forward, warmth, vapour)
    grad_heat, grad_vapour = pullback((cot_heat, cot_vapour, cot_liquid, cot_ice))
    return (cot_heat + grad_heat, cot_vapour + grad_vapour)


def centred(padded, dim, count):

    def part(start):
        return lax.slice_in_dim(padded, start, start + count, axis=dim)

    return (8.0 * (part(3) - part(1)) - (part(4) - part(0))) / 12.0


def solve_blocks(states, kinds, moist, live):
    trips = (live + BLOCK - 1) // BLOCK

    def advance(turn, solved):
        offset = turn * BLOCK
        block_state = lax.dynamic_slice_in_dim(states, offset, BLOCK, 1)
        block_kind = lax.dynamic_slice_in_dim(kinds, offset, BLOCK, 0)
        block_moist = lax.dynamic_slice_in_dim(moist, offset, BLOCK, 1)
        new_heat, new_vapour = sat_adjoint(
            block_state[0],
            block_state[1],
            block_kind,
            block_moist[0],
            block_moist[1],
            block_moist[2],
            block_moist[3],
        )
        return lax.dynamic_update_slice_in_dim(solved, jnp.stack([new_heat, new_vapour]), offset, 1)

    return lax.fori_loop(0, trips, advance, moist[:2])


def on_device(trajectory, cotangent, courant, branch, cloud_list, cloud_count):
    fields, local_lon, local_lat, levels = cotangent.shape
    columns = local_lon * local_lat
    index = cloud_list[0, 0]
    count = cloud_count[0, 0]
    capacity = index.shape[0]
    flat_cot = cotangent[:4].reshape(4, columns, levels)
    flat_state = trajectory.reshape(2, columns, levels)
    flat_kind = branch.reshape(columns, levels)
    slot_cot = jnp.take(flat_cot, index, axis=1)
    slot_number = jnp.arange(capacity, dtype=jnp.int32)
    slot_state = jnp.take(flat_state, index, axis=1)
    slot_kind = jnp.take(flat_kind, index, axis=0)
    results = solve_blocks(slot_state, slot_kind, slot_cot, count)
    live_slot = jnp.where(slot_number < count, slot_number, capacity)
    slot_of = jnp.full((columns,), capacity, jnp.int32).at[index].set(live_slot)
    fetched = jnp.take(results, jnp.minimum(slot_of, capacity - 1), axis=1)
    chosen = jnp.where((slot_of < capacity)[None, :, None], fetched, flat_cot[:2])
    first = chosen.reshape(2, local_lon, local_lat, levels)
    after = jnp.concatenate([first, cotangent[2:]], 0)
    weighted_lon = courant[0] * after
    weighted_lat = courant[1] * after
    lon_part = with_halo(weighted_lon, (("lon", 1),), 2, True)
    lat_part = with_halo(weighted_lat, (("lat", 2),), 2, False)
    return after + centred(lon_part, 1, local_lon) + centred(lat_part, 2, local_lat)


def solution(mesh):
    placed = (
        P(None, "lon", "lat", None),
        P(None, "lon", "lat", None),
        P(None, "lon", "lat", None),
        P("lon", "lat", None),
        P("lon", "lat", None),
        P("lon", "lat"),
    )
    return jax.shard_map(
        on_device,
        mesh=mesh,
        in_specs=placed,
        out_specs=P(None, "lon", "lat", None),
        check_vma=False,
    )
```

profile of v0, /device:TPU:2, one launch (start us, length us, event | category | flops | bytes accessed | tf_op | source)
XLA Modules:
  0.0 81.1 jit_solution(6224660036658259878)
XLA Ops:
  0.7 0.7 fusion.45
  1.4 3.4 %scatter_custom_fusion = s32[1024]{0:T(1024)S(1)} fusion(s32[768]{0:T(1024)S(1)} %fusion.45, s32[768]{0:T(1024)S(1)} %iota_select_fusion, s32[]{:T(128)} %constant.140.clone.1), kind=kCustom, calls=%fused_computation.115 | custom fusion | bytes 4100 | tf_op jit(solution)/shard_map/scatter | solution.py:99
  4.9 0.7 reduce.1
  5.6 2.2 %copy-done.2 = f32[8,16,64,128]{3,2,1,0:T(8,128)S(1)} copy-done((f32[8,16,64,128]{3,2,1,0:T(8,128)S(1)}, f32[8,16,64,128]{3,2,1,0:T(8,128)}, u32[]{:S(2)}) %copy-start.2) | copy-done | bytes 4194328
  7.8 1.9 %slice.103 = f32[6,16,64,128]{3,2,1,0:T(8,128)} slice(f32[8,16,64,128]{3,2,1,0:T(8,128)S(1)} %copy-done.2), slice={[2:8], [0:16], [0:64], [0:128]} | slice | bytes 6291456 | tf_op jit(solution)/shard_map/slice | solution.py:103
  9.8 1.8 %copy.8 = f32[2,16,64,128]{3,0,2,1:T(2,128)} copy(f32[2,16,64,128]{3,2,1,0:T(8,128)S(1)} %copy-done.5) | data formatting | bytes 2097152 | tf_op args[0]
  11.6 1.6 %gather_fusion.1 = s32[768,128]{1,0:T(8,128)S(1)} fusion(s32[1024,128]{1,0:T(8,128)S(1)} %bitcast.58, s32[1024]{0:T(1024)S(1)} %pad_clamp_fusion), kind=kCustom, calls=%fused_computation.1 | custom fusion | bytes 789504 | tf_op jit(solution)/shard_map/jit(_take)/gather | solution.py:96
  13.2 4.1 %gather_fusion.2 = f32[768,2,128]{2,1,0:T(2,128)} fusion(f32[2,1024,128]{2,0,1:T(2,128)} %bitcast.73, s32[1024]{0:T(1024)S(1)} %pad_clamp_fusion), kind=kCustom, calls=%fused_computation.2 | custom fusion | bytes 1575936 | tf_op jit(solution)/shard_map/jit(_take)/gather | solution.py:95
  17.2 0.9 %broadcast_select_fusion = s32[768,128]{1,0:T(8,128)} fusion(s32[768,128]{1,0:T(8,128)S(1)} %gather_fusion.1, pred[768]{0:T(1024)(128)(4,1)S(1)} %compare_and_fusion), kind=kLoop, calls=%fused_computation.103 | loop fusion | flops 98304 | bytes 787200 | tf_op jit(solution)/shard_map/jit(_take)/select_n | solution.py:96
  18.2 3.9 %select_bitcast_fusion.1 = f32[2,768,128]{2,0,1:T(2,128)S(1)} fusion(f32[768,2,128]{2,1,0:T(2,128)} %gather_fusion.2, pred[768]{0:T(1024)(128)(4,1)S(1)} %compare_and_fusion), kind=kLoop, calls=%fused_computation.100 | loop fusion | flops 196608 | bytes 1573632 | tf_op jit(solution)/shard_map/jit(_take)/select_n | solution.py:95
  22.1 2.3 %slice_bitcast_fusion.1 = (f32[16,64,128]{2,1,0:T(8,128)}, f32[16,64,128]{2,1,0:T(8,128)}) fusion(f32[2,16,64,128]{3,2,1,0:T(8,128)} %param.10), kind=kLoop, calls=%fused_computation.102 | loop fusion | bytes 2097152 | tf_op jit(solution)/shard_map/mul | solution.py:104
  24.4 2.7 %copy.7 = f32[4,16,64,128]{3,0,2,1:T(4,128)} copy(f32[4,16,64,128]{3,2,1,0:T(8,128)S(1)} %slice-done) | data formatting | bytes 4194304 | tf_op jit(solution)/shard_map/slice | solution.py:90
  27.1 4.7 %gather_fusion = f32[768,4,128]{2,1,0:T(4,128)} fusion(f32[4,1024,128]{2,0,1:T(4,128)} %bitcast.71, s32[1024]{0:T(1024)S(1)} %pad_clamp_fusion), kind=kCustom, calls=%fused_computation | custom fusion | bytes 3148800 | tf_op jit(solution)/shard_map/jit(_take)/gather | solution.py:93
  31.8 4.1 %select_bitcast_fusion = f32[4,768,128]{2,0,1:T(4,128)S(1)} fusion(f32[768,4,128]{2,1,0:T(4,128)} %gather_fusion, pred[768]{0:T(1024)(128)(4,1)S(1)} %compare_and_fusion), kind=kLoop, calls=%fused_computation.97 | loop fusion | flops 393216 | bytes 3146496 | tf_op jit(solution)/shard_map/jit(_take)/select_n | solution.py:93
  35.9 1.2 %slice.126 = f32[2,768,128]{2,0,1:T(2,128)} slice(f32[4,768,128]{2,0,1:T(4,128)S(1)} %select_bitcast_fusion), slice={[0:2], [0:768], [0:128]} | slice | bytes 1572864 | tf_op jit(solution)/shard_map/slice | solution.py:81
  37.0 8.0 %while.12 = (s32[]{:T(128)}, f32[2,768,128]{2,0,1:T(2,128)}, s32[]{:T(128)}, f32[4,768,128]{2,0,1:T(4,128)S(1)}, s32[768,128]{1,0:T(8,128)}, /*index=5*/f32[2,76...) while((s32[]{:T(128)}, f32[2,768,128]{2,0,1:T(2,128)}, ...), condition=%wide.region_2.3_spmd, body=%wide.region_1.2_spmd.sunk | while | flops 8126473 | bytes 4784359 | solution.py:81
  37.0 0.7 constant_dynamic-slice_fusion.7
  37.7 1.8 %fusion.51 = (f32[1,256,128]{2,1,0:T(8,128)S(1)}, pred[256,128]{1,0:T(8,128)(4,1)S(1)}, pred[256,128]{1,0:T(8,128)(4,1)S(1)}, pred[256,128]{1,0:T(8,128)(4,1)S(1)}) fusion(f32[256,128]{1,0:T(8,128)S(1)} %bitcast.63, f32[256,128]{1,0:T(8,128)S(1)} %bitcast.61, f32[256,128]{1,0:T(8,128)S(1)} %bitcast.59, f32[256,128]{1,0:T(8,128)S(1)} %bitcast.67, ...), kind=kLoop, calls=%fused_computation.12.clone.1 | loop fusion | flops 4882432 | bytes 1146884 | tf_op jit(solution)/shard_map/while/body/stack | solution.py:79
  39.5 0.6 add_bitcast_fusion.2
  40.1 0.9 %copy_dynamic-update-slice_fusion.2 = f32[2,768,128]{2,0,1:T(2,128)} fusion(f32[2,768,128]{2,0,1:T(2,128)} %get-tuple-element.198, s32[]{:T(128)S(6)} %select_n.148, f32[2,256,128]{2,1,0:T(8,128)S(1)} %pad_maximum_fusion.7), kind=kLoop, calls=%fused_computation.6.clone.1 | loop fusion | bytes 524292 | tf_op jit(solution)/shard_map/while/body/dynamic_update_slice | solution.py:79
  41.1 0.7 constant_dynamic-slice_fusion.7
  41.7 1.8 %fusion.51 = (f32[1,256,128]{2,1,0:T(8,128)S(1)}, pred[256,128]{1,0:T(8,128)(4,1)S(1)}, pred[256,128]{1,0:T(8,128)(4,1)S(1)}, pred[256,128]{1,0:T(8,128)(4,1)S(1)}) fusion(f32[256,128]{1,0:T(8,128)S(1)} %bitcast.63, f32[256,128]{1,0:T(8,128)S(1)} %bitcast.61, f32[256,128]{1,0:T(8,128)S(1)} %bitcast.59, f32[256,128]{1,0:T(8,128)S(1)} %bitcast.67, ...), kind=kLoop, calls=%fused_computation.12.clone.1 | loop fusion | flops 4882432 | bytes 1146884 | tf_op jit(solution)/shard_map/while/body/stack | solution.py:79
  43.5 0.6 add_bitcast_fusion.2
  44.2 0.9 %copy_dynamic-update-slice_fusion.2 = f32[2,768,128]{2,0,1:T(2,128)} fusion(f32[2,768,128]{2,0,1:T(2,128)} %get-tuple-element.198, s32[]{:T(128)S(6)} %select_n.148, f32[2,256,128]{2,1,0:T(8,128)S(1)} %pad_maximum_fusion.7), kind=kLoop, calls=%fused_computation.6.clone.1 | loop fusion | bytes 524292 | tf_op jit(solution)/shard_map/while/body/dynamic_update_slice | solution.py:79
  45.1 4.8 %gather_fusion.3 = f32[1024,2,128]{2,1,0:T(2,128)S(1)} fusion(f32[2,768,128]{2,0,1:T(2,128)} %get-tuple-element.85, s32[1024]{0:T(1024)S(1)} %fusion.44), kind=kCustom, calls=%fused_computation.3 | custom fusion | bytes 2101248 | tf_op jit(solution)/shard_map/jit(_take)/gather | solution.py:100
  49.9 1.7 %fusion.43 = f32[2,16,64,128]{3,2,1,0:T(8,128)S(1)} fusion(f32[2,16,64,128]{3,0,2,1:T(2,128)S(1)} %bitcast.72, f32[8,16,64,128]{3,2,1,0:T(8,128)} %param.9, pred[16,64]{1,0:T(8,128)(4,1)S(1)} %broadcast_in_dim.82, pred[16,64]{1,0:T(8,128)(4,1)S(1)} %broadcast_in_dim.80), kind=kLoop, calls=%fused_computation.99 | loop fusion | flops 524288 | bytes 3147776 | tf_op jit(solution)/shard_map/jit(_where)/select_n | solution.py:101
  51.5 0.5 copy-done.1
  52.1 1.6 %fusion.42 = (f32[8,16,64,128]{3,2,1,0:T(8,128)S(1)}, f32[8,16,64,128]{3,2,1,0:T(8,128)S(1)}) fusion(f32[6,16,64,128]{3,2,1,0:T(8,128)S(1)} %copy-done.1, f32[2,16,64,128]{3,2,1,0:T(8,128)S(1)} %fusion.43, f32[16,64,128]{2,1,0:T(8,128)S(1)} %copy-done.3, f32[16,64,128]{2,1,0:T(8,128)S(1)} %copy-done.4), kind=kLoop, calls=%fused_computation.96 | loop fusion | flops 3145728 | bytes 13631488 | tf_op jit(solution)/shard_map/mul | solution.py:104
  54.5 5.9 %collective-permute-start.2 = (f32[8,16,2,128]{3,2,1,0:T(2,128)S(1)}, f32[8,16,2,128]{3,2,1,0:T(2,128)S(1)}, u32[]{:S(2)}, u32[]{:S(2)}) collective-permute-start(f32[8,16,2,128]{3,2,1,0:T(2,128)S(1)} %get-tuple-element.120), channel_id=1, source_target_pairs={{1,0},{2,1},{3,2},{4,3},{5,4},{6,5},{7,6},{9,8},{10,9},{11,10},{12... | collective-permute-start | bytes 393224 | tf_op jit(solution)/shard_map/ppermute | solution.py:25
  60.4 6.0 %collective-permute-start.3 = (f32[8,16,2,128]{3,2,1,0:T(2,128)S(1)}, f32[8,16,2,128]{3,2,1,0:T(2,128)S(1)}, u32[]{:S(2)}, u32[]{:S(2)}) collective-permute-start(f32[8,16,2,128]{3,2,1,0:T(2,128)S(1)} %get-tuple-element.121), channel_id=1, source_target_pairs={{0,1},{1,2},{2,3},{3,4},{4,5},{5,6},{6,7},{8,9},{9,10},{10,11},{11... | collective-permute-start | bytes 393224 | tf_op jit(solution)/shard_map/ppermute | solution.py:22
  66.4 8.0 %collective-permute-done.2 = f32[8,16,2,128]{3,2,1,0:T(2,128)S(1)} collective-permute-done((f32[8,16,2,128]{3,2,1,0:T(2,128)S(1)}, f32[8,16,2,128]{3,2,1,0:T(2,128)S(1)}, u32[]{:S(2)}, u32[]{:S(2)}) %collective-permute-start.2) | collective-permute-done | bytes 131104 | tf_op jit(solution)/shard_map/ppermute | solution.py:25
  74.4 6.6 %fusion.30 = f32[8,16,64,128]{3,2,1,0:T(8,128)} fusion(f32[8,16,2,128]{3,2,1,0:T(2,128)S(1)} %collective-permute-done.3, f32[8,16,64,128]{3,2,1,0:T(8,128)S(1)} %get-tuple-element.119, f32[8,16,2,128]{3,2,1,0:T(2,128)S(1)} %collective-permute-done.2, f32[8,2,64,128]{3,2,1,0:T(8,128)S(1)} %collective-permute-done.1, ...), kind=kLoop, calls=%fused_computation.79 | loop fusion | flops 22020096 | bytes 18087936 | tf_op jit(solution)/shard_map/add | solution.py:108
  (28 shorter events, 1.1 us)
Async XLA Ops:
  0.0 11.6 %copy-start = (s32[16,64,128]{2,1,0:T(8,128)S(1)}, s32[16,64,128]{2,1,0:T(8,128)}, u32[]{:S(2)}) copy-start(s32[16,64,128]{2,1,0:T(8,128)} %param.11) | copy-start | bytes 1572868
  5.6 2.2 %copy-start.2 = (f32[8,16,64,128]{3,2,1,0:T(8,128)S(1)}, f32[8,16,64,128]{3,2,1,0:T(8,128)}, u32[]{:S(2)}) copy-start(f32[8,16,64,128]{3,2,1,0:T(8,128)} %param.9) | copy-start | bytes 12582916
  7.8 2.1 %copy-start.5 = (f32[2,16,64,128]{3,2,1,0:T(8,128)S(1)}, f32[2,16,64,128]{3,2,1,0:T(8,128)}, u32[]{:S(2)}) copy-start(f32[2,16,64,128]{3,2,1,0:T(8,128)} %param.8) | copy-start | bytes 3145732
  11.6 12.8 %slice-start = ((f32[8,16,64,128]{3,2,1,0:T(8,128)}), f32[4,16,64,128]{3,2,1,0:T(8,128)S(1)}, s32[]{:S(2)}) async-start(f32[8,16,64,128]{3,2,1,0:T(8,128)} %param.9), calls=%async_computation | async-start | bytes 4194304 | tf_op jit(solution)/shard_map/slice | solution.py:90
  45.1 6.4 %copy-start.3 = (f32[16,64,128]{2,1,0:T(8,128)S(1)}, f32[16,64,128]{2,1,0:T(8,128)}, u32[]{:S(2)}) copy-start(f32[16,64,128]{2,1,0:T(8,128)} %get-tuple-element.122) | copy-start | bytes 1572868
  45.1 6.5 %copy-start.4 = (f32[16,64,128]{2,1,0:T(8,128)S(1)}, f32[16,64,128]{2,1,0:T(8,128)}, u32[]{:S(2)}) copy-start(f32[16,64,128]{2,1,0:T(8,128)} %get-tuple-element.123) | copy-start | bytes 1572868
  49.9 2.2 %copy-start.1 = (f32[6,16,64,128]{3,2,1,0:T(8,128)S(1)}, f32[6,16,64,128]{3,2,1,0:T(8,128)}, u32[]{:S(2)}) copy-start(f32[6,16,64,128]{3,2,1,0:T(8,128)} %slice.103) | copy-start | bytes 9437188
  53.8 20.7 %collective-permute-start = (f32[8,2,64,128]{3,2,1,0:T(8,128)S(1)}, f32[8,2,64,128]{3,2,1,0:T(8,128)S(1)}, u32[]{:S(2)}, u32[]{:S(2)}) collective-permute-start(f32[8,2,64,128]{3,2,1,0:T(8,128)S(1)} %get-tuple-element.116), channel_id=1, source_target_pairs={{8,0},{16,8},{24,16},{32,24},{40,32},{48,40},{56,48},{64,56},{72,6... | collective-permute-start | bytes 1572872 | tf_op jit(solution)/shard_map/ppermute | solution.py:25
  53.8 20.6 %collective-permute-start.1 = (f32[8,2,64,128]{3,2,1,0:T(8,128)S(1)}, f32[8,2,64,128]{3,2,1,0:T(8,128)S(1)}, u32[]{:S(2)}, u32[]{:S(2)}) collective-permute-start(f32[8,2,64,128]{3,2,1,0:T(8,128)S(1)} %get-tuple-element.117), channel_id=1, source_target_pairs={{0,8},{8,16},{16,24},{24,32},{32,40},{40,48},{48,56},{56,64},{64,7... | collective-permute-start | bytes 1572872 | tf_op jit(solution)/shard_map/ppermute | solution.py:22
  54.5 20.0 %collective-permute-start.2 = (f32[8,16,2,128]{3,2,1,0:T(2,128)S(1)}, f32[8,16,2,128]{3,2,1,0:T(2,128)S(1)}, u32[]{:S(2)}, u32[]{:S(2)}) collective-permute-start(f32[8,16,2,128]{3,2,1,0:T(2,128)S(1)} %get-tuple-element.120), channel_id=1, source_target_pairs={{1,0},{2,1},{3,2},{4,3},{5,4},{6,5},{7,6},{9,8},{10,9},{11,10},{12... | collective-permute-start | bytes 393224 | tf_op jit(solution)/shard_map/ppermute | solution.py:25
  60.4 14.0 %collective-permute-start.3 = (f32[8,16,2,128]{3,2,1,0:T(2,128)S(1)}, f32[8,16,2,128]{3,2,1,0:T(2,128)S(1)}, u32[]{:S(2)}, u32[]{:S(2)}) collective-permute-start(f32[8,16,2,128]{3,2,1,0:T(2,128)S(1)} %get-tuple-element.121), channel_id=1, source_target_pairs={{0,1},{1,2},{2,3},{3,4},{4,5},{5,6},{6,7},{8,9},{9,10},{10,11},{11... | collective-permute-start | bytes 393224 | tf_op jit(solution)/shard_map/ppermute | solution.py:22
where the time goes:
time: 81.7 us; the launch traced here: 81.1 us
  local copies, waits for them, and re-layouts  34.6 us (42%)
  other arithmetic  25 us (31%)
  starting transfers between devices  12.5 us (15%)
  waiting for transfers between devices  8.03 us (10%)
  between operations  0.9 us (1%)
    ppermute x2, waiting for transfers between devices, with_halo(): lax.ppermute(lax.slice_in_dim(block, 0, width, axis=dim), axis, backward)  8.03 us
    add x1, other arithmetic, on_device(): after + centred(lon_part, 1, local_lon) + centred(lat_part, 2, local_lat)  6.63 us
    ppermute x2, starting transfers between devices, with_halo(): lax.ppermute(lax.slice_in_dim(block, block.shape[dim] - width, None, axis...  6.48 us
    ppermute x2, starting transfers between devices, with_halo(): lax.ppermute(lax.slice_in_dim(block, 0, width, axis=dim), axis, backward)  6.03 us
    another operation x6, other arithmetic, advance(): jnp.stack([new_heat, new_vapour])  4.82 us
    gather x1, local copies, waits for them, and re-layouts, on_device(): fetched = jnp.take(results, jnp.minimum(slot_of, capacity - 1), axis=1)  4.76 us
    gather x1, local copies, waits for them, and re-layouts, on_device(): slot_cot = jnp.take(flat_cot, index, axis=1)  4.66 us
    unnamed x13, local copies, waits for them, and re-layouts  4.51 us
  transfers between devices with their start and end apart: 4, of which 1 were waited for; matrix products, arithmetic and copies ran while one was open for 0% of the time, Pallas kernels for 0%

commit v1 on v0

--- a/solution.py
+++ b/solution.py
@@ -4,7 +4,6 @@
 from jax.sharding import PartitionSpec as P
 
 NEWT = 4
-BLOCK = 256
 
 
 growth = 0.5
@@ -59,47 +58,30 @@
     return (8.0 * (part(3) - part(1)) - (part(4) - part(0))) / 12.0
 
 
-def solve_blocks(states, kinds, moist, live):
-    trips = (live + BLOCK - 1) // BLOCK
-
-    def advance(turn, solved):
-        offset = turn * BLOCK
-        block_state = lax.dynamic_slice_in_dim(states, offset, BLOCK, 1)
-        block_kind = lax.dynamic_slice_in_dim(kinds, offset, BLOCK, 0)
-        block_moist = lax.dynamic_slice_in_dim(moist, offset, BLOCK, 1)
-        new_heat, new_vapour = sat_adjoint(
-            block_state[0],
-            block_state[1],
-            block_kind,
-            block_moist[0],
-            block_moist[1],
-            block_moist[2],
-            block_moist[3],
-        )
-        return lax.dynamic_update_slice_in_dim(solved, jnp.stack([new_heat, new_vapour]), offset, 1)
-
-    return lax.fori_loop(0, trips, advance, moist[:2])
+def cloudy_columns(cloud_list, cloud_count, columns):
+    index = cloud_list[0, 0]
+    count = cloud_count[0, 0]
+    slot = jnp.arange(index.shape[0], dtype=jnp.int32)
+    hit = (index[:, None] == jnp.arange(columns, dtype=jnp.int32)[None, :]) & (slot < count)[:, None]
+    return jnp.any(hit, axis=0)
 
 
 def on_device(trajectory, cotangent, courant, branch, cloud_list, cloud_count):
     fields, local_lon, local_lat, levels = cotangent.shape
-    columns = local_lon * local_lat
-    index = cloud_list[0, 0]
-    count = cloud_count[0, 0]
-    capacity = index.shape[0]
-    flat_cot = cotangent[:4].reshape(4, columns, levels)
-    flat_state = trajectory.reshape(2, columns, levels)
-    flat_kind = branch.reshape(columns, levels)
-    slot_cot = jnp.take(flat_cot, index, axis=1)
-    slot_number = jnp.arange(capacity, dtype=jnp.int32)
-    slot_state = jnp.take(flat_state, index, axis=1)
-    slot_kind = jnp.take(flat_kind, index, axis=0)
-    results = solve_blocks(slot_state, slot_kind, slot_cot, count)
-    live_slot = jnp.where(slot_number < count, slot_number, capacity)
-    slot_of = jnp.full((columns,), capacity, jnp.int32).at[index].set(live_slot)
-    fetched = jnp.take(results, jnp.minimum(slot_of, capacity - 1), axis=1)
-    chosen = jnp.where((slot_of < capacity)[None, :, None], fetched, flat_cot[:2])
-    first = chosen.reshape(2, local_lon, local_lat, levels)
+    cloudy = cloudy_columns(cloud_list, cloud_count, local_lon * local_lat)
+    cloudy = cloudy.reshape(local_lon, local_lat, 1)
+    new_heat, new_vapour = sat_adjoint(
+        trajectory[0],
+        trajectory[1],
+        branch,
+        cotangent[0],
+        cotangent[1],
+        cotangent[2],
+        cotangent[3],
+    )
+    first = jnp.stack(
+        [jnp.where(cloudy, new_heat, cotangent[0]), jnp.where(cloudy, new_vapour, cotangent[1])]
+    )
     after = jnp.concatenate([first, cotangent[2:]], 0)
     weighted_lon = courant[0] * after
     weighted_lat = courant[1] * after

time: 81.7 us -> 42.1 us (0.52)
  local copies, waits for them, and re-layouts: 34.6 us -> 4.46 us
  other arithmetic: 25 us -> 15.1 us
  starting transfers between devices: 12.5 us -> 13.8 us
    gather x4 -> x0, local copies, waits for them, and re-layouts: 15 us -> none  [the longest x1 4.76 us: on_device(): fetched = jnp.take(results, jnp.minimum(slot_of, capacity - 1), axis=1)]
    select_n x6 -> x0, other arithmetic: 11.3 us -> none  [the longest x1 4.08 us: on_device(): slot_cot = jnp.take(flat_cot, index, axis=1)]
    slice x6 -> x0, local copies, waits for them, and re-layouts: 5.26 us -> none  [the longest x3 2.74 us: on_device(): flat_cot = cotangent[:4].reshape(4, columns, levels)]
    ppermute x2, starting transfers between devices: 6.03 us -> 10.6 us  [with_halo(): lax.ppermute(lax.slice_in_dim(block, 0, width, axis=dim), axis, backward)]
    unnamed x13 -> x6, local copies, waits for them, and re-layouts: 4.51 us -> 0.01 us
    scatter x1 -> x0, local copies, waits for them, and re-layouts: 3.38 us -> none  [on_device(): slot_of = jnp.full((columns,), capacity, jnp.int32).at[index].set(live_slot)]
    ppermute x2, starting transfers between devices: 6.48 us -> 3.29 us  [with_halo(): lax.ppermute(lax.slice_in_dim(block, block.shape[dim] - width, None, axis...]
    dynamic_update_slice x2 -> x0, local copies, waits for them, and re-layouts: 1.84 us -> none  [advance(): lax.dynamic_update_slice_in_dim(solved, jnp.stack([new_heat, new_vapour])...]
  transfers between devices with their start and end apart: 4 -> 4, of which waited for: 1 -> 2; matrix products, arithmetic and copies ran while one was open for 0% -> 0% of each run, Pallas kernels for 0% -> 0%
where the time goes in v1:
time: 42.1 us; the launch traced here: 41.9 us
  other arithmetic  15.1 us (36%)
  starting transfers between devices  13.8 us (33%)
  waiting for transfers between devices  7.75 us (18%)
  local copies, waits for them, and re-layouts  4.46 us (11%)
  between operations  0.76 us (2%)
    ppermute x2, starting transfers between devices, with_halo(): lax.ppermute(lax.slice_in_dim(block, 0, width, axis=dim), axis, backward)  10.6 us
    ppermute x2, waiting for transfers between devices, with_halo(): lax.ppermute(lax.slice_in_dim(block, 0, width, axis=dim), axis, backward)  7.43 us
    add x1, other arithmetic, on_device(): after + centred(lon_part, 1, local_lon) + centred(lat_part, 2, local_lat)  6.85 us
    another operation x2, other arithmetic, on_device(): jnp.stack([jnp.where(cloudy, new_heat, cotangent[0]), jnp.where(cloudy, n...  5.48 us
    ppermute x2, starting transfers between devices, with_halo(): lax.ppermute(lax.slice_in_dim(block, block.shape[dim] - width, None, axis...  3.29 us
    slice x1, local copies, waits for them, and re-layouts, on_device(): after = jnp.concatenate([first, cotangent[2:]], 0)  2.72 us
    mul x1, other arithmetic, on_device(): weighted_lon = courant[0] * after  1.57 us
    mul x1, local copies, waits for them, and re-layouts, on_device(): weighted_lon = courant[0] * after  1.42 us
  transfers between devices with their start and end apart: 4, of which 2 were waited for; matrix products, arithmetic and copies ran while one was open for 0% of the time, Pallas kernels for 0%

profile of v1, /device:TPU:2, one launch (start us, length us, event | category | flops | bytes accessed | tf_op | source)
XLA Modules:
  0.0 41.9 jit_solution(13004146538965105440)
XLA Ops:
  0.7 0.7 %reduce = s32[768]{0:T(1024)S(1)} reduce(s32[1,1,768]{2,1,0:T(1,128)} %param.10, s32[]{:T(128)} %constant.29.clone.1), dimensions={0,1}, to_apply=%param.10.reduce_sub_computation | reduce | bytes 6148 | tf_op args[4]
  1.4 0.5 %fusion.17 = pred[1024]{0:T(1024)(128)(4,1)S(1)} fusion(s32[768]{0:T(1024)S(1)} %reduce, pred[768]{0:T(1024)(128)(4,1)S(1)} %iota_compare_fusion.1), kind=kLoop, calls=%fused_computation.31 | loop fusion | flops 2358272 | bytes 4864 | tf_op jit(solution)/shard_map/reduce_or | solution.py:66
  1.9 0.1 broadcast_in_dim.26
  1.9 0.0 copy-start
  1.9 0.0 copy-start.1
  1.9 0.0 copy-start.2
  1.9 1.4 %slice_bitcast_fusion.1 = (f32[16,64,128]{2,1,0:T(8,128)S(1)}, f32[16,64,128]{2,1,0:T(8,128)S(1)}) fusion(f32[2,16,64,128]{3,2,1,0:T(8,128)} %param.8), kind=kLoop, calls=%fused_computation.92 | loop fusion | bytes 2097152 | tf_op jit(solution)/shard_map/mul | solution.py:86
  3.4 2.7 %slice.79 = f32[6,16,64,128]{3,2,1,0:T(8,128)S(1)} slice(f32[8,16,64,128]{3,2,1,0:T(8,128)} %param.7), slice={[2:8], [0:16], [0:64], [0:128]} | slice | bytes 6291456 | tf_op jit(solution)/shard_map/slice | solution.py:85
  6.1 0.0 copy-done
  6.1 0.0 copy-done.1
  6.1 0.0 copy-done.2
  6.1 3.3 %fusion.21 = (f32[1,16,64,128]{3,2,1,0:T(8,128)S(1)}, f32[16,64,128]{2,1,0:T(8,128)S(1)}, pred[16,64,128]{2,1,0:T(8,128)(4,1)S(1)}, pred[16,64,128]{2,1,0:T(8,128)(4,1)S(1)}) fusion(f32[2,16,64,128]{3,2,1,0:T(8,128)S(1)} %copy-done.1, f32[8,16,64,128]{3,2,1,0:T(8,128)S(1)} %copy-done, pred[16,64]{1,0:T(8,128)(4,1)S(1)} %broadcast_in_dim.26, ...), kind=kLoop, calls=%fused_computation.40 | loop fusion | flops 19660800 | bytes 4981760 | tf_op jit(solution)/shard_map/stack | solution.py:82
  9.5 2.1 %fusion.22 = f32[1,16,64,128]{3,2,1,0:T(8,128)S(1)} fusion(f32[16,64,128]{2,1,0:T(8,128)S(1)} %get-tuple-element.6, f32[2,16,64,128]{3,2,1,0:T(8,128)S(1)} %copy-done.1, f32[8,16,64,128]{3,2,1,0:T(8,128)S(1)} %copy-done, pred[16,64,128]{2,1,0:T(8,128)(4,1)S(1)} %get-tuple-element.8, pred[16,64,128]{2,1,0:T(8,128)(4,1)S(1)} %get-tuple-element.7, ...), kind=kLoop, calls=%fused_computation.41 | loop fusion | flops 11796480 | bytes 2884608 | tf_op jit(solution)/shard_map/stack | solution.py:82
  11.6 1.6 %broadcast_multiply_fusion.1 = (f32[8,16,64,128]{3,2,1,0:T(8,128)S(1)}, f32[8,16,64,128]{3,2,1,0:T(8,128)S(1)}) fusion(f32[16,64,128]{2,1,0:T(8,128)S(1)} %get-tuple-element.15, f32[6,16,64,128]{3,2,1,0:T(8,128)S(1)} %slice.79, f32[1,16,64,128]{3,2,1,0:T(8,128)S(1)} %fusion.22, f32[1,16,64,128]{3,2,1,0:T(8,128)S(1)} %get-tuple-element.5, ...), kind=kLoop, calls=%fused_computation.33 | loop fusion | flops 4194304 | bytes 13631488 | tf_op jit(solution)/shard_map/mul | solution.py:86
  13.2 0.1 fusion.78
  13.3 8.0 %collective-permute-start = (f32[8,2,64,128]{3,2,1,0:T(8,128)S(1)}, f32[8,2,64,128]{3,2,1,0:T(8,128)S(1)}, u32[]{:S(2)}, u32[]{:S(2)}) collective-permute-start(f32[8,2,64,128]{3,2,1,0:T(8,128)S(1)} %get-tuple-element.9), channel_id=1, source_target_pairs={{8,0},{16,8},{24,16},{32,24},{40,32},{48,40},{56,48},{64,56},{72,6... | collective-permute-start | bytes 1572872 | tf_op jit(solution)/shard_map/ppermute | solution.py:24
  21.3 0.0 collective-permute-start.1
  21.3 0.1 fusion.79
  21.4 2.6 %collective-permute-start.2 = (f32[8,16,2,128]{3,2,1,0:T(2,128)S(1)}, f32[8,16,2,128]{3,2,1,0:T(2,128)S(1)}, u32[]{:S(2)}, u32[]{:S(2)}) collective-permute-start(f32[8,16,2,128]{3,2,1,0:T(2,128)S(1)} %get-tuple-element.13), channel_id=1, source_target_pairs={{1,0},{2,1},{3,2},{4,3},{5,4},{6,5},{7,6},{9,8},{10,9},{11,10},{12... | collective-permute-start | bytes 393224 | tf_op jit(solution)/shard_map/ppermute | solution.py:24
  24.0 3.3 %collective-permute-start.3 = (f32[8,16,2,128]{3,2,1,0:T(2,128)S(1)}, f32[8,16,2,128]{3,2,1,0:T(2,128)S(1)}, u32[]{:S(2)}, u32[]{:S(2)}) collective-permute-start(f32[8,16,2,128]{3,2,1,0:T(2,128)S(1)} %get-tuple-element.14), channel_id=1, source_target_pairs={{0,1},{1,2},{2,3},{3,4},{4,5},{5,6},{6,7},{8,9},{9,10},{10,11},{11... | collective-permute-start | bytes 393224 | tf_op jit(solution)/shard_map/ppermute | solution.py:21
  27.3 7.4 %collective-permute-done.2 = f32[8,16,2,128]{3,2,1,0:T(2,128)S(1)} collective-permute-done((f32[8,16,2,128]{3,2,1,0:T(2,128)S(1)}, f32[8,16,2,128]{3,2,1,0:T(2,128)S(1)}, u32[]{:S(2)}, u32[]{:S(2)}) %collective-permute-start.2) | collective-permute-done | bytes 131104 | tf_op jit(solution)/shard_map/ppermute | solution.py:24
  34.7 0.0 collective-permute-done.3
  34.7 0.0 collective-permute-done
  34.7 0.3 collective-permute-done.1
  35.0 6.9 %fusion.5 = f32[8,16,64,128]{3,2,1,0:T(8,128)} fusion(f32[8,16,2,128]{3,2,1,0:T(2,128)S(1)} %collective-permute-done.3, f32[8,16,64,128]{3,2,1,0:T(8,128)S(1)} %get-tuple-element.12, f32[8,16,2,128]{3,2,1,0:T(2,128)S(1)} %collective-permute-done.2, f32[8,2,64,128]{3,2,1,0:T(8,128)S(1)} %collective-permute-done.1, ...), kind=kLoop, calls=%fused_computation.13 | loop fusion | flops 23068672 | bytes 18087936 | tf_op jit(solution)/shard_map/add | solution.py:90
  (1 shorter events, 0.0 us)
Async XLA Ops:
  1.9 4.2 %copy-start = (f32[8,16,64,128]{3,2,1,0:T(8,128)S(1)}, f32[8,16,64,128]{3,2,1,0:T(8,128)}, u32[]{:S(2)}) copy-start(f32[8,16,64,128]{3,2,1,0:T(8,128)} %param.7) | copy-start | bytes 12582916
  1.9 4.2 %copy-start.1 = (f32[2,16,64,128]{3,2,1,0:T(8,128)S(1)}, f32[2,16,64,128]{3,2,1,0:T(8,128)}, u32[]{:S(2)}) copy-start(f32[2,16,64,128]{3,2,1,0:T(8,128)} %param.6) | copy-start | bytes 3145732
  1.9 4.2 %copy-start.2 = (s32[16,64,128]{2,1,0:T(8,128)S(1)}, s32[16,64,128]{2,1,0:T(8,128)}, u32[]{:S(2)}) copy-start(s32[16,64,128]{2,1,0:T(8,128)} %param.9) | copy-start | bytes 1572868
  13.3 21.4 %collective-permute-start = (f32[8,2,64,128]{3,2,1,0:T(8,128)S(1)}, f32[8,2,64,128]{3,2,1,0:T(8,128)S(1)}, u32[]{:S(2)}, u32[]{:S(2)}) collective-permute-start(f32[8,2,64,128]{3,2,1,0:T(8,128)S(1)} %get-tuple-element.9), channel_id=1, source_target_pairs={{8,0},{16,8},{24,16},{32,24},{40,32},{48,40},{56,48},{64,56},{72,6... | collective-permute-start | bytes 1572872 | tf_op jit(solution)/shard_map/ppermute | solution.py:24
  21.3 13.7 %collective-permute-start.1 = (f32[8,2,64,128]{3,2,1,0:T(8,128)S(1)}, f32[8,2,64,128]{3,2,1,0:T(8,128)S(1)}, u32[]{:S(2)}, u32[]{:S(2)}) collective-permute-start(f32[8,2,64,128]{3,2,1,0:T(8,128)S(1)} %get-tuple-element.10), channel_id=1, source_target_pairs={{0,8},{8,16},{16,24},{24,32},{32,40},{40,48},{48,56},{56,64},{64,7... | collective-permute-start | bytes 1572872 | tf_op jit(solution)/shard_map/ppermute | solution.py:21
  21.4 13.3 %collective-permute-start.2 = (f32[8,16,2,128]{3,2,1,0:T(2,128)S(1)}, f32[8,16,2,128]{3,2,1,0:T(2,128)S(1)}, u32[]{:S(2)}, u32[]{:S(2)}) collective-permute-start(f32[8,16,2,128]{3,2,1,0:T(2,128)S(1)} %get-tuple-element.13), channel_id=1, source_target_pairs={{1,0},{2,1},{3,2},{4,3},{5,4},{6,5},{7,6},{9,8},{10,9},{11,10},{12... | collective-permute-start | bytes 393224 | tf_op jit(solution)/shard_map/ppermute | solution.py:24
  24.0 10.7 %collective-permute-start.3 = (f32[8,16,2,128]{3,2,1,0:T(2,128)S(1)}, f32[8,16,2,128]{3,2,1,0:T(2,128)S(1)}, u32[]{:S(2)}, u32[]{:S(2)}) collective-permute-start(f32[8,16,2,128]{3,2,1,0:T(2,128)S(1)} %get-tuple-element.14), channel_id=1, source_target_pairs={{0,1},{1,2},{2,3},{3,4},{4,5},{5,6},{6,7},{8,9},{9,10},{10,11},{11... | collective-permute-start | bytes 393224 | tf_op jit(solution)/shard_map/ppermute | solution.py:21

commit v2 on v1

--- a/solution.py
+++ b/solution.py
@@ -9,21 +9,6 @@
 growth = 0.5
 latent_liquid = 1.0
 latent_ice = 1.3
-
-
-def with_halo(block, sides, width, periodic):
-    for axis, dim in sides:
-        count = lax.axis_size(axis)
-        forward = [(i, i + 1) for i in range(count - 1)]
-        if periodic:
-            forward.append((count - 1, 0))
-        backward = [(target, source) for source, target in forward]
-        low = lax.ppermute(
-            lax.slice_in_dim(block, block.shape[dim] - width, None, axis=dim), axis, forward
-        )
-        high = lax.ppermute(lax.slice_in_dim(block, 0, width, axis=dim), axis, backward)
-        block = jnp.concatenate([low, block, high], axis=dim)
-    return block
 
 
 def increments(warmth, vapour, kinds):
@@ -58,6 +43,12 @@
     return (8.0 * (part(3) - part(1)) - (part(4) - part(0))) / 12.0
 
 
+def zero_padded_centred(field, dim):
+    widths = [(0, 0)] * field.ndim
+    widths[dim] = (2, 2)
+    return centred(jnp.pad(field, widths), dim, field.shape[dim])
+
+
 def cloudy_columns(cloud_list, cloud_count, columns):
     index = cloud_list[0, 0]
     count = cloud_count[0, 0]
@@ -66,10 +57,7 @@
     return jnp.any(hit, axis=0)
 
 
-def on_device(trajectory, cotangent, courant, branch, cloud_list, cloud_count):
-    fields, local_lon, local_lat, levels = cotangent.shape
-    cloudy = cloudy_columns(cloud_list, cloud_count, local_lon * local_lat)
-    cloudy = cloudy.reshape(local_lon, local_lat, 1)
+def first_pair(trajectory, cotangent, branch, cloudy):
     new_heat, new_vapour = sat_adjoint(
         trajectory[0],
         trajectory[1],
@@ -79,15 +67,61 @@
         cotangent[2],
         cotangent[3],
     )
-    first = jnp.stack(
+    return jnp.stack(
         [jnp.where(cloudy, new_heat, cotangent[0]), jnp.where(cloudy, new_vapour, cotangent[1])]
     )
-    after = jnp.concatenate([first, cotangent[2:]], 0)
-    weighted_lon = courant[0] * after
-    weighted_lat = courant[1] * after
-    lon_part = with_halo(weighted_lon, (("lon", 1),), 2, True)
-    lat_part = with_halo(weighted_lat, (("lat", 2),), 2, False)
-    return after + centred(lon_part, 1, local_lon) + centred(lat_part, 2, local_lat)
+
+
+def edge(array, dim, start, width=2):
+    return lax.slice_in_dim(array, start, start + width, axis=dim)
+
+
+def edge_after(trajectory, cotangent, branch, cloudy, dim, start):
+    sub = lambda a, d: edge(a, d, start)
+    pair = first_pair(sub(trajectory, dim), sub(cotangent[:4], dim), sub(branch, dim - 1), sub(cloudy, dim - 1))
+    return jnp.concatenate([pair, sub(cotangent[2:], dim)], 0)
+
+
+def exchange(trajectory, cotangent, courant, branch, cloudy, axis, dim, periodic):
+    size = cotangent.shape[dim]
+    count = lax.axis_size(axis)
+    forward = [(i, i + 1) for i in range(count - 1)]
+    if periodic:
+        forward.append((count - 1, 0))
+    backward = [(target, source) for source, target in forward]
+    weight = courant[dim - 1]
+    top = edge(weight, dim - 1, size - 2) * edge_after(trajectory, cotangent, branch, cloudy, dim, size - 2)
+    bottom = edge(weight, dim - 1, 0) * edge_after(trajectory, cotangent, branch, cloudy, dim, 0)
+    low = lax.ppermute(top, axis, forward)
+    high = lax.ppermute(bottom, axis, backward)
+    return low, high
+
+
+def add_halo(out, low, high, dim):
+    size = out.shape[dim]
+    row = lambda a, i: lax.slice_in_dim(a, i, i + 1, axis=dim)
+    first = jnp.concatenate(
+        [(row(low, 0) - 8.0 * row(low, 1)) / 12.0, row(low, 1) / 12.0], dim
+    )
+    last = jnp.concatenate(
+        [-row(high, 0) / 12.0, (8.0 * row(high, 0) - row(high, 1)) / 12.0], dim
+    )
+    out = lax.dynamic_update_slice_in_dim(out, edge(out, dim, 0) + first, 0, dim)
+    out = lax.dynamic_update_slice_in_dim(out, edge(out, dim, size - 2) + last, size - 2, dim)
+    return out
+
+
+def on_device(trajectory, cotangent, courant, branch, cloud_list, cloud_count):
+    fields, local_lon, local_lat, levels = cotangent.shape
+    cloudy = cloudy_columns(cloud_list, cloud_count, local_lon * local_lat)
+    cloudy = cloudy.reshape(local_lon, local_lat, 1)
+    lon_low, lon_high = exchange(trajectory, cotangent, courant, branch, cloudy, "lon", 1, True)
+    lat_low, lat_high = exchange(trajectory, cotangent, courant, branch, cloudy, "lat", 2, False)
+    after = jnp.concatenate([first_pair(trajectory, cotangent[:4], branch, cloudy), cotangent[2:]], 0)
+    out = after + zero_padded_centred(courant[0] * after, 1) + zero_padded_centred(courant[1] * after, 2)
+    out = add_halo(out, lon_low, lon_high, 1)
+    out = add_halo(out, lat_low, lat_high, 2)
+    return out
 
 
 def solution(mesh):

time: 42.1 us -> 65.2 us (1.55); the launches traced: 41.9 us -> 64.3 us
  other arithmetic: 15.1 us -> 39.4 us
  waiting for transfers between devices: 7.75 us -> 0.01 us
  local copies, waits for them, and re-layouts: 4.46 us -> 9.23 us
  starting transfers between devices: 13.8 us -> 14.7 us
    ppermute x4, waiting for transfers between devices: 7.75 us -> 0.01 us  [the longest x2 0.01 us: exchange(): low = lax.ppermute(top, axis, forward)]
    dynamic_update_slice x0 -> x4, other arithmetic: none -> 7.45 us  [the longest x2 3.73 us: add_halo(): lax.dynamic_update_slice_in_dim(out, edge(out, dim, size - 2) + last, siz...]
    another operation x2 -> x8, other arithmetic: 5.48 us -> 12.5 us  [first_pair(): jnp.stack([jnp.where(cloudy, new_heat, cotangent[0]), jnp.where(cloudy, n...]
    slice x3 -> x12, local copies, waits for them, and re-layouts: 2.94 us -> 7.1 us  [the longest x10 3.74 us: edge(): return lax.slice_in_dim(array, start, start + width, axis=dim)]
    div x0 -> x4, other arithmetic: none -> 3.09 us  [the longest x2 1.98 us: add_halo(): -row(high, 0) / 12.0]
    add x1, other arithmetic: 6.85 us -> 9.86 us  [on_device(): after + zero_padded_centred(courant[0] * after, 1)]
    mul x1 -> x5, other arithmetic: 1.57 us -> 4.4 us  [the longest x1 2.69 us: on_device(): courant[0] * after]
    gt x0 -> x1, other arithmetic: none -> 0.89 us  [increments(): active = (kinds > 0).astype(warmth.dtype)]
  transfers between devices with their start and end apart: 4 -> 4, of which waited for: 2 -> 0; matrix products, arithmetic and copies ran while one was open for 0% -> 52% of each run, Pallas kernels for 0% -> 0%
where the time goes in v2:
time: 65.2 us; the launch traced here: 64.3 us
  other arithmetic  39.4 us (60%)
  starting transfers between devices  14.7 us (23%)
  local copies, waits for them, and re-layouts  9.23 us (14%)
  between operations  0.99 us (2%)
    another operation x8, other arithmetic, first_pair(): jnp.stack([jnp.where(cloudy, new_heat, cotangent[0]), jnp.where(cloudy, n...  12.5 us
    ppermute x2, starting transfers between devices, exchange(): high = lax.ppermute(bottom, axis, backward)  12.1 us
    add x1, other arithmetic, on_device(): after + zero_padded_centred(courant[0] * after, 1)  9.86 us
    slice x10, local copies, waits for them, and re-layouts, edge(): return lax.slice_in_dim(array, start, start + width, axis=dim)  3.74 us
    dynamic_update_slice x2, other arithmetic, add_halo(): lax.dynamic_update_slice_in_dim(out, edge(out, dim, size - 2) + last, siz...  3.73 us
    dynamic_update_slice x2, other arithmetic, add_halo(): lax.dynamic_update_slice_in_dim(out, edge(out, dim, 0) + first, 0, dim)  3.72 us
    mul x1, other arithmetic, on_device(): courant[0] * after  2.69 us
    ppermute x2, starting transfers between devices, exchange(): low = lax.ppermute(top, axis, forward)  2.59 us
  transfers between devices with their start and end apart: 4, of which 0 were waited for; matrix products, arithmetic and copies ran while one was open for 52% of the time, Pallas kernels for 0%

profile of v2, /device:TPU:2, one launch (start us, length us, event | category | flops | bytes accessed | tf_op | source)
XLA Modules:
  0.0 64.3 jit_solution(14685403859621493188)
XLA Ops:
  0.8 1.2 %fusion.254 = (f32[6,2,64,128]{3,2,1,0:T(8,128)S(1)}, f32[6,2,64,128]{3,2,1,0:T(8,128)S(1)}) fusion(f32[8,16,64,128]{3,2,1,0:T(8,128)} %param.7), kind=kLoop, calls=%fused_computation.464 | loop fusion | bytes 1572864 | tf_op jit(solution)/shard_map/slice | solution.py:76
  1.9 0.9 %slice_compare_fusion = (pred[2,64,128]{2,1,0:T(8,128)(4,1)S(1)}, pred[2,64,128]{2,1,0:T(8,128)(4,1)S(1)}) fusion(s32[16,64,128]{2,1,0:T(8,128)} %param.9), kind=kLoop, calls=%fused_computation.335 | loop fusion | flops 32768 | bytes 163840 | tf_op jit(solution)/shard_map/jvp()/gt | solution.py:18
  2.8 0.7 %reduce = s32[768]{0:T(1024)S(1)} reduce(s32[1,1,768]{2,1,0:T(1,128)} %param.10, s32[]{:T(128)} %constant.83.clone.1), dimensions={0,1}, to_apply=%param.10.reduce_sub_computation | reduce | bytes 6148 | tf_op args[4]
  3.5 0.5 fusion.13
  4.2 0.9 %slice_bitcast_fusion.2 = (f32[2,64,128]{2,1,0:T(8,128)S(1)}, f32[2,64,128]{2,1,0:T(8,128)S(1)}) fusion(f32[2,16,64,128]{3,2,1,0:T(8,128)} %param.8), kind=kLoop, calls=%fused_computation.297 | loop fusion | bytes 262144 | tf_op jit(solution)/shard_map/mul | solution.py:94
  5.1 2.1 %fusion.87 = (f32[1,2,64,128]{3,2,1,0:T(8,128)S(1)}, f32[2,64,128]{2,1,0:T(8,128)S(1)}, pred[2,64,128]{2,1,0:T(8,128)(4,1)S(1)}, pred[2,64,128]{2,1,0:T(8,128)(4...) fusion(pred[2,64,128]{2,1,0:T(8,128)(4,1)S(1)} %get-tuple-eleme, ...), kind=kLoop, calls=%fused_computation.157 | loop fusion | flops 4882432 | bytes 1278208 | tf_op jit(solution)/shard_map/stack | solution.py:70
  7.1 1.5 %fusion.88 = (f32[1,2,64,128]{3,2,1,0:T(8,128)S(1)}, f32[1,2,64,128]{3,2,1,0:T(8,128)S(1)}) fusion(f32[2,64,128]{2,1,0:T(8,128)S(1)} %get-tuple-element.14, f32[2,16,64,128]{3,2,1,0:T(8,128)} %param.6, f32[8,16,64,128]{3,2,1,0:T(8,128)} %param.7, pred[2,64,128]{2,1,0:T(8,128)(4,1)S(1)} %get-tuple-element.16, pred[2,64,128]{2,1,0:T(8,128)(4,1)S(1)} %get-tuple-element.15, ...), kind=kLoop, calls=%fused_computation.158 | loop fusion | flops 2949120 | bytes 721152 | tf_op jit(solution)/shard_map/stack | solution.py:70
  8.7 0.8 %maximum_multiply_fusion = f32[8,2,64,128]{3,2,1,0:T(8,128)} fusion(f32[6,2,64,128]{3,2,1,0:T(8,128)S(1)} %get-tuple-element.42, f32[1,2,64,128]{3,2,1,0:T(8,128)S(1)} %get-tuple-element.30, f32[1,2,64,128]{3,2,1,0:T(8,128)S(1)} %get-tuple-element.25, f32[2,64,128]{2,1,0:T(8,128)S(1)} %get-tuple-element.50), kind=kLoop, calls=%fused_computation.38 | loop fusion | flops 393216 | bytes 1114112 | tf_op jit(solution)/shard_map/mul | solution.py:93
  9.5 0.8 %maximum_multiply_fusion.1 = f32[8,2,64,128]{3,2,1,0:T(8,128)} fusion(f32[6,2,64,128]{3,2,1,0:T(8,128)S(1)} %get-tuple-element.41, f32[1,2,64,128]{3,2,1,0:T(8,128)S(1)} %get-tuple-element.29, f32[1,2,64,128]{3,2,1,0:T(8,128)S(1)} %get-tuple-element.13, f32[2,64,128]{2,1,0:T(8,128)S(1)} %get-tuple-element.49), kind=kLoop, calls=%fused_computation.39 | loop fusion | flops 393216 | bytes 1114112 | tf_op jit(solution)/shard_map/mul | solution.py:94
  10.4 7.9 %collective-permute-start.1 = (f32[8,2,64,128]{3,2,1,0:T(8,128)}, f32[8,2,64,128]{3,2,1,0:T(8,128)}, u32[]{:S(2)}, u32[]{:S(2)}) collective-permute-start(f32[8,2,64,128]{3,2,1,0:T(8,128)} %maximum_multiply_fusion.1), channel_id=1, source_target_pairs={{8,0},{16,8},{24,16},{32,24},{40,32},{48,40},{56,48},{64,56},{72,6... | collective-permute-start | bytes 1572872 | tf_op jit(solution)/shard_map/ppermute | solution.py:96
  18.3 0.9 %slice_bitcast_fusion.1 = (f32[16,64,128]{2,1,0:T(8,128)}, f32[16,64,128]{2,1,0:T(8,128)S(1)}) fusion(f32[2,16,64,128]{3,2,1,0:T(8,128)S(1)} %copy-done.4), kind=kLoop, calls=%fused_computation.90 | loop fusion | bytes 2097152 | tf_op jit(solution)/shard_map/mul | solution.py:121
  19.2 1.4 %fusion.253 = (f32[6,16,2,128]{3,2,1,0:T(2,128)S(1)}, f32[6,16,2,128]{3,2,1,0:T(2,128)S(1)}) fusion(f32[8,16,64,128]{3,2,1,0:T(8,128)} %param.7), kind=kLoop, calls=%fused_computation.463 | loop fusion | bytes 393216 | tf_op jit(solution)/shard_map/slice | solution.py:76
  20.6 1.2 %fusion.252 = (f32[1,16,2,128]{3,2,1,0:T(2,128)S(1)}, f32[1,16,2,128]{3,2,1,0:T(2,128)S(1)}, f32[1,16,2,128]{3,2,1,0:T(2,128)S(1)}, f32[1,16,2,128]{3,2,1,0:T(2,...) fusion(f32[8,16,64,128]{3,2,1,0:T(8,128)} %param.7, ...), kind=kLoop, calls=%fused_computation.462 | loop fusion | bytes 393216 | tf_op jit(solution)/shard_map/slice | solution.py:67
  21.9 0.9 %fusion.257 = (s32[16,2,128]{2,1,0:T(2,128)S(1)}, s32[16,2,128]{2,1,0:T(2,128)S(1)}) fusion(s32[16,64,128]{2,1,0:T(8,128)} %param.9), kind=kLoop, calls=%fused_computation.467 | loop fusion | bytes 65536 | tf_op jit(solution)/shard_map/slice | solution.py:76
  23.0 0.3 fusion.202
  23.4 0.1 fusion.203
  23.5 2.6 %collective-permute-start.2 = (f32[8,16,2,128]{3,1,2,0:T(8,128)S(1)}, f32[8,16,2,128]{3,1,2,0:T(8,128)S(1)}, u32[]{:S(2)}, u32[]{:S(2)}) collective-permute-start(f32[8,16,2,128]{3,1,2,0:T(8,128)S(1)} %maximum_multiply_fusion.2), channel_id=1, source_target_pairs={{0,1},{1,2},{2,3},{3,4},{4,5},{5,6},{6,7},{8,9},{9,10},{10,11},{11... | collective-permute-start | bytes 393224 | tf_op jit(solution)/shard_map/ppermute | solution.py:95
  26.3 0.3 fusion.207
  26.6 0.1 fusion.208
  26.8 4.2 %collective-permute-start.3 = (f32[8,16,2,128]{3,1,2,0:T(8,128)S(1)}, f32[8,16,2,128]{3,1,2,0:T(8,128)}, u32[]{:S(2)}, u32[]{:S(2)}) collective-permute-start(f32[8,16,2,128]{3,1,2,0:T(8,128)S(1)} %maximum_multiply_fusion.3), channel_id=1, source_target_pairs={{1,0},{2,1},{3,2},{4,3},{5,4},{6,5},{7,6},{9,8},{10,9},{11,10},{12... | collective-permute-start | bytes 393224 | tf_op jit(solution)/shard_map/ppermute | solution.py:96
  30.9 2.1 %slice.304 = f32[6,16,64,128]{3,2,1,0:T(8,128)S(1)} slice(f32[8,16,64,128]{3,2,1,0:T(8,128)} %param.7), slice={[2:8], [0:16], [0:64], [0:128]} | slice | bytes 6291456 | tf_op jit(solution)/shard_map/slice | solution.py:120
  33.1 4.9 %fusion.17 = (f32[1,16,64,128]{3,2,1,0:T(8,128)S(1)}, f32[16,64,128]{2,1,0:T(8,128)S(1)}, pred[16,64,128]{2,1,0:T(8,128)(4,1)S(1)}, pred[16,64,128]{2,1,0:T(8,128)(4,1)S(1)}) fusion(f32[2,16,64,128]{3,2,1,0:T(8,128)} %param.6, f32[8,16,64,128]{3,2,1,0:T(8,128)} %param.7, pred[16,64]{1,0:T(8,128)(4,1)S(1)} %broadcast_in_dim.104, s32[16,64,128]{2,1,0:T(8,128)} %param.9), kind=kLoop, calls=%fused_computation.32 | loop fusion | flops 19660800 | bytes 4981760 | tf_op jit(solution)/shard_map/stack | solution.py:70
  38.0 3.1 %fusion.18 = f32[1,16,64,128]{3,2,1,0:T(8,128)S(1)} fusion(f32[16,64,128]{2,1,0:T(8,128)S(1)} %get-tuple-element.22, f32[2,16,64,128]{3,2,1,0:T(8,128)S(1)} %copy-done, f32[8,16,64,128]{3,2,1,0:T(8,128)} %param.7, pred[16,64,128]{2,1,0:T(8,128)(4,1)S(1)} %get-tuple-element.24, pred[16,64,128]{2,1,0:T(8,128)(4,1)S(1)} %get-tuple-element.23, ...), kind=kLoop, calls=%fused_computation.33 | loop fusion | flops 11796480 | bytes 2884608 | tf_op jit(solution)/shard_map/stack | solution.py:70
  41.2 2.7 %broadcast_multiply_fusion.1 = (f32[8,16,64,128]{3,2,1,0:T(8,128)S(1)}, f32[8,16,64,128]{3,2,1,0:T(8,128)}) fusion(f32[16,64,128]{2,1,0:T(8,128)S(1)} %copy-done.3, f32[6,16,64,128]{3,2,1,0:T(8,128)S(1)} %slice.304, f32[1,16,64,128]{3,2,1,0:T(8,128)S(1)} %fusion.18, f32[1,16,64,128]{3,2,1,0:T(8,128)S(1)} %get-tuple-element.21, f32[16,64,128]{2,1,0:T(8,128)S(1)} %copy-done.2), kind=kLoop, calls=%fused_computation.25 | loop fusion | flops 4194304 | bytes 13631488 | tf_op jit(solution)/shard_map/mul | solution.py:121
  43.8 9.9 %fusion.4 = f32[8,16,64,128]{3,2,1,0:T(8,128)} fusion(f32[8,16,64,128]{3,2,1,0:T(8,128)} %get-tuple-element.44, f32[8,16,64,128]{3,2,1,0:T(8,128)S(1)} %get-tuple-element.43, f32[6,16,64,128]{3,2,1,0:T(8,128)S(1)} %slice.304, f32[1,16,64,128]{3,2,1,0:T(8,128)S(1)} %fusion.18, f32[1,16,64,128]{3,2,1,0:T(8,128)S(1)} %get-tuple-element.21), kind=kLoop, calls=%fused_computation.12 | loop fusion | flops 14680064 | bytes 16777216 | tf_op jit(solution)/shard_map/add | solution.py:121
  53.8 0.9 %negate_multiply_fusion.1 = (f32[8,16,1,128]{3,1,2,0:T(8,128)S(1)}, f32[8,16,1,128]{3,1,2,0:T(8,128)S(1)}) fusion(f32[8,16,2,128]{3,1,2,0:T(8,128)} %collective-permute-done.3), kind=kLoop, calls=%fused_computation.261 | loop fusion | flops 81920 | bytes 262144 | tf_op jit(solution)/shard_map/div | solution.py:107
  54.7 1.1 %fusion.76 = (f32[8,1,64,128]{3,2,1,0:T(8,128)S(1)}, f32[8,1,64,128]{3,2,1,0:T(8,128)S(1)}) fusion(f32[8,2,64,128]{3,2,1,0:T(8,128)} %collective-permute-done), kind=kLoop, calls=%fused_computation.129 | loop fusion | flops 262144 | bytes 1048576 | tf_op jit(solution)/shard_map/div | solution.py:104
  55.8 1.9 %fusion.20 = f32[8,16,64,128]{3,2,1,0:T(8,128)} fusion(f32[8,16,64,128]{3,2,1,0:T(8,128)} %fusion.4, f32[8,1,64,128]{3,2,1,0:T(8,128)S(1)} %get-tuple-element.62, f32[8,1,64,128]{3,2,1,0:T(8,128)S(1)} %get-tuple-element.61), kind=kLoop, calls=%fused_computation.37 | loop fusion | flops 262144 | bytes 1572864 | tf_op jit(solution)/shard_map/dynamic_update_slice | solution.py:109
  57.7 1.1 %negate_multiply_fusion = (f32[8,1,64,128]{3,2,1,0:T(8,128)S(1)}, f32[8,1,64,128]{3,2,1,0:T(8,128)S(1)}) fusion(f32[8,2,64,128]{3,2,1,0:T(8,128)} %collective-permute-done.1), kind=kLoop, calls=%fused_computation.130 | loop fusion | flops 327680 | bytes 1048576 | tf_op jit(solution)/shard_map/div | solution.py:107
  58.8 1.9 %fusion.19 = f32[8,16,64,128]{3,2,1,0:T(8,128)} fusion(f32[8,16,64,128]{3,2,1,0:T(8,128)} %fusion.20, f32[8,1,64,128]{3,2,1,0:T(8,128)S(1)} %get-tuple-element.58, f32[8,1,64,128]{3,2,1,0:T(8,128)S(1)} %get-tuple-element.57), kind=kLoop, calls=%fused_computation.35 | loop fusion | flops 262144 | bytes 1572864 | tf_op jit(solution)/shard_map/dynamic_update_slice | solution.py:110
  60.7 1.8 %fusion.78 = f32[8,16,64,128]{3,2,1,0:T(8,128)} fusion(f32[8,16,64,128]{3,2,1,0:T(8,128)} %fusion.19, f32[8,16,2,128]{3,1,2,0:T(8,128)S(1)} %pad_maximum_fusion.1), kind=kLoop, calls=%fused_computation.138 | loop fusion | flops 32768 | bytes 393216 | tf_op jit(solution)/shard_map/dynamic_update_slice | solution.py:109
  62.5 1.8 %fusion.77 = f32[8,16,64,128]{3,2,1,0:T(8,128)} fusion(f32[8,16,64,128]{3,2,1,0:T(8,128)} %fusion.78, f32[8,16,2,128]{3,1,2,0:T(8,128)S(1)} %pad_maximum_fusion.2), kind=kLoop, calls=%fused_computation.136 | loop fusion | flops 32768 | bytes 393216 | tf_op jit(solution)/shard_map/dynamic_update_slice | solution.py:110
  (34 shorter events, 0.7 us)
Async XLA Ops:
  0.0 18.3 %copy-start.4 = (f32[2,16,64,128]{3,2,1,0:T(8,128)S(1)}, f32[2,16,64,128]{3,2,1,0:T(8,128)}, u32[]{:S(2)}) copy-start(f32[2,16,64,128]{3,2,1,0:T(8,128)} %param.8) | copy-start | bytes 3145732
  9.5 45.1 %collective-permute-start = (f32[8,2,64,128]{3,2,1,0:T(8,128)}, f32[8,2,64,128]{3,2,1,0:T(8,128)}, u32[]{:S(2)}, u32[]{:S(2)}) collective-permute-start(f32[8,2,64,128]{3,2,1,0:T(8,128)} %maximum_multiply_fusion), channel_id=1, source_target_pairs={{0,8},{8,16},{16,24},{24,32},{32,40},{40,48},{48,56},{56,64},{64,7... | collective-permute-start | bytes 1572872 | tf_op jit(solution)/shard_map/ppermute | solution.py:95
  10.4 47.3 %collective-permute-start.1 = (f32[8,2,64,128]{3,2,1,0:T(8,128)}, f32[8,2,64,128]{3,2,1,0:T(8,128)}, u32[]{:S(2)}, u32[]{:S(2)}) collective-permute-start(f32[8,2,64,128]{3,2,1,0:T(8,128)} %maximum_multiply_fusion.1), channel_id=1, source_target_pairs={{8,0},{16,8},{24,16},{32,24},{40,32},{48,40},{56,48},{64,56},{72,6... | collective-permute-start | bytes 1572872 | tf_op jit(solution)/shard_map/ppermute | solution.py:96
  19.2 7.5 %copy-start.1 = (f32[16,64,128]{2,1,0:T(8,128)}, f32[16,64,128]{2,1,0:T(8,128)S(1)}, u32[]{:S(2)}) copy-start(f32[16,64,128]{2,1,0:T(8,128)S(1)} %get-tuple-element.52) | copy-start | bytes 1572868
  23.5 30.2 %collective-permute-start.2 = (f32[8,16,2,128]{3,1,2,0:T(8,128)S(1)}, f32[8,16,2,128]{3,1,2,0:T(8,128)S(1)}, u32[]{:S(2)}, u32[]{:S(2)}) collective-permute-start(f32[8,16,2,128]{3,1,2,0:T(8,128)S(1)} %maximum_multiply_fusion.2), channel_id=1, source_target_pairs={{0,1},{1,2},{2,3},{3,4},{4,5},{5,6},{6,7},{8,9},{9,10},{10,11},{11... | collective-permute-start | bytes 393224 | tf_op jit(solution)/shard_map/ppermute | solution.py:95
  26.8 27.0 %collective-permute-start.3 = (f32[8,16,2,128]{3,1,2,0:T(8,128)S(1)}, f32[8,16,2,128]{3,1,2,0:T(8,128)}, u32[]{:S(2)}, u32[]{:S(2)}) collective-permute-start(f32[8,16,2,128]{3,1,2,0:T(8,128)S(1)} %maximum_multiply_fusion.3), channel_id=1, source_target_pairs={{1,0},{2,1},{3,2},{4,3},{5,4},{6,5},{7,6},{9,8},{10,9},{11,10},{12... | collective-permute-start | bytes 393224 | tf_op jit(solution)/shard_map/ppermute | solution.py:96
  33.1 4.9 %copy-start = (f32[2,16,64,128]{3,2,1,0:T(8,128)S(1)}, f32[2,16,64,128]{3,2,1,0:T(8,128)}, u32[]{:S(2)}) copy-start(f32[2,16,64,128]{3,2,1,0:T(8,128)} %param.6) | copy-start | bytes 3145732
  33.1 8.0 %copy-start.2 = (f32[16,64,128]{2,1,0:T(8,128)S(1)}, f32[16,64,128]{2,1,0:T(8,128)}, u32[]{:S(2)}) copy-start(f32[16,64,128]{2,1,0:T(8,128)} %copy-done.1) | copy-start | bytes 1572868
  33.1 8.0 %copy-start.3 = (f32[16,64,128]{2,1,0:T(8,128)S(1)}, f32[16,64,128]{2,1,0:T(8,128)}, u32[]{:S(2)}) copy-start(f32[16,64,128]{2,1,0:T(8,128)} %get-tuple-element.51) | copy-start | bytes 1572868

commit v3 on v1

v3 whole, which is shorter than its diff:
```python
import jax
import jax.numpy as jnp
from jax import lax
from jax.experimental import pallas as pl
from jax.experimental.pallas import tpu as pltpu
from jax.sharding import PartitionSpec as P

NEWT = 4


growth = 0.5
latent_liquid = 1.0
latent_ice = 1.3


def increments(warmth, vapour, kinds):
    mixed = jax.nn.sigmoid(2.0 * warmth)
    liquid_share = jnp.where(kinds == 1, 1.0, jnp.where(kinds == 2, 0.0, mixed))
    latent = latent_liquid * liquid_share + latent_ice * (1.0 - liquid_share)
    active = (kinds > 0).astype(warmth.dtype)
    amount = jnp.zeros_like(warmth)
    for newton_step in range(NEWT):
        saturated = jnp.exp(growth * (warmth + latent * amount))
        excess = vapour - amount - saturated
        amount = amount + excess / (1.0 + growth * latent * saturated)
    amount = active * amount
    return (latent * amount, -amount, liquid_share * amount, (1.0 - liquid_share) * amount)


def sat_adjoint(warmth, vapour, kinds, cot_heat, cot_vapour, cot_liquid, cot_ice):

    def forward(first_in, second_in):
        return increments(first_in, second_in, kinds)

    unused, pullback = jax.vjp(forward, warmth, vapour)
    grad_heat, grad_vapour = pullback((cot_heat, cot_vapour, cot_liquid, cot_ice))
    return (cot_heat + grad_heat, cot_vapour + grad_vapour)


def cloudy_columns(cloud_list, cloud_count, columns):
    index = cloud_list[0, 0]
    count = cloud_count[0, 0]
    slot = jnp.arange(index.shape[0], dtype=jnp.int32)
    hit = (index[:, None] == jnp.arange(columns, dtype=jnp.int32)[None, :]) & (slot < count)[:, None]
    return jnp.any(hit, axis=0)


def sat_kernel(traj_ref, cot_ref, kind_ref, mask_ref, out_ref):
    rows = traj_ref.shape[1]
    tiles = traj_ref.shape[2] // 8

    def step(i, carry):
        r = i // tiles
        lat = pl.ds(pl.multiple_of((i % tiles) * 8, 8), 8)
        cot = [cot_ref[k, r, lat, :] for k in range(4)]
        new_heat, new_vapour = sat_adjoint(
            traj_ref[0, r, lat, :], traj_ref[1, r, lat, :], kind_ref[r, lat, :], *cot
        )
        cloudy = mask_ref[r, lat, :] > 0.0
        out_ref[0, r, lat, :] = jnp.where(cloudy, new_heat, cot[0])
        out_ref[1, r, lat, :] = jnp.where(cloudy, new_vapour, cot[1])
        return carry

    lax.fori_loop(0, rows * tiles, step, 0)


def first_pair(trajectory, cotangent, branch, mask):
    _, nlon, nlat, lev = trajectory.shape
    rows = 4
    return pl.pallas_call(
        sat_kernel,
        grid=(nlon // rows,),
        in_specs=[
            pl.BlockSpec((2, rows, nlat, lev), lambda i: (0, i, 0, 0)),
            pl.BlockSpec((4, rows, nlat, lev), lambda i: (0, i, 0, 0)),
            pl.BlockSpec((rows, nlat, lev), lambda i: (i, 0, 0)),
            pl.BlockSpec((rows, nlat, lev), lambda i: (i, 0, 0)),
        ],
        out_specs=pl.BlockSpec((2, rows, nlat, lev), lambda i: (0, i, 0, 0)),
        out_shape=jax.ShapeDtypeStruct((2, nlon, nlat, lev), jnp.float32),
    )(trajectory, cotangent, branch, mask)


def stencil_kernel(first_ref, cot_ref, cour_ref, lon_low, lon_high, lat_low, lat_high, out_ref, lon_pad, lat_pad):
    nlon, nlat = out_ref.shape[1], out_ref.shape[2]
    f = pl.program_id(0)

    def compute(src):
        for r in range(nlon):
            lon_pad[r + 2] = cour_ref[0, r] * src[0, r]
        lon_pad[0:2] = lon_low[0]
        lon_pad[nlon + 2:nlon + 4] = lon_high[0]
        for r in range(nlon):
            lat_pad[8:8 + nlat] = cour_ref[1, r] * src[0, r]
            lat_pad[6:8] = lat_low[0, 2 * r:2 * r + 2]
            lat_pad[8 + nlat:10 + nlat] = lat_high[0, 2 * r:2 * r + 2]
            d_lat = (8.0 * (lat_pad[9:9 + nlat] - lat_pad[7:7 + nlat]) - (lat_pad[10:10 + nlat] - lat_pad[6:6 + nlat])) / 12.0
            d_lon = (8.0 * (lon_pad[r + 3] - lon_pad[r + 1]) - (lon_pad[r + 4] - lon_pad[r])) / 12.0
            out_ref[0, r] = src[0, r] + d_lon + d_lat

    @pl.when(f < 2)
    def _():
        compute(first_ref)

    @pl.when(f >= 2)
    def _():
        compute(cot_ref)


def advect(first, cotangent, courant, lon_low, lon_high, lat_low, lat_high):
    fields, nlon, nlat, lev = cotangent.shape
    return pl.pallas_call(
        stencil_kernel,
        grid=(fields,),
        in_specs=[
            pl.BlockSpec((1, nlon, nlat, lev), lambda f: (jnp.minimum(f, 1), 0, 0, 0)),
            pl.BlockSpec((1, nlon, nlat, lev), lambda f: (f, 0, 0, 0)),
            pl.BlockSpec((2, nlon, nlat, lev), lambda f: (0, 0, 0, 0)),
            pl.BlockSpec((1, 2, nlat, lev), lambda f: (f, 0, 0, 0)),
            pl.BlockSpec((1, 2, nlat, lev), lambda f: (f, 0, 0, 0)),
            pl.BlockSpec((1, 2 * nlon, lev), lambda f: (f, 0, 0)),
            pl.BlockSpec((1, 2 * nlon, lev), lambda f: (f, 0, 0)),
        ],
        out_specs=pl.BlockSpec((1, nlon, nlat, lev), lambda f: (f, 0, 0, 0)),
        out_shape=jax.ShapeDtypeStruct(cotangent.shape, jnp.float32),
        scratch_shapes=[
            pltpu.VMEM((nlon + 4, nlat, lev), jnp.float32),
            pltpu.VMEM((nlat + 16, lev), jnp.float32),
        ],
    )(first, cotangent, courant, lon_low, lon_high, lat_low, lat_high)


def neighbours(axis, periodic):
    count = lax.axis_size(axis)
    forward = [(i, i + 1) for i in range(count - 1)]
    if periodic:
        forward.append((count - 1, 0))
    backward = [(target, source) for source, target in forward]
    return forward, backward


def on_device(trajectory, cotangent, courant, branch, cloud_list, cloud_count):
    fields, nlon, nlat, lev = cotangent.shape
    cloudy = cloudy_columns(cloud_list, cloud_count, nlon * nlat)
    mask = jnp.broadcast_to(cloudy.reshape(nlon, nlat, 1), (nlon, nlat, lev)).astype(jnp.float32)
    first = first_pair(trajectory, cotangent, branch, mask)
    after = lambda dim, start: jnp.concatenate(
        [lax.slice_in_dim(first, start, start + 2, axis=dim), lax.slice_in_dim(cotangent[2:], start, start + 2, axis=dim)], 0
    )
    weight = lambda dim, start: lax.slice_in_dim(courant[dim - 1], start, start + 2, axis=dim - 1)
    forward, backward = neighbours("lon", True)
    lon_low = lax.ppermute(weight(1, nlon - 2) * after(1, nlon - 2), "lon", forward)
    lon_high = lax.ppermute(weight(1, 0) * after(1, 0), "lon", backward)
    forward, backward = neighbours("lat", False)
    flat = lambda a: a.reshape(fields, 2 * nlon, lev)
    lat_low = lax.ppermute(flat(weight(2, nlat - 2) * after(2, nlat - 2)), "lat", forward)
    lat_high = lax.ppermute(flat(weight(2, 0) * after(2, 0)), "lat", backward)
    return advect(first, cotangent, courant, lon_low, lon_high, lat_low, lat_high)


def solution(mesh):
    placed = (
        P(None, "lon", "lat", None),
        P(None, "lon", "lat", None),
        P(None, "lon", "lat", None),
        P("lon", "lat", None),
        P("lon", "lat", None),
        P("lon", "lat"),
    )
    return jax.shard_map(
        on_device,
        mesh=mesh,
        in_specs=placed,
        out_specs=P(None, "lon", "lat", None),
        check_vma=False,
    )
```

time: 42.1 us -> 58.1 us (1.38)
  the two profiles are of different devices: /device:TPU:2 before, /device:TPU:8 now
where the time goes in v3:
time: 58.1 us; the launch traced here: 57.7 us
  Pallas kernels  28.4 us (49%)
  starting transfers between devices  13.3 us (23%)
  local copies, waits for them, and re-layouts  7.99 us (14%)
  waiting for transfers between devices  5.83 us (10%)
  other arithmetic  1.32 us (2%)
  between operations  0.78 us (1%)
    pallas_call x1, Pallas kernels, first_pair(): pl.pallas_call(sat_kernel, grid=(nlon // rows,), in_specs=[pl.BlockSpec((...  19.9 us
    pallas_call x1, Pallas kernels, advect(): pl.pallas_call(stencil_kernel, grid=(fields,), in_specs=[pl.BlockSpec((1,...  8.49 us
    ppermute x1, starting transfers between devices, on_device(): lon_high = lax.ppermute(weight(1, 0) * after(1, 0), 'lon', backward)  7.1 us
    ppermute x1, waiting for transfers between devices, on_device(): lat_high = lax.ppermute(flat(weight(2, 0) * after(2, 0)), 'lat', backward)  4.89 us
    ppermute x1, starting transfers between devices, on_device(): lax.ppermute(flat(weight(2, nlat - 2) * after(2, nlat - 2)), 'lat', forward)  4.18 us
    slice x2, local copies, waits for them, and re-layouts, on_device(): lax.slice_in_dim(cotangent[2:], start, start + 2, axis=dim)  2.37 us
    slice x2, local copies, waits for them, and re-layouts, on_device(): lax.slice_in_dim(first, start, start + 2, axis=dim)  1.98 us
    ppermute x1, starting transfers between devices, on_device(): lat_high = lax.ppermute(flat(weight(2, 0) * after(2, 0)), 'lat', backward)  1.92 us
  transfers between devices with their start and end apart: 4, of which 2 were waited for; matrix products, arithmetic and copies ran while one was open for 4% of the time, Pallas kernels for 0%

profile of v3, /device:TPU:8, one launch (start us, length us, event | category | flops | bytes accessed | tf_op | source)
XLA Modules:
  0.0 57.7 jit_solution(13736316765113021046)
XLA Ops:
  0.7 0.7 %reduce = s32[768]{0:T(1024)S(1)} reduce(s32[1,1,768]{2,1,0:T(1,128)} %param.10, s32[]{:T(128)} %constant.8), dimensions={0,1}, to_apply=%param.10.reduce_sub_computation | reduce | bytes 6148 | tf_op args[4]
  1.4 0.5 fusion.1
  1.9 0.1 reshape.25
  1.9 0.9 %slice_bitcast_fusion.1 = (f32[2,64,128]{2,1,0:T(8,128)S(1)}, f32[2,64,128]{2,1,0:T(8,128)S(1)}) fusion(f32[2,16,64,128]{3,2,1,0:T(8,128)} %cour_ref.1), kind=kLoop, calls=%fused_computation.8 | loop fusion | bytes 262144 | tf_op jit(solution)/shard_map/mul | solution.py:153
  2.8 1.2 %fusion.3 = (f32[6,2,64,128]{3,2,1,0:T(8,128)S(1)}, f32[6,2,64,128]{3,2,1,0:T(8,128)S(1)}) fusion(f32[8,16,64,128]{3,2,1,0:T(8,128)} %cot_ref.3), kind=kLoop, calls=%fused_computation.12 | loop fusion | bytes 1572864 | tf_op jit(solution)/shard_map/slice | solution.py:148
  4.0 1.0 %broadcast_in_dim.2.mask_ref = f32[16,64,128]{2,1,0:T(8,128)} broadcast(f32[16,64]{1,0:T(8,128)S(1)} %reshape.25), dimensions={0,1} | broadcast | bytes 528384 | tf_op jit(solution)/shard_map/broadcast_in_dim | solution.py:145
  5.0 0.0 copy-start
  5.0 19.9 %shard_map.64.first_ref = f32[2,16,64,128]{3,2,1,0:T(8,128)} custom-call(f32[2,16,64,128]{3,2,1,0:T(8,128)} %traj_ref.1, f32[8,16,64,128]{3,2,1,0:T(8,128)} %cot_ref.3, s32[16,64,128]{2,1,0:T(8,128)} %kind_ref.1, f32[16,64,128]{2,1,0:T(8,128)} %broadcast_in_dim.2.mask_ref), custom_call_target="tpu_custom_call" | custom-call | tf_op jit(solution)/shard_map/pallas_call | solution.py:70
  24.9 1.0 %fusion.5 = (f32[2,2,64,128]{3,2,1,0:T(8,128)S(1)}, f32[2,2,64,128]{3,2,1,0:T(8,128)S(1)}) fusion(f32[2,16,64,128]{3,2,1,0:T(8,128)} %shard_map.64.first_ref), kind=kLoop, calls=%fused_computation.14 | loop fusion | bytes 524288 | tf_op jit(solution)/shard_map/slice | solution.py:148
  26.0 0.1 collective-permute-start
  26.1 7.1 %collective-permute-start.1 = (f32[8,2,64,128]{3,2,1,0:T(8,128)S(1)}, f32[8,2,64,128]{3,2,1,0:T(8,128)S(1)}, u32[]{:S(2)}, u32[]{:S(2)}) collective-permute-start(f32[8,2,64,128]{3,2,1,0:T(8,128)S(1)} %maximum_multiply_fusion.1), channel_id=1, source_target_pairs={{8,0},{16,8},{24,16},{32,24},{40,32},{48,40},{56,48},{64,56},{72,6... | collective-permute-start | bytes 1572872 | tf_op jit(solution)/shard_map/ppermute | solution.py:153
  33.2 1.2 %fusion.2 = (f32[6,16,2,128]{3,2,1,0:T(2,128)S(1)}, f32[6,16,2,128]{3,2,1,0:T(2,128)S(1)}) fusion(f32[8,16,64,128]{3,2,1,0:T(8,128)} %cot_ref.3), kind=kLoop, calls=%fused_computation.11 | loop fusion | bytes 393216 | tf_op jit(solution)/shard_map/slice | solution.py:148
  34.4 1.0 %fusion.4 = (f32[2,16,2,128]{3,2,1,0:T(2,128)S(1)}, f32[2,16,2,128]{3,2,1,0:T(2,128)S(1)}) fusion(f32[2,16,64,128]{3,2,1,0:T(8,128)} %shard_map.64.first_ref), kind=kLoop, calls=%fused_computation.13 | loop fusion | bytes 131072 | tf_op jit(solution)/shard_map/slice | solution.py:148
  35.4 0.0 copy-done
  35.5 4.2 %collective-permute-start.2 = (f32[8,32,128]{2,1,0:T(8,128)S(1)}, f32[8,32,128]{2,1,0:T(8,128)S(1)}, u32[]{:S(2)}, u32[]{:S(2)}) collective-permute-start(f32[8,32,128]{2,1,0:T(8,128)S(1)} %maximum_multiply_fusion.2), channel_id=1, source_target_pairs={{0,1},{1,2},{2,3},{3,4},{4,5},{5,6},{6,7},{8,9},{9,10},{10,11},{11... | collective-permute-start | bytes 393224 | tf_op jit(solution)/shard_map/ppermute | solution.py:156
  39.7 1.9 %collective-permute-start.3 = (f32[8,32,128]{2,1,0:T(8,128)S(1)}, f32[8,32,128]{2,1,0:T(8,128)S(1)}, u32[]{:S(2)}, u32[]{:S(2)}) collective-permute-start(f32[8,32,128]{2,1,0:T(8,128)S(1)} %maximum_multiply_fusion.3), channel_id=1, source_target_pairs={{1,0},{2,1},{3,2},{4,3},{5,4},{6,5},{7,6},{9,8},{10,9},{11,10},{12... | collective-permute-start | bytes 393224 | tf_op jit(solution)/shard_map/ppermute | solution.py:157
  41.7 0.9 %collective-permute-done.2.lat_low = f32[8,32,128]{2,1,0:T(8,128)S(1)} collective-permute-done((f32[8,32,128]{2,1,0:T(8,128)S(1)}, f32[8,32,128]{2,1,0:T(8,128)S(1)}, u32[]{:S(2)}, u32[]{:S(2)}) %collective-permute-start.2) | collective-permute-done | bytes 131104 | tf_op jit(solution)/shard_map/ppermute | solution.py:156
  42.6 0.0 copy-start.3
  42.6 4.9 %collective-permute-done.3.lat_high = f32[8,32,128]{2,1,0:T(8,128)S(1)} collective-permute-done((f32[8,32,128]{2,1,0:T(8,128)S(1)}, f32[8,32,128]{2,1,0:T(8,128)S(1)}, u32[]{:S(2)}, u32[]{:S(2)}) %collective-permute-start.3) | collective-permute-done | bytes 131104 | tf_op jit(solution)/shard_map/ppermute | solution.py:157
  47.5 0.0 copy-start.4
  47.5 0.0 collective-permute-done.lon_low
  47.5 0.0 copy-start.1
  47.5 0.0 collective-permute-done.1.lon_high
  47.5 0.0 copy-done.3
  47.5 0.6 %copy-done.4 = f32[8,32,128]{2,1,0:T(8,128)} copy-done((f32[8,32,128]{2,1,0:T(8,128)}, f32[8,32,128]{2,1,0:T(8,128)S(1)}, u32[]{:S(2)}) %copy-start.4) | copy-done | bytes 131096
  48.2 0.2 copy-done.1
  48.4 0.0 copy-start.2
  48.4 0.8 %copy-done.2 = f32[8,2,64,128]{3,2,1,0:T(8,128)} copy-done((f32[8,2,64,128]{3,2,1,0:T(8,128)}, f32[8,2,64,128]{3,2,1,0:T(8,128)S(1)}, u32[]{:S(2)}) %copy-start.2) | copy-done | bytes 524312
  49.2 8.5 %shard_map.65 = f32[8,16,64,128]{3,2,1,0:T(8,128)} custom-call(f32[2,16,64,128]{3,2,1,0:T(8,128)} %shard_map.64.first_ref, f32[8,16,64,128]{3,2,1,0:T(8,128)} %cot_ref.3, f32[2,16,64,128]{3,2,1,0:T(8,128)} %cour_ref.1, f32[8,2,64,128]{3,2,1,0:T(8,128)} %copy-done.1, f32[8,2,64,128]{3,2,1,0:T(8,128)} %copy-done.2, f32[8,32,128]{2,1,0:T(8,128)} %copy-done.3, ...), custom_call_target="tpu_custom_call" | custom-call | tf_op jit(solution)/shard_map/pallas_call | solution.py:112
  (8 shorter events, 0.2 us)
Async XLA Ops:
  5.0 30.4 %copy-start = (f32[2,16,64,128]{3,2,1,0:T(8,128)S(1)}, f32[2,16,64,128]{3,2,1,0:T(8,128)}, u32[]{:S(2)}) copy-start(f32[2,16,64,128]{3,2,1,0:T(8,128)} %cour_ref.1) | copy-start | bytes 3145732
  26.0 21.5 %collective-permute-start = (f32[8,2,64,128]{3,2,1,0:T(8,128)S(1)}, f32[8,2,64,128]{3,2,1,0:T(8,128)S(1)}, u32[]{:S(2)}, u32[]{:S(2)}) collective-permute-start(f32[8,2,64,128]{3,2,1,0:T(8,128)S(1)} %maximum_multiply_fusion), channel_id=1, source_target_pairs={{0,8},{8,16},{16,24},{24,32},{32,40},{40,48},{48,56},{56,64},{64,7... | collective-permute-start | bytes 1572872 | tf_op jit(solution)/shard_map/ppermute | solution.py:152
  26.1 21.4 %collective-permute-start.1 = (f32[8,2,64,128]{3,2,1,0:T(8,128)S(1)}, f32[8,2,64,128]{3,2,1,0:T(8,128)S(1)}, u32[]{:S(2)}, u32[]{:S(2)}) collective-permute-start(f32[8,2,64,128]{3,2,1,0:T(8,128)S(1)} %maximum_multiply_fusion.1), channel_id=1, source_target_pairs={{8,0},{16,8},{24,16},{32,24},{40,32},{48,40},{56,48},{64,56},{72,6... | collective-permute-start | bytes 1572872 | tf_op jit(solution)/shard_map/ppermute | solution.py:153
  35.5 7.1 %collective-permute-start.2 = (f32[8,32,128]{2,1,0:T(8,128)S(1)}, f32[8,32,128]{2,1,0:T(8,128)S(1)}, u32[]{:S(2)}, u32[]{:S(2)}) collective-permute-start(f32[8,32,128]{2,1,0:T(8,128)S(1)} %maximum_multiply_fusion.2), channel_id=1, source_target_pairs={{0,1},{1,2},{2,3},{3,4},{4,5},{5,6},{6,7},{8,9},{9,10},{10,11},{11... | collective-permute-start | bytes 393224 | tf_op jit(solution)/shard_map/ppermute | solution.py:156
  39.7 7.8 %collective-permute-start.3 = (f32[8,32,128]{2,1,0:T(8,128)S(1)}, f32[8,32,128]{2,1,0:T(8,128)S(1)}, u32[]{:S(2)}, u32[]{:S(2)}) collective-permute-start(f32[8,32,128]{2,1,0:T(8,128)S(1)} %maximum_multiply_fusion.3), channel_id=1, source_target_pairs={{1,0},{2,1},{3,2},{4,3},{5,4},{6,5},{7,6},{9,8},{10,9},{11,10},{12... | collective-permute-start | bytes 393224 | tf_op jit(solution)/shard_map/ppermute | solution.py:157
  42.6 4.9 %copy-start.3 = (f32[8,32,128]{2,1,0:T(8,128)}, f32[8,32,128]{2,1,0:T(8,128)S(1)}, u32[]{:S(2)}) copy-start(f32[8,32,128]{2,1,0:T(8,128)S(1)} %collective-permute-done.2.lat_low) | copy-start | bytes 393220
  47.5 0.6 %copy-start.4 = (f32[8,32,128]{2,1,0:T(8,128)}, f32[8,32,128]{2,1,0:T(8,128)S(1)}, u32[]{:S(2)}) copy-start(f32[8,32,128]{2,1,0:T(8,128)S(1)} %collective-permute-done.3.lat_high) | copy-start | bytes 393220
  47.5 0.9 %copy-start.1 = (f32[8,2,64,128]{3,2,1,0:T(8,128)}, f32[8,2,64,128]{3,2,1,0:T(8,128)S(1)}, u32[]{:S(2)}) copy-start(f32[8,2,64,128]{3,2,1,0:T(8,128)S(1)} %collective-permute-done.lon_low) | copy-start | bytes 1572868
  48.4 0.8 %copy-start.2 = (f32[8,2,64,128]{3,2,1,0:T(8,128)}, f32[8,2,64,128]{3,2,1,0:T(8,128)S(1)}, u32[]{:S(2)}) copy-start(f32[8,2,64,128]{3,2,1,0:T(8,128)S(1)} %collective-permute-done.1.lon_high) | copy-start | bytes 1572868

commit v4 on v3

--- a/solution.py
+++ b/solution.py
@@ -46,12 +46,11 @@
 
 
 def sat_kernel(traj_ref, cot_ref, kind_ref, mask_ref, out_ref):
-    rows = traj_ref.shape[1]
-    tiles = traj_ref.shape[2] // 8
-
-    def step(i, carry):
-        r = i // tiles
-        lat = pl.ds(pl.multiple_of((i % tiles) * 8, 8), 8)
+    rows, nlat = traj_ref.shape[1], traj_ref.shape[2]
+    chunk = 32
+    for i in range(rows * (nlat // chunk)):
+        r = i // (nlat // chunk)
+        lat = pl.ds((i % (nlat // chunk)) * chunk, chunk)
         cot = [cot_ref[k, r, lat, :] for k in range(4)]
         new_heat, new_vapour = sat_adjoint(
             traj_ref[0, r, lat, :], traj_ref[1, r, lat, :], kind_ref[r, lat, :], *cot
@@ -59,14 +58,11 @@
         cloudy = mask_ref[r, lat, :] > 0.0
         out_ref[0, r, lat, :] = jnp.where(cloudy, new_heat, cot[0])
         out_ref[1, r, lat, :] = jnp.where(cloudy, new_vapour, cot[1])
-        return carry
-
-    lax.fori_loop(0, rows * tiles, step, 0)
 
 
 def first_pair(trajectory, cotangent, branch, mask):
     _, nlon, nlat, lev = trajectory.shape
-    rows = 4
+    rows = 8
     return pl.pallas_call(
         sat_kernel,
         grid=(nlon // rows,),
@@ -81,19 +77,20 @@
     )(trajectory, cotangent, branch, mask)
 
 
-def stencil_kernel(first_ref, cot_ref, cour_ref, lon_low, lon_high, lat_low, lat_high, out_ref, lon_pad, lat_pad):
+def stencil_kernel(first_ref, cot_ref, cour_ref, out_ref, lon_pad, lat_pad):
     nlon, nlat = out_ref.shape[1], out_ref.shape[2]
     f = pl.program_id(0)
+    zeros = jnp.zeros((2,) + lon_pad.shape[1:], jnp.float32)
 
     def compute(src):
         for r in range(nlon):
             lon_pad[r + 2] = cour_ref[0, r] * src[0, r]
-        lon_pad[0:2] = lon_low[0]
-        lon_pad[nlon + 2:nlon + 4] = lon_high[0]
+        lon_pad[0:2] = zeros
+        lon_pad[nlon + 2:nlon + 4] = zeros
+        lat_pad[6:8] = zeros[0, 0:2]
+        lat_pad[8 + nlat:10 + nlat] = zeros[0, 0:2]
         for r in range(nlon):
             lat_pad[8:8 + nlat] = cour_ref[1, r] * src[0, r]
-            lat_pad[6:8] = lat_low[0, 2 * r:2 * r + 2]
-            lat_pad[8 + nlat:10 + nlat] = lat_high[0, 2 * r:2 * r + 2]
             d_lat = (8.0 * (lat_pad[9:9 + nlat] - lat_pad[7:7 + nlat]) - (lat_pad[10:10 + nlat] - lat_pad[6:6 + nlat])) / 12.0
             d_lon = (8.0 * (lon_pad[r + 3] - lon_pad[r + 1]) - (lon_pad[r + 4] - lon_pad[r])) / 12.0
             out_ref[0, r] = src[0, r] + d_lon + d_lat
@@ -107,8 +104,9 @@
         compute(cot_ref)
 
 
-def advect(first, cotangent, courant, lon_low, lon_high, lat_low, lat_high):
+def advect(first, cotangent, courant):
     fields, nlon, nlat, lev = cotangent.shape
+    size = cotangent.size * 4
     return pl.pallas_call(
         stencil_kernel,
         grid=(fields,),
@@ -116,10 +114,6 @@
             pl.BlockSpec((1, nlon, nlat, lev), lambda f: (jnp.minimum(f, 1), 0, 0, 0)),
             pl.BlockSpec((1, nlon, nlat, lev), lambda f: (f, 0, 0, 0)),
             pl.BlockSpec((2, nlon, nlat, lev), lambda f: (0, 0, 0, 0)),
-            pl.BlockSpec((1, 2, nlat, lev), lambda f: (f, 0, 0, 0)),
-            pl.BlockSpec((1, 2, nlat, lev), lambda f: (f, 0, 0, 0)),
-            pl.BlockSpec((1, 2 * nlon, lev), lambda f: (f, 0, 0)),
-            pl.BlockSpec((1, 2 * nlon, lev), lambda f: (f, 0, 0)),
         ],
         out_specs=pl.BlockSpec((1, nlon, nlat, lev), lambda f: (f, 0, 0, 0)),
         out_shape=jax.ShapeDtypeStruct(cotangent.shape, jnp.float32),
@@ -127,7 +121,82 @@
             pltpu.VMEM((nlon + 4, nlat, lev), jnp.float32),
             pltpu.VMEM((nlat + 16, lev), jnp.float32),
         ],
-    )(first, cotangent, courant, lon_low, lon_high, lat_low, lat_high)
+        cost_estimate=pl.CostEstimate(flops=12 * cotangent.size, transcendentals=0, bytes_accessed=3 * size),
+    )(first, cotangent, courant)
+
+
+def halo_kernel(lon_low, lon_high, lat_low, lat_high, out_hbm, out_ref, lon_lo_buf, lon_hi_buf, lat_lo_buf, lat_hi_buf, sems):
+    fields, nlon, nlat, lev = out_hbm.shape
+    regions = [
+        (out_hbm.at[:, 0:2], lon_lo_buf),
+        (out_hbm.at[:, nlon - 2:nlon], lon_hi_buf),
+        (out_hbm.at[:, 2:nlon - 2, 0:8], lat_lo_buf),
+        (out_hbm.at[:, 2:nlon - 2, nlat - 8:nlat], lat_hi_buf),
+    ]
+    copies = [pltpu.make_async_copy(src, dst, sems.at[i]) for i, (src, dst) in enumerate(regions)]
+    for c in copies:
+        c.start()
+    for c in copies:
+        c.wait()
+    lane = lax.broadcasted_iota(jnp.int32, (8, lev), 0)
+
+    def lat_fix(tile, low_rows, high_rows, at_low):
+        if at_low:
+            row0 = (low_rows[0:1] - 8.0 * low_rows[1:2]) / 12.0
+            row1 = low_rows[1:2] / 12.0
+            return tile + jnp.where(lane == 0, row0, jnp.where(lane == 1, row1, 0.0))
+        row6 = -high_rows[0:1] / 12.0
+        row7 = (8.0 * high_rows[0:1] - high_rows[1:2]) / 12.0
+        return tile + jnp.where(lane == 6, row6, jnp.where(lane == 7, row7, 0.0))
+
+    for f in range(fields):
+        lo = lon_low[f]
+        hi = lon_high[f]
+        first = [(lo[0] - 8.0 * lo[1]) / 12.0, lo[1] / 12.0]
+        last = [-hi[0] / 12.0, (8.0 * hi[0] - hi[1]) / 12.0]
+        for k, r in enumerate((0, 1)):
+            block = lon_lo_buf[f, k] + first[k]
+            low_rows = lat_low[f, 2 * r:2 * r + 2]
+            high_rows = lat_high[f, 2 * r:2 * r + 2]
+            lon_lo_buf[f, k] = block
+            lon_lo_buf[f, k, 0:8] = lat_fix(block[0:8], low_rows, high_rows, True)
+            lon_lo_buf[f, k, nlat - 8:nlat] = lat_fix(block[nlat - 8:nlat], low_rows, high_rows, False)
+        for k, r in enumerate((nlon - 2, nlon - 1)):
+            block = lon_hi_buf[f, k] + last[k]
+            low_rows = lat_low[f, 2 * r:2 * r + 2]
+            high_rows = lat_high[f, 2 * r:2 * r + 2]
+            lon_hi_buf[f, k] = block
+            lon_hi_buf[f, k, 0:8] = lat_fix(block[0:8], low_rows, high_rows, True)
+            lon_hi_buf[f, k, nlat - 8:nlat] = lat_fix(block[nlat - 8:nlat], low_rows, high_rows, False)
+        for r in range(2, nlon - 2):
+            low_rows = lat_low[f, 2 * r:2 * r + 2]
+            high_rows = lat_high[f, 2 * r:2 * r + 2]
+            lat_lo_buf[f, r - 2] = lat_fix(lat_lo_buf[f, r - 2], low_rows, high_rows, True)
+            lat_hi_buf[f, r - 2] = lat_fix(lat_hi_buf[f, r - 2], low_rows, high_rows, False)
+    copies = [pltpu.make_async_copy(dst, src, sems.at[i]) for i, (src, dst) in enumerate(regions)]
+    for c in copies:
+        c.start()
+    for c in copies:
+        c.wait()
+
+
+def add_halos(out, lon_low, lon_high, lat_low, lat_high):
+    fields, nlon, nlat, lev = out.shape
+    vmem = pl.BlockSpec(memory_space=pltpu.VMEM)
+    return pl.pallas_call(
+        halo_kernel,
+        in_specs=[vmem, vmem, vmem, vmem, pl.BlockSpec(memory_space=pl.ANY)],
+        out_specs=pl.BlockSpec(memory_space=pl.ANY),
+        out_shape=jax.ShapeDtypeStruct(out.shape, jnp.float32),
+        scratch_shapes=[
+            pltpu.VMEM((fields, 2, nlat, lev), jnp.float32),
+            pltpu.VMEM((fields, 2, nlat, lev), jnp.float32),
+            pltpu.VMEM((fields, nlon - 4, 8, lev), jnp.float32),
+            pltpu.VMEM((fields, nlon - 4, 8, lev), jnp.float32),
+            pltpu.SemaphoreType.DMA((4,)),
+        ],
+        input_output_aliases={4: 0},
+    )(lon_low, lon_high, lat_low, lat_high, out)
 
 
 def neighbours(axis, periodic):
@@ -155,7 +224,8 @@
     flat = lambda a: a.reshape(fields, 2 * nlon, lev)
     lat_low = lax.ppermute(flat(weight(2, nlat - 2) * after(2, nlat - 2)), "lat", forward)
     lat_high = lax.ppermute(flat(weight(2, 0) * after(2, 0)), "lat", backward)
-    return advect(first, cotangent, courant, lon_low, lon_high, lat_low, lat_high)
+    out = advect(first, cotangent, courant)
+    return add_halos(out, lon_low, lon_high, lat_low, lat_high)
 
 
 def solution(mesh):

time: 58.1 us -> 43.3 us (0.75)
  the two profiles are of different devices: /device:TPU:8 before, /device:TPU:2 now
where the time goes in v4:
time: 43.3 us; the launch traced here: 42.8 us
  Pallas kernels  17.8 us (41%)
  starting transfers between devices  14.8 us (34%)
  local copies, waits for them, and re-layouts  7.98 us (18%)
  other arithmetic  1.31 us (3%)
  between operations  0.81 us (2%)
    pallas_call x1, Pallas kernels, advect(): pl.pallas_call(stencil_kernel, grid=(fields,), in_specs=[pl.BlockSpec((1,...  8.16 us
    ppermute x1, starting transfers between devices, on_device(): lon_high = lax.ppermute(weight(1, 0) * after(1, 0), 'lon', backward)  8 us
    pallas_call x1, Pallas kernels, first_pair(): pl.pallas_call(sat_kernel, grid=(nlon // rows,), in_specs=[pl.BlockSpec((...  5.59 us
    ppermute x1, starting transfers between devices, on_device(): lat_high = lax.ppermute(flat(weight(2, 0) * after(2, 0)), 'lat', backward)  4.16 us
    pallas_call x1, Pallas kernels, add_halos(): pl.pallas_call(halo_kernel, in_specs=[vmem, vmem, vmem, vmem, pl.BlockSpe...  4.1 us
    ppermute x1, starting transfers between devices, on_device(): lax.ppermute(flat(weight(2, nlat - 2) * after(2, nlat - 2)), 'lat', forward)  2.59 us
    slice x2, local copies, waits for them, and re-layouts, on_device(): lax.slice_in_dim(cotangent[2:], start, start + 2, axis=dim)  2.37 us
    slice x2, local copies, waits for them, and re-layouts, on_device(): lax.slice_in_dim(first, start, start + 2, axis=dim)  1.98 us
  transfers between devices with their start and end apart: 4, of which 0 were waited for; matrix products, arithmetic and copies ran while one was open for 5% of the time, Pallas kernels for 19%

profile of v4, /device:TPU:2, one launch (start us, length us, event | category | flops | bytes accessed | tf_op | source)
XLA Modules:
  0.0 42.8 jit_solution(15896841613810609947)
XLA Ops:
  0.7 0.7 %reduce = s32[768]{0:T(1024)S(1)} reduce(s32[1,1,768]{2,1,0:T(1,128)} %param.10, s32[]{:T(128)} %constant.8), dimensions={0,1}, to_apply=%param.10.reduce_sub_computation | reduce | bytes 6148 | tf_op args[4]
  1.4 0.5 %fusion.1 = pred[1024]{0:T(1024)(128)(4,1)S(1)} fusion(s32[768]{0:T(1024)S(1)} %reduce, pred[768]{0:T(1024)(128)(4,1)S(1)} %iota_compare_fusion.1), kind=kLoop, calls=%fused_computation.2 | loop fusion | flops 2358272 | bytes 4864 | tf_op jit(solution)/shard_map/reduce_or | solution.py:45
  1.9 0.1 reshape.25
  1.9 0.9 %slice_bitcast_fusion.1 = (f32[2,64,128]{2,1,0:T(8,128)S(1)}, f32[2,64,128]{2,1,0:T(8,128)S(1)}) fusion(f32[2,16,64,128]{3,2,1,0:T(8,128)} %cour_ref.1), kind=kLoop, calls=%fused_computation.8 | loop fusion | bytes 262144 | tf_op jit(solution)/shard_map/mul | solution.py:222
  2.8 1.2 %fusion.3 = (f32[6,2,64,128]{3,2,1,0:T(8,128)S(1)}, f32[6,2,64,128]{3,2,1,0:T(8,128)S(1)}) fusion(f32[8,16,64,128]{3,2,1,0:T(8,128)} %cot_ref.3), kind=kLoop, calls=%fused_computation.12 | loop fusion | bytes 1572864 | tf_op jit(solution)/shard_map/slice | solution.py:217
  4.0 1.0 %broadcast_in_dim.2.mask_ref = f32[16,64,128]{2,1,0:T(8,128)} broadcast(f32[16,64]{1,0:T(8,128)S(1)} %reshape.25), dimensions={0,1} | broadcast | bytes 528384 | tf_op jit(solution)/shard_map/broadcast_in_dim | solution.py:214
  5.0 0.0 copy-start
  5.0 5.6 %shard_map.64.first_ref = f32[2,16,64,128]{3,2,1,0:T(8,128)} custom-call(f32[2,16,64,128]{3,2,1,0:T(8,128)} %traj_ref.1, f32[8,16,64,128]{3,2,1,0:T(8,128)} %cot_ref.3, s32[16,64,128]{2,1,0:T(8,128)} %kind_ref.1, f32[16,64,128]{2,1,0:T(8,128)} %broadcast_in_dim.2.mask_ref), custom_call_target="tpu_custom_call" | custom-call | tf_op jit(solution)/shard_map/pallas_call | solution.py:66
  10.6 1.0 %fusion.5 = (f32[2,2,64,128]{3,2,1,0:T(8,128)S(1)}, f32[2,2,64,128]{3,2,1,0:T(8,128)S(1)}) fusion(f32[2,16,64,128]{3,2,1,0:T(8,128)} %shard_map.64.first_ref), kind=kLoop, calls=%fused_computation.14 | loop fusion | bytes 524288 | tf_op jit(solution)/shard_map/slice | solution.py:217
  11.6 0.1 collective-permute-start
  11.8 8.0 %collective-permute-start.1 = (f32[8,2,64,128]{3,2,1,0:T(8,128)S(1)}, f32[8,2,64,128]{3,2,1,0:T(8,128)S(1)}, u32[]{:S(2)}, u32[]{:S(2)}) collective-permute-start(f32[8,2,64,128]{3,2,1,0:T(8,128)S(1)} %maximum_multiply_fusion.1), channel_id=1, source_target_pairs={{8,0},{16,8},{24,16},{32,24},{40,32},{48,40},{56,48},{64,56},{72,6... | collective-permute-start | bytes 1572872 | tf_op jit(solution)/shard_map/ppermute | solution.py:222
  19.8 1.2 %fusion.2 = (f32[6,16,2,128]{3,2,1,0:T(2,128)S(1)}, f32[6,16,2,128]{3,2,1,0:T(2,128)S(1)}) fusion(f32[8,16,64,128]{3,2,1,0:T(8,128)} %cot_ref.3), kind=kLoop, calls=%fused_computation.11 | loop fusion | bytes 393216 | tf_op jit(solution)/shard_map/slice | solution.py:217
  21.0 1.0 %fusion.4 = (f32[2,16,2,128]{3,2,1,0:T(2,128)S(1)}, f32[2,16,2,128]{3,2,1,0:T(2,128)S(1)}) fusion(f32[2,16,64,128]{3,2,1,0:T(8,128)} %shard_map.64.first_ref), kind=kLoop, calls=%fused_computation.13 | loop fusion | bytes 131072 | tf_op jit(solution)/shard_map/slice | solution.py:217
  22.0 0.0 copy-done
  22.1 2.6 %collective-permute-start.2 = (f32[8,32,128]{2,1,0:T(8,128)S(1)}, f32[8,32,128]{2,1,0:T(8,128)S(1)}, u32[]{:S(2)}, u32[]{:S(2)}) collective-permute-start(f32[8,32,128]{2,1,0:T(8,128)S(1)} %maximum_multiply_fusion.2), channel_id=1, source_target_pairs={{0,1},{1,2},{2,3},{3,4},{4,5},{5,6},{6,7},{8,9},{9,10},{10,11},{11... | collective-permute-start | bytes 393224 | tf_op jit(solution)/shard_map/ppermute | solution.py:225
  24.7 4.2 %collective-permute-start.3 = (f32[8,32,128]{2,1,0:T(8,128)S(1)}, f32[8,32,128]{2,1,0:T(8,128)S(1)}, u32[]{:S(2)}, u32[]{:S(2)}) collective-permute-start(f32[8,32,128]{2,1,0:T(8,128)S(1)} %maximum_multiply_fusion.3), channel_id=1, source_target_pairs={{1,0},{2,1},{3,2},{4,3},{5,4},{6,5},{7,6},{9,8},{10,9},{11,10},{12... | collective-permute-start | bytes 393224 | tf_op jit(solution)/shard_map/ppermute | solution.py:226
  28.8 8.2 %shard_map.65.out_hbm = f32[8,16,64,128]{3,2,1,0:T(8,128)} custom-call(f32[2,16,64,128]{3,2,1,0:T(8,128)} %shard_map.64.first_ref, f32[8,16,64,128]{3,2,1,0:T(8,128)} %cot_ref.3, f32[2,16,64,128]{3,2,1,0:T(8,128)} %cour_ref.1), custom_call_target="tpu_custom_call" | custom-call | flops 12582912 | bytes 12582912 | tf_op jit(solution)/shard_map/pallas_call | solution.py:110
  37.0 0.0 collective-permute-done.2.lat_low
  37.0 0.0 copy-start.3
  37.0 0.0 collective-permute-done.3.lat_high
  37.0 0.0 copy-start.4
  37.0 0.0 collective-permute-done.lon_low
  37.0 0.0 copy-start.1
  37.1 0.0 collective-permute-done.1.lon_high
  37.1 0.6 %copy-done.3 = f32[8,32,128]{2,1,0:T(8,128)} copy-done((f32[8,32,128]{2,1,0:T(8,128)}, f32[8,32,128]{2,1,0:T(8,128)S(1)}, u32[]{:S(2)}) %copy-start.3) | copy-done | bytes 131096
  37.7 0.1 copy-done.4
  37.7 0.2 copy-done.1
  37.9 0.0 copy-start.2
  37.9 0.8 %copy-done.2 = f32[8,2,64,128]{3,2,1,0:T(8,128)} copy-done((f32[8,2,64,128]{3,2,1,0:T(8,128)}, f32[8,2,64,128]{3,2,1,0:T(8,128)S(1)}, u32[]{:S(2)}) %copy-start.2) | copy-done | bytes 524312
  38.7 4.1 %shard_map.66 = f32[8,16,64,128]{3,2,1,0:T(8,128)} custom-call(f32[8,2,64,128]{3,2,1,0:T(8,128)} %copy-done.1, f32[8,2,64,128]{3,2,1,0:T(8,128)} %copy-done.2, f32[8,32,128]{2,1,0:T(8,128)} %copy-done.3, f32[8,32,128]{2,1,0:T(8,128)} %copy-done.4, f32[8,16,64,128]{3,2,1,0:T(8,128)} %shard_map.65.out_hbm), custom_call_target="tpu_custom_call", output_to_operand_aliasing={{}: (4, {})} | custom-call | tf_op jit(solution)/shard_map/pallas_call | solution.py:186
  (8 shorter events, 0.2 us)
Async XLA Ops:
  5.0 17.0 %copy-start = (f32[2,16,64,128]{3,2,1,0:T(8,128)S(1)}, f32[2,16,64,128]{3,2,1,0:T(8,128)}, u32[]{:S(2)}) copy-start(f32[2,16,64,128]{3,2,1,0:T(8,128)} %cour_ref.1) | copy-start | bytes 3145732
  11.6 25.4 %collective-permute-start = (f32[8,2,64,128]{3,2,1,0:T(8,128)S(1)}, f32[8,2,64,128]{3,2,1,0:T(8,128)S(1)}, u32[]{:S(2)}, u32[]{:S(2)}) collective-permute-start(f32[8,2,64,128]{3,2,1,0:T(8,128)S(1)} %maximum_multiply_fusion), channel_id=1, source_target_pairs={{0,8},{8,16},{16,24},{24,32},{32,40},{40,48},{48,56},{56,64},{64,7... | collective-permute-start | bytes 1572872 | tf_op jit(solution)/shard_map/ppermute | solution.py:221
  11.8 25.3 %collective-permute-start.1 = (f32[8,2,64,128]{3,2,1,0:T(8,128)S(1)}, f32[8,2,64,128]{3,2,1,0:T(8,128)S(1)}, u32[]{:S(2)}, u32[]{:S(2)}) collective-permute-start(f32[8,2,64,128]{3,2,1,0:T(8,128)S(1)} %maximum_multiply_fusion.1), channel_id=1, source_target_pairs={{8,0},{16,8},{24,16},{32,24},{40,32},{48,40},{56,48},{64,56},{72,6... | collective-permute-start | bytes 1572872 | tf_op jit(solution)/shard_map/ppermute | solution.py:222
  22.1 14.9 %collective-permute-start.2 = (f32[8,32,128]{2,1,0:T(8,128)S(1)}, f32[8,32,128]{2,1,0:T(8,128)S(1)}, u32[]{:S(2)}, u32[]{:S(2)}) collective-permute-start(f32[8,32,128]{2,1,0:T(8,128)S(1)} %maximum_multiply_fusion.2), channel_id=1, source_target_pairs={{0,1},{1,2},{2,3},{3,4},{4,5},{5,6},{6,7},{8,9},{9,10},{10,11},{11... | collective-permute-start | bytes 393224 | tf_op jit(solution)/shard_map/ppermute | solution.py:225
  24.7 12.3 %collective-permute-start.3 = (f32[8,32,128]{2,1,0:T(8,128)S(1)}, f32[8,32,128]{2,1,0:T(8,128)S(1)}, u32[]{:S(2)}, u32[]{:S(2)}) collective-permute-start(f32[8,32,128]{2,1,0:T(8,128)S(1)} %maximum_multiply_fusion.3), channel_id=1, source_target_pairs={{1,0},{2,1},{3,2},{4,3},{5,4},{6,5},{7,6},{9,8},{10,9},{11,10},{12... | collective-permute-start | bytes 393224 | tf_op jit(solution)/shard_map/ppermute | solution.py:226
  37.0 0.7 %copy-start.3 = (f32[8,32,128]{2,1,0:T(8,128)}, f32[8,32,128]{2,1,0:T(8,128)S(1)}, u32[]{:S(2)}) copy-start(f32[8,32,128]{2,1,0:T(8,128)S(1)} %collective-permute-done.2.lat_low) | copy-start | bytes 393220
  37.0 0.7 %copy-start.4 = (f32[8,32,128]{2,1,0:T(8,128)}, f32[8,32,128]{2,1,0:T(8,128)S(1)}, u32[]{:S(2)}) copy-start(f32[8,32,128]{2,1,0:T(8,128)S(1)} %collective-permute-done.3.lat_high) | copy-start | bytes 393220
  37.0 0.9 %copy-start.1 = (f32[8,2,64,128]{3,2,1,0:T(8,128)}, f32[8,2,64,128]{3,2,1,0:T(8,128)S(1)}, u32[]{:S(2)}) copy-start(f32[8,2,64,128]{3,2,1,0:T(8,128)S(1)} %collective-permute-done.lon_low) | copy-start | bytes 1572868
  37.9 0.8 %copy-start.2 = (f32[8,2,64,128]{3,2,1,0:T(8,128)}, f32[8,2,64,128]{3,2,1,0:T(8,128)S(1)}, u32[]{:S(2)}) copy-start(f32[8,2,64,128]{3,2,1,0:T(8,128)S(1)} %collective-permute-done.1.lon_high) | copy-start | bytes 1572868

commit v5 on v4

v5 whole, which is shorter than its diff:
```python
import jax
import jax.numpy as jnp
from jax import lax
from jax.experimental import pallas as pl
from jax.experimental.pallas import tpu as pltpu
from jax.sharding import PartitionSpec as P

NEWT = 4


growth = 0.5
latent_liquid = 1.0
latent_ice = 1.3


def increments(warmth, vapour, kinds):
    mixed = jax.nn.sigmoid(2.0 * warmth)
    liquid_share = jnp.where(kinds == 1, 1.0, jnp.where(kinds == 2, 0.0, mixed))
    latent = latent_liquid * liquid_share + latent_ice * (1.0 - liquid_share)
    active = (kinds > 0).astype(warmth.dtype)
    amount = jnp.zeros_like(warmth)
    for newton_step in range(NEWT):
        saturated = jnp.exp(growth * (warmth + latent * amount))
        excess = vapour - amount - saturated
        amount = amount + excess / (1.0 + growth * latent * saturated)
    amount = active * amount
    return (latent * amount, -amount, liquid_share * amount, (1.0 - liquid_share) * amount)


def sat_adjoint(warmth, vapour, kinds, cot_heat, cot_vapour, cot_liquid, cot_ice):

    def forward(first_in, second_in):
        return increments(first_in, second_in, kinds)

    unused, pullback = jax.vjp(forward, warmth, vapour)
    grad_heat, grad_vapour = pullback((cot_heat, cot_vapour, cot_liquid, cot_ice))
    return (cot_heat + grad_heat, cot_vapour + grad_vapour)


def cloudy_columns(cloud_list, cloud_count, nlon, nlat, rows):
    index = cloud_list[0, 0]
    count = cloud_count[0, 0]
    slot = jnp.arange(index.shape[0], dtype=jnp.int32)
    lon = jnp.arange(nlon, dtype=jnp.int32).reshape(nlon // rows, 1, rows)
    lat = jnp.arange(nlat, dtype=jnp.int32).reshape(1, nlat, 1)
    column = (lon * nlat + lat)[None]
    hit = (index[:, None, None, None] == column) & (slot < count)[:, None, None, None]
    return jnp.any(hit, axis=0).astype(jnp.float32)


def sat_kernel(traj_ref, cot_ref, kind_ref, mask_ref, cour_ref,
               out_ref, lon_bottom, lon_top, lat_bottom, lat_top):
    fields, rows, nlat, lev = cot_ref.shape
    step = pl.program_id(0)
    last = pl.num_programs(0) - 1
    chunk = 32
    parts = nlat // chunk
    for r in range(rows):
        after = [[None] * parts for _ in range(fields)]
        for j in range(parts):
            lat = pl.ds(j * chunk, chunk)
            cot = [cot_ref[k, r, lat, :] for k in range(4)]
            new_heat, new_vapour = sat_adjoint(
                traj_ref[0, r, lat, :], traj_ref[1, r, lat, :], kind_ref[r, lat, :], *cot
            )
            cloudy = jnp.broadcast_to(mask_ref[0, lat, r:r + 1], (chunk, lev)) > 0.0
            heat = jnp.where(cloudy, new_heat, cot[0])
            vapour = jnp.where(cloudy, new_vapour, cot[1])
            out_ref[0, r, lat, :] = heat
            out_ref[1, r, lat, :] = vapour
            after[0][j] = heat
            after[1][j] = vapour
            for f in range(2, fields):
                after[f][j] = cot_ref[f, r, lat, :]
        low_weight = cour_ref[1, r, 0:2, :]
        high_weight = cour_ref[1, r, nlat - 2:nlat, :]
        for f in range(fields):
            lat_bottom[f, 2 * r:2 * r + 2, :] = low_weight * after[f][0][0:2]
            lat_top[f, 2 * r:2 * r + 2, :] = high_weight * after[f][parts - 1][chunk - 2:chunk]
        if r < 2:
            @pl.when(step == 0)
            def _():
                for f in range(fields):
                    for j in range(parts):
                        lat = pl.ds(j * chunk, chunk)
                        lon_bottom[f, r, lat, :] = cour_ref[0, r, lat, :] * after[f][j]
        if r >= rows - 2:
            @pl.when(step == last)
            def _():
                for f in range(fields):
                    for j in range(parts):
                        lat = pl.ds(j * chunk, chunk)
                        lon_top[f, r - rows + 2, lat, :] = cour_ref[0, r, lat, :] * after[f][j]


def first_pair(trajectory, cotangent, branch, mask, courant, rows):
    fields, nlon, nlat, lev = cotangent.shape
    lon_send = jax.ShapeDtypeStruct((fields, 2, nlat, lev), jnp.float32)
    lat_send = jax.ShapeDtypeStruct((fields, 2 * nlon, lev), jnp.float32)
    return pl.pallas_call(
        sat_kernel,
        grid=(nlon // rows,),
        in_specs=[
            pl.BlockSpec((2, rows, nlat, lev), lambda i: (0, i, 0, 0)),
            pl.BlockSpec((fields, rows, nlat, lev), lambda i: (0, i, 0, 0)),
            pl.BlockSpec((rows, nlat, lev), lambda i: (i, 0, 0)),
            pl.BlockSpec((1, nlat, rows), lambda i: (i, 0, 0)),
            pl.BlockSpec((2, rows, nlat, lev), lambda i: (0, i, 0, 0)),
        ],
        out_specs=[
            pl.BlockSpec((2, rows, nlat, lev), lambda i: (0, i, 0, 0)),
            pl.BlockSpec((fields, 2, nlat, lev), lambda i: (0, 0, 0, 0)),
            pl.BlockSpec((fields, 2, nlat, lev), lambda i: (0, 0, 0, 0)),
            pl.BlockSpec((fields, 2 * rows, lev), lambda i: (0, i, 0)),
            pl.BlockSpec((fields, 2 * rows, lev), lambda i: (0, i, 0)),
        ],
        out_shape=[jax.ShapeDtypeStruct((2, nlon, nlat, lev), jnp.float32), lon_send, lon_send, lat_send, lat_send],
    )(trajectory, cotangent, branch, mask, courant)


def stencil_kernel(first_ref, cot_ref, cour_ref, out_ref, lon_pad, lat_pad):
    nlon, nlat = out_ref.shape[1], out_ref.shape[2]
    f = pl.program_id(0)
    zeros = jnp.zeros((2,) + lon_pad.shape[1:], jnp.float32)

    def compute(src):
        for r in range(nlon):
            lon_pad[r + 2] = cour_ref[0, r] * src[0, r]
        lon_pad[0:2] = zeros
        lon_pad[nlon + 2:nlon + 4] = zeros
        lat_pad[6:8] = zeros[0, 0:2]
        lat_pad[8 + nlat:10 + nlat] = zeros[0, 0:2]
        for r in range(nlon):
            lat_pad[8:8 + nlat] = cour_ref[1, r] * src[0, r]
            d_lat = (8.0 * (lat_pad[9:9 + nlat] - lat_pad[7:7 + nlat]) - (lat_pad[10:10 + nlat] - lat_pad[6:6 + nlat])) / 12.0
            d_lon = (8.0 * (lon_pad[r + 3] - lon_pad[r + 1]) - (lon_pad[r + 4] - lon_pad[r])) / 12.0
            out_ref[0, r] = src[0, r] + d_lon + d_lat

    @pl.when(f < 2)
    def _():
        compute(first_ref)

    @pl.when(f >= 2)
    def _():
        compute(cot_ref)


def advect(first, cotangent, courant):
    fields, nlon, nlat, lev = cotangent.shape
    size = cotangent.size * 4
    return pl.pallas_call(
        stencil_kernel,
        grid=(fields,),
        in_specs=[
            pl.BlockSpec((1, nlon, nlat, lev), lambda f: (jnp.minimum(f, 1), 0, 0, 0)),
            pl.BlockSpec((1, nlon, nlat, lev), lambda f: (f, 0, 0, 0)),
            pl.BlockSpec((2, nlon, nlat, lev), lambda f: (0, 0, 0, 0)),
        ],
        out_specs=pl.BlockSpec((1, nlon, nlat, lev), lambda f: (f, 0, 0, 0)),
        out_shape=jax.ShapeDtypeStruct(cotangent.shape, jnp.float32),
        scratch_shapes=[
            pltpu.VMEM((nlon + 4, nlat, lev), jnp.float32),
            pltpu.VMEM((nlat + 16, lev), jnp.float32),
        ],
        cost_estimate=pl.CostEstimate(flops=12 * cotangent.size, transcendentals=0, bytes_accessed=3 * size),
    )(first, cotangent, courant)


def halo_kernel(lon_low_hbm, lon_high_hbm, lat_low_hbm, lat_high_hbm, out_hbm, out_ref,
                lon_low, lon_high, lat_low, lat_high, lon_lo_buf, lon_hi_buf, lat_lo_buf, lat_hi_buf, sems):
    fields, nlon, nlat, lev = out_hbm.shape
    halos = [(lon_low_hbm, lon_low), (lon_high_hbm, lon_high), (lat_low_hbm, lat_low), (lat_high_hbm, lat_high)]
    regions = [
        (out_hbm.at[:, 0:2], lon_lo_buf),
        (out_hbm.at[:, nlon - 2:nlon], lon_hi_buf),
        (out_hbm.at[:, 2:nlon - 2, 0:8], lat_lo_buf),
        (out_hbm.at[:, 2:nlon - 2, nlat - 8:nlat], lat_hi_buf),
    ]
    copies = [pltpu.make_async_copy(s, d, sems.at[i]) for i, (s, d) in enumerate(halos + regions)]
    for c in copies:
        c.start()
    for c in copies:
        c.wait()
    sub = lax.broadcasted_iota(jnp.int32, (8, lev), 0)

    def lat_fix(tile, low_rows, high_rows, at_low):
        if at_low:
            row0 = (low_rows[0:1] - 8.0 * low_rows[1:2]) / 12.0
            row1 = low_rows[1:2] / 12.0
            return tile + jnp.where(sub == 0, row0, jnp.where(sub == 1, row1, 0.0))
        row6 = -high_rows[0:1] / 12.0
        row7 = (8.0 * high_rows[0:1] - high_rows[1:2]) / 12.0
        return tile + jnp.where(sub == 6, row6, jnp.where(sub == 7, row7, 0.0))

    for f in range(fields):
        lo = lon_low[f]
        hi = lon_high[f]
        edge_terms = [(lo[0] - 8.0 * lo[1]) / 12.0, lo[1] / 12.0, -hi[0] / 12.0, (8.0 * hi[0] - hi[1]) / 12.0]
        for k, r in enumerate((0, 1, nlon - 2, nlon - 1)):
            buf = lon_lo_buf if k < 2 else lon_hi_buf
            block = buf[f, k % 2] + edge_terms[k]
            low_rows = lat_low[f, 2 * r:2 * r + 2]
            high_rows = lat_high[f, 2 * r:2 * r + 2]
            buf[f, k % 2] = block
            buf[f, k % 2, 0:8] = lat_fix(block[0:8], low_rows, high_rows, True)
            buf[f, k % 2, nlat - 8:nlat] = lat_fix(block[nlat - 8:nlat], low_rows, high_rows, False)
        for r in range(2, nlon - 2):
            low_rows = lat_low[f, 2 * r:2 * r + 2]
            high_rows = lat_high[f, 2 * r:2 * r + 2]
            lat_lo_buf[f, r - 2] = lat_fix(lat_lo_buf[f, r - 2], low_rows, high_rows, True)
            lat_hi_buf[f, r - 2] = lat_fix(lat_hi_buf[f, r - 2], low_rows, high_rows, False)
    copies = [pltpu.make_async_copy(d, s, sems.at[4 + i]) for i, (s, d) in enumerate(regions)]
    for c in copies:
        c.start()
    for c in copies:
        c.wait()


def add_halos(out, lon_low, lon_high, lat_low, lat_high):
    fields, nlon, nlat, lev = out.shape
    hbm = pl.BlockSpec(memory_space=pl.ANY)
    return pl.pallas_call(
        halo_kernel,
        in_specs=[hbm] * 5,
        out_specs=hbm,
        out_shape=jax.ShapeDtypeStruct(out.shape, jnp.float32),
        scratch_shapes=[
            pltpu.VMEM(lon_low.shape, jnp.float32),
            pltpu.VMEM(lon_high.shape, jnp.float32),
            pltpu.VMEM(lat_low.shape, jnp.float32),
            pltpu.VMEM(lat_high.shape, jnp.float32),
            pltpu.VMEM((fields, 2, nlat, lev), jnp.float32),
            pltpu.VMEM((fields, 2, nlat, lev), jnp.float32),
            pltpu.VMEM((fields, nlon - 4, 8, lev), jnp.float32),
            pltpu.VMEM((fields, nlon - 4, 8, lev), jnp.float32),
            pltpu.SemaphoreType.DMA((8,)),
        ],
        input_output_aliases={4: 0},
    )(lon_low, lon_high, lat_low, lat_high, out)


def neighbours(axis, periodic):
    count = lax.axis_size(axis)
    forward = [(i, i + 1) for i in range(count - 1)]
    if periodic:
        forward.append((count - 1, 0))
    backward = [(target, source) for source, target in forward]
    return forward, backward


def on_device(trajectory, cotangent, courant, branch, cloud_list, cloud_count):
    fields, nlon, nlat, lev = cotangent.shape
    rows = 8
    mask = cloudy_columns(cloud_list, cloud_count, nlon, nlat, rows)
    first, lon_bottom, lon_top, lat_bottom, lat_top = first_pair(trajectory, cotangent, branch, mask, courant, rows)
    forward, backward = neighbours("lon", True)
    lon_low = lax.ppermute(lon_top, "lon", forward)
    lon_high = lax.ppermute(lon_bottom, "lon", backward)
    forward, backward = neighbours("lat", False)
    lat_low = lax.ppermute(lat_top, "lat", forward)
    lat_high = lax.ppermute(lat_bottom, "lat", backward)
    out = advect(first, cotangent, courant)
    return add_halos(out, lon_low, lon_high, lat_low, lat_high)


def solution(mesh):
    placed = (
        P(None, "lon", "lat", None),
        P(None, "lon", "lat", None),
        P(None, "lon", "lat", None),
        P("lon", "lat", None),
        P("lon", "lat", None),
        P("lon", "lat"),
    )
    return jax.shard_map(
        on_device,
        mesh=mesh,
        in_specs=placed,
        out_specs=P(None, "lon", "lat", None),
        check_vma=False,
    )
```

time: 43.3 us -> 39.4 us (0.910)
  local copies, waits for them, and re-layouts: 7.98 us -> 1.63 us
  other arithmetic: 1.31 us -> 3.81 us
    slice x5 -> x0, local copies, waits for them, and re-layouts: 4.36 us -> none  [the longest x2 2.37 us: on_device(): lax.slice_in_dim(cotangent[2:], start, start + 2, axis=dim)]
    reduce_or x1, other arithmetic: 0.49 us -> 2.44 us  [cloudy_columns(): return jnp.any(hit, axis=0).astype(jnp.float32)]
    pallas_call x1, Pallas kernels: 5.59 us -> 6.65 us  [first_pair(): pl.pallas_call(sat_kernel, grid=(nlon // rows,), in_specs=[pl.BlockSpec((...]
    broadcast_in_dim x1 -> x0, local copies, waits for them, and re-layouts: 0.99 us -> none  [on_device(): jnp.broadcast_to(cloudy.reshape(nlon, nlat, 1), (nlon, nlat, lev))]
    mul x1 -> x0, local copies, waits for them, and re-layouts: 0.88 us -> none  [on_device(): lon_high = lax.ppermute(weight(1, 0) * after(1, 0), 'lon', backward)]
    pallas_call x1, Pallas kernels: 4.1 us -> 3.27 us  [add_halos(): pl.pallas_call(halo_kernel, in_specs=[hbm] * 5, out_specs=hbm, out_shape=...]
    convert_element_type x1, other arithmetic: 0.01 us -> 0.64 us  [cloudy_columns(): return jnp.any(hit, axis=0).astype(jnp.float32)]
    unnamed x10 -> x8, local copies, waits for them, and re-layouts: 1.63 us -> 1.63 us
  transfers between devices with their start and end apart: 4 -> 4, of which waited for: 0 -> 0; matrix products, arithmetic and copies ran while one was open for 5% -> 0% of each run, Pallas kernels for 19% -> 21%
where the time goes in v5:
time: 39.4 us; the launch traced here: 39 us
  Pallas kernels  18.1 us (46%)
  starting transfers between devices  14.8 us (38%)
  other arithmetic  3.81 us (10%)
  local copies, waits for them, and re-layouts  1.63 us (4%)
  between operations  0.74 us (2%)
    pallas_call x1, Pallas kernels, advect(): pl.pallas_call(stencil_kernel, grid=(fields,), in_specs=[pl.BlockSpec((1,...  8.16 us
    ppermute x1, starting transfers between devices, on_device(): lon_high = lax.ppermute(lon_bottom, 'lon', backward)  8 us
    pallas_call x1, Pallas kernels, first_pair(): pl.pallas_call(sat_kernel, grid=(nlon // rows,), in_specs=[pl.BlockSpec((...  6.65 us
    ppermute x1, starting transfers between devices, on_device(): lat_high = lax.ppermute(lat_bottom, 'lat', backward)  4.16 us
    pallas_call x1, Pallas kernels, add_halos(): pl.pallas_call(halo_kernel, in_specs=[hbm] * 5, out_specs=hbm, out_shape=...  3.27 us
    ppermute x1, starting transfers between devices, on_device(): lat_low = lax.ppermute(lat_top, 'lat', forward)  2.57 us
    reduce_or x1, other arithmetic, cloudy_columns(): return jnp.any(hit, axis=0).astype(jnp.float32)  2.44 us
    unnamed x8, local copies, waits for them, and re-layouts  1.63 us
  transfers between devices with their start and end apart: 4, of which 0 were waited for; matrix products, arithmetic and copies ran while one was open for 0% of the time, Pallas kernels for 21%

profile of v5, /device:TPU:2, one launch (start us, length us, event | category | flops | bytes accessed | tf_op | source)
XLA Modules:
  0.0 39.0 jit_solution(7282692355441111547)
XLA Ops:
  0.7 0.7 %reduce = s32[768]{0:T(1024)S(1)} reduce(s32[1,1,768]{2,1,0:T(1,128)} %param.10, s32[]{:T(128)} %constant.14), dimensions={0,1}, to_apply=%param.10.reduce_sub_computation | reduce | bytes 6148 | tf_op args[4]
  1.4 2.4 %and_reduce_fusion = pred[2,64,8]{2,1,0:T(8,128)(4,1)S(1)} fusion(s32[2,64,8]{2,1,0:T(8,128)S(1)} %iota_add_fusion, s32[768]{0:T(1024)S(1)} %reduce, pred[768]{0:T(1024)(128)(4,1)S(1)} %iota_compare_fusion), kind=kLoop, calls=%fused_computation | loop fusion | flops 2358272 | bytes 8960 | tf_op jit(solution)/shard_map/reduce_or | solution.py:48
  3.8 0.6 %convert_element_type.3.mask_ref = f32[2,64,8]{2,1,0:T(8,128)} convert(pred[2,64,8]{2,1,0:T(8,128)(4,1)S(1)} %and_reduce_fusion) | non-fusion elementwise | flops 1024 | bytes 5120 | tf_op jit(solution)/shard_map/convert_element_type | solution.py:48
  4.5 6.7 %shard_map.64 = (f32[2,16,64,128]{3,2,1,0:T(8,128)}, f32[8,2,64,128]{3,2,1,0:T(8,128)}, f32[8,2,64,128]{3,2,1,0:T(8,128)}, f32[8,32,128]{2,1,0:T(8,128)}, f32[8,32,128]{2,1,0:T(8,128)}) custom-call(f32[2,16,64,128]{3,2,1,0:T(8,128)} %traj_ref.1, f32[8,16,64,128]{3,2,1,0:T(8,128)} %cot_ref.3, s32[16,64,128]{2,1,0:T(8,128)} %kind_ref.1, ...), custom_call_target="tpu_custom_call" | custom-call | tf_op jit(solution)/shard_map/pallas_call | solution.py:100
  11.1 0.0 collective-permute-start
  11.2 8.0 %collective-permute-start.1 = (f32[8,2,64,128]{3,2,1,0:T(8,128)}, f32[8,2,64,128]{3,2,1,0:T(8,128)S(1)}, u32[]{:S(2)}, u32[]{:S(2)}) collective-permute-start(f32[8,2,64,128]{3,2,1,0:T(8,128)} %get-tuple-element.11), channel_id=1, source_target_pairs={{8,0},{16,8},{24,16},{32,24},{40,32},{48,40},{56,48},{64,56},{72,6... | collective-permute-start | bytes 1572872 | tf_op jit(solution)/shard_map/ppermute | solution.py:258
  19.2 2.6 %collective-permute-start.2 = (f32[8,32,128]{2,1,0:T(8,128)}, f32[8,32,128]{2,1,0:T(8,128)S(1)}, u32[]{:S(2)}, u32[]{:S(2)}) collective-permute-start(f32[8,32,128]{2,1,0:T(8,128)} %get-tuple-element.12), channel_id=1, source_target_pairs={{0,1},{1,2},{2,3},{3,4},{4,5},{5,6},{6,7},{8,9},{9,10},{10,11},{11... | collective-permute-start | bytes 393224 | tf_op jit(solution)/shard_map/ppermute | solution.py:260
  21.8 4.2 %collective-permute-start.3 = (f32[8,32,128]{2,1,0:T(8,128)}, f32[8,32,128]{2,1,0:T(8,128)S(1)}, u32[]{:S(2)}, u32[]{:S(2)}) collective-permute-start(f32[8,32,128]{2,1,0:T(8,128)} %get-tuple-element.13), channel_id=1, source_target_pairs={{1,0},{2,1},{3,2},{4,3},{5,4},{6,5},{7,6},{9,8},{10,9},{11,10},{12... | collective-permute-start | bytes 393224 | tf_op jit(solution)/shard_map/ppermute | solution.py:261
  25.9 8.2 %shard_map.65.out_hbm = f32[8,16,64,128]{3,2,1,0:T(8,128)} custom-call(f32[2,16,64,128]{3,2,1,0:T(8,128)} %get-tuple-element.14.first_ref, f32[8,16,64,128]{3,2,1,0:T(8,128)} %cot_ref.3, f32[2,16,64,128]{3,2,1,0:T(8,128)} %cour_ref.3), custom_call_target="tpu_custom_call" | custom-call | flops 12582912 | bytes 12582912 | tf_op jit(solution)/shard_map/pallas_call | solution.py:151
  34.1 0.0 collective-permute-done.2.lat_low_hbm
  34.1 0.0 copy-start.2
  34.1 0.0 collective-permute-done.3.lat_high_hbm
  34.1 0.0 copy-start.3
  34.1 0.0 collective-permute-done.lon_low_hbm
  34.1 0.0 copy-start
  34.1 0.0 collective-permute-done.1.lon_high_hbm
  34.1 0.6 %copy-done.2 = f32[8,32,128]{2,1,0:T(8,128)} copy-done((f32[8,32,128]{2,1,0:T(8,128)}, f32[8,32,128]{2,1,0:T(8,128)S(1)}, u32[]{:S(2)}) %copy-start.2) | copy-done | bytes 131096
  34.7 0.1 copy-done.3
  34.8 0.2 copy-done
  35.0 0.0 copy-start.1
  35.0 0.8 %copy-done.1 = f32[8,2,64,128]{3,2,1,0:T(8,128)} copy-done((f32[8,2,64,128]{3,2,1,0:T(8,128)}, f32[8,2,64,128]{3,2,1,0:T(8,128)S(1)}, u32[]{:S(2)}) %copy-start.1) | copy-done | bytes 524312
  35.8 3.3 %shard_map.66 = f32[8,16,64,128]{3,2,1,0:T(8,128)} custom-call(f32[8,2,64,128]{3,2,1,0:T(8,128)} %copy-done, f32[8,2,64,128]{3,2,1,0:T(8,128)} %copy-done.1, f32[8,32,128]{2,1,0:T(8,128)} %copy-done.2, f32[8,32,128]{2,1,0:T(8,128)} %copy-done.3, f32[8,16,64,128]{3,2,1,0:T(8,128)} %shard_map.65.out_hbm), custom_call_target="tpu_custom_call", output_to_operand_aliasing={{}: (4, {})} | custom-call | tf_op jit(solution)/shard_map/pallas_call | solution.py:222
  (3 shorter events, 0.0 us)
Async XLA Ops:
  11.1 23.0 %collective-permute-start = (f32[8,2,64,128]{3,2,1,0:T(8,128)}, f32[8,2,64,128]{3,2,1,0:T(8,128)S(1)}, u32[]{:S(2)}, u32[]{:S(2)}) collective-permute-start(f32[8,2,64,128]{3,2,1,0:T(8,128)} %get-tuple-element.10), channel_id=1, source_target_pairs={{0,8},{8,16},{16,24},{24,32},{32,40},{40,48},{48,56},{56,64},{64,7... | collective-permute-start | bytes 1572872 | tf_op jit(solution)/shard_map/ppermute | solution.py:257
  11.2 23.0 %collective-permute-start.1 = (f32[8,2,64,128]{3,2,1,0:T(8,128)}, f32[8,2,64,128]{3,2,1,0:T(8,128)S(1)}, u32[]{:S(2)}, u32[]{:S(2)}) collective-permute-start(f32[8,2,64,128]{3,2,1,0:T(8,128)} %get-tuple-element.11), channel_id=1, source_target_pairs={{8,0},{16,8},{24,16},{32,24},{40,32},{48,40},{56,48},{64,56},{72,6... | collective-permute-start | bytes 1572872 | tf_op jit(solution)/shard_map/ppermute | solution.py:258
  19.2 14.9 %collective-permute-start.2 = (f32[8,32,128]{2,1,0:T(8,128)}, f32[8,32,128]{2,1,0:T(8,128)S(1)}, u32[]{:S(2)}, u32[]{:S(2)}) collective-permute-start(f32[8,32,128]{2,1,0:T(8,128)} %get-tuple-element.12), channel_id=1, source_target_pairs={{0,1},{1,2},{2,3},{3,4},{4,5},{5,6},{6,7},{8,9},{9,10},{10,11},{11... | collective-permute-start | bytes 393224 | tf_op jit(solution)/shard_map/ppermute | solution.py:260
  21.8 12.3 %collective-permute-start.3 = (f32[8,32,128]{2,1,0:T(8,128)}, f32[8,32,128]{2,1,0:T(8,128)S(1)}, u32[]{:S(2)}, u32[]{:S(2)}) collective-permute-start(f32[8,32,128]{2,1,0:T(8,128)} %get-tuple-element.13), channel_id=1, source_target_pairs={{1,0},{2,1},{3,2},{4,3},{5,4},{6,5},{7,6},{9,8},{10,9},{11,10},{12... | collective-permute-start | bytes 393224 | tf_op jit(solution)/shard_map/ppermute | solution.py:261
  34.1 0.6 %copy-start.2 = (f32[8,32,128]{2,1,0:T(8,128)}, f32[8,32,128]{2,1,0:T(8,128)S(1)}, u32[]{:S(2)}) copy-start(f32[8,32,128]{2,1,0:T(8,128)S(1)} %collective-permute-done.2.lat_low_hbm) | copy-start | bytes 393220
  34.1 0.7 %copy-start.3 = (f32[8,32,128]{2,1,0:T(8,128)}, f32[8,32,128]{2,1,0:T(8,128)S(1)}, u32[]{:S(2)}) copy-start(f32[8,32,128]{2,1,0:T(8,128)S(1)} %collective-permute-done.3.lat_high_hbm) | copy-start | bytes 393220
  34.1 0.9 %copy-start = (f32[8,2,64,128]{3,2,1,0:T(8,128)}, f32[8,2,64,128]{3,2,1,0:T(8,128)S(1)}, u32[]{:S(2)}) copy-start(f32[8,2,64,128]{3,2,1,0:T(8,128)S(1)} %collective-permute-done.lon_low_hbm) | copy-start | bytes 1572868
  35.0 0.8 %copy-start.1 = (f32[8,2,64,128]{3,2,1,0:T(8,128)}, f32[8,2,64,128]{3,2,1,0:T(8,128)S(1)}, u32[]{:S(2)}) copy-start(f32[8,2,64,128]{3,2,1,0:T(8,128)S(1)} %collective-permute-done.1.lon_high_hbm) | copy-start | bytes 1572868

commit v6 on v5

--- a/solution.py
+++ b/solution.py
@@ -41,11 +41,9 @@
     index = cloud_list[0, 0]
     count = cloud_count[0, 0]
     slot = jnp.arange(index.shape[0], dtype=jnp.int32)
-    lon = jnp.arange(nlon, dtype=jnp.int32).reshape(nlon // rows, 1, rows)
-    lat = jnp.arange(nlat, dtype=jnp.int32).reshape(1, nlat, 1)
-    column = (lon * nlat + lat)[None]
-    hit = (index[:, None, None, None] == column) & (slot < count)[:, None, None, None]
-    return jnp.any(hit, axis=0).astype(jnp.float32)
+    hit = (index[:, None] == jnp.arange(nlon * nlat, dtype=jnp.int32)[None, :]) & (slot < count)[:, None]
+    cloudy = jnp.any(hit, axis=0).astype(jnp.float32)
+    return jnp.transpose(cloudy.reshape(nlon // rows, rows, nlat), (0, 2, 1))
 
 
 def sat_kernel(traj_ref, cot_ref, kind_ref, mask_ref, cour_ref,
@@ -118,49 +116,58 @@
     )(trajectory, cotangent, branch, mask, courant)
 
 
-def stencil_kernel(first_ref, cot_ref, cour_ref, out_ref, lon_pad, lat_pad):
-    nlon, nlat = out_ref.shape[1], out_ref.shape[2]
-    f = pl.program_id(0)
-    zeros = jnp.zeros((2,) + lon_pad.shape[1:], jnp.float32)
-
-    def compute(src):
+def stencil_kernel(first_hbm, cot_hbm, cour_hbm, out_hbm, field_v, cour_v, out_v, lon_pad, lat_pad, in_sems, out_sems):
+    fields, nlon, nlat, lev = cot_hbm.shape
+    zeros = jnp.zeros((2, nlat, lev), jnp.float32)
+    cour_copy = pltpu.make_async_copy(cour_hbm, cour_v, in_sems.at[0])
+    cour_copy.start()
+    loads = [pltpu.make_async_copy(first_hbm, field_v.at[0:2], in_sems.at[1])]
+    loads += [pltpu.make_async_copy(cot_hbm.at[f], field_v.at[f], in_sems.at[f]) for f in range(2, fields)]
+    for c in loads:
+        c.start()
+    lon_pad[0:2] = zeros
+    lon_pad[nlon + 2:nlon + 4] = zeros
+    lat_pad[6:8] = zeros[0, 0:2]
+    lat_pad[8 + nlat:10 + nlat] = zeros[0, 0:2]
+    cour_copy.wait()
+    stores = []
+    for f in range(fields):
+        if f == 0:
+            loads[0].wait()
+        elif f >= 2:
+            loads[f - 1].wait()
+        src = field_v.at[f]
         for r in range(nlon):
-            lon_pad[r + 2] = cour_ref[0, r] * src[0, r]
-        lon_pad[0:2] = zeros
-        lon_pad[nlon + 2:nlon + 4] = zeros
-        lat_pad[6:8] = zeros[0, 0:2]
-        lat_pad[8 + nlat:10 + nlat] = zeros[0, 0:2]
+            lon_pad[r + 2] = cour_v[0, r] * src[r]
         for r in range(nlon):
-            lat_pad[8:8 + nlat] = cour_ref[1, r] * src[0, r]
+            lat_pad[8:8 + nlat] = cour_v[1, r] * src[r]
             d_lat = (8.0 * (lat_pad[9:9 + nlat] - lat_pad[7:7 + nlat]) - (lat_pad[10:10 + nlat] - lat_pad[6:6 + nlat])) / 12.0
             d_lon = (8.0 * (lon_pad[r + 3] - lon_pad[r + 1]) - (lon_pad[r + 4] - lon_pad[r])) / 12.0
-            out_ref[0, r] = src[0, r] + d_lon + d_lat
-
-    @pl.when(f < 2)
-    def _():
-        compute(first_ref)
-
-    @pl.when(f >= 2)
-    def _():
-        compute(cot_ref)
+            out_v[f, r] = src[r] + d_lon + d_lat
+        store = pltpu.make_async_copy(out_v.at[f], out_hbm.at[f], out_sems.at[f])
+        store.start()
+        stores.append(store)
+    for store in stores:
+        store.wait()
 
 
 def advect(first, cotangent, courant):
     fields, nlon, nlat, lev = cotangent.shape
     size = cotangent.size * 4
+    hbm = pl.BlockSpec(memory_space=pl.ANY)
     return pl.pallas_call(
         stencil_kernel,
-        grid=(fields,),
-        in_specs=[
-            pl.BlockSpec((1, nlon, nlat, lev), lambda f: (jnp.minimum(f, 1), 0, 0, 0)),
-            pl.BlockSpec((1, nlon, nlat, lev), lambda f: (f, 0, 0, 0)),
-            pl.BlockSpec((2, nlon, nlat, lev), lambda f: (0, 0, 0, 0)),
-        ],
-        out_specs=pl.BlockSpec((1, nlon, nlat, lev), lambda f: (f, 0, 0, 0)),
+        in_specs=[hbm, hbm, hbm],
+        out_specs=hbm,
         out_shape=jax.ShapeDtypeStruct(cotangent.shape, jnp.float32),
         scratch_shapes=[
+            pltpu.VMEM(cotangent.shape, jnp.float32),
+            pltpu.VMEM(courant.shape, jnp.float32),
+            pltpu.VMEM(cotangent.shape, jnp.float32),
             pltpu.VMEM((nlon + 4, nlat, lev), jnp.float32),
             pltpu.VMEM((nlat + 16, lev), jnp.float32),
+            pltpu.SemaphoreType.DMA((fields,)),
+            pltpu.SemaphoreType.DMA((fields,)),
         ],
         cost_estimate=pl.CostEstimate(flops=12 * cotangent.size, transcendentals=0, bytes_accessed=3 * size),
     )(first, cotangent, courant)

time: 39.4 us -> 34.4 us (0.87)
  Pallas kernels: 18.1 us -> 15.1 us
  other arithmetic: 3.81 us -> 1.2 us
  local copies, waits for them, and re-layouts: 1.63 us -> 2.43 us
    pallas_call x1, Pallas kernels: 8.16 us -> 5.18 us  [advect(): pl.pallas_call(stencil_kernel, in_specs=[hbm, hbm, hbm], out_specs=hbm, o...]
    reduce_or x1, other arithmetic: 2.44 us -> 0.49 us  [cloudy_columns(): cloudy = jnp.any(hit, axis=0).astype(jnp.float32)]
    transpose x0 -> x2, local copies, waits for them, and re-layouts: none -> 0.8 us  [cloudy_columns(): return jnp.transpose(cloudy.reshape(nlon // rows, rows, nlat), (0, 2, 1))]
    convert_element_type x1 -> x0, other arithmetic: 0.64 us -> none  [cloudy_columns(): return jnp.any(hit, axis=0).astype(jnp.float32)]
  transfers between devices with their start and end apart: 4 -> 4, of which waited for: 0 -> 0; matrix products, arithmetic and copies ran while one was open for 0% -> 0% of each run, Pallas kernels for 21% -> 15%
where the time goes in v6:
time: 34.4 us; the launch traced here: 34.3 us
  Pallas kernels  15.1 us (44%)
  starting transfers between devices  14.8 us (43%)
  local copies, waits for them, and re-layouts  2.43 us (7%)
  other arithmetic  1.2 us (3%)
  between operations  0.76 us (2%)
    ppermute x1, starting transfers between devices, on_device(): lon_high = lax.ppermute(lon_bottom, 'lon', backward)  8 us
    pallas_call x1, Pallas kernels, first_pair(): pl.pallas_call(sat_kernel, grid=(nlon // rows,), in_specs=[pl.BlockSpec((...  6.65 us
    pallas_call x1, Pallas kernels, advect(): pl.pallas_call(stencil_kernel, in_specs=[hbm, hbm, hbm], out_specs=hbm, o...  5.18 us
    ppermute x1, starting transfers between devices, on_device(): lat_high = lax.ppermute(lat_bottom, 'lat', backward)  4.16 us
    pallas_call x1, Pallas kernels, add_halos(): pl.pallas_call(halo_kernel, in_specs=[hbm] * 5, out_specs=hbm, out_shape=...  3.27 us
    ppermute x1, starting transfers between devices, on_device(): lat_low = lax.ppermute(lat_top, 'lat', forward)  2.57 us
    unnamed x8, local copies, waits for them, and re-layouts  1.63 us
    transpose x2, local copies, waits for them, and re-layouts, cloudy_columns(): return jnp.transpose(cloudy.reshape(nlon // rows, rows, nlat), (0, 2, 1))  0.8 us
  transfers between devices with their start and end apart: 4, of which 0 were waited for; matrix products, arithmetic and copies ran while one was open for 0% of the time, Pallas kernels for 15%

profile of v6, /device:TPU:2, one launch (start us, length us, event | category | flops | bytes accessed | tf_op | source)
XLA Modules:
  0.0 34.3 jit_solution(16657467529813693103)
XLA Ops:
  0.7 0.7 %reduce = s32[768]{0:T(1024)S(1)} reduce(s32[1,1,768]{2,1,0:T(1,128)} %param.10, s32[]{:T(128)} %constant.8), dimensions={0,1}, to_apply=%param.10.reduce_sub_computation | reduce | bytes 6148 | tf_op args[4]
  1.4 0.5 %fusion.1 = pred[1024]{0:T(1024)(128)(4,1)S(1)} fusion(s32[768]{0:T(1024)S(1)} %reduce, pred[768]{0:T(1024)(128)(4,1)S(1)} %iota_compare_fusion.1), kind=kLoop, calls=%fused_computation.2 | loop fusion | flops 2358272 | bytes 4864 | tf_op jit(solution)/shard_map/reduce_or | solution.py:45
  1.9 0.1 reshape.9
  1.9 0.7 %copy.9 = f32[2,8,64]{1,2,0:T(8,128)} copy(f32[2,8,64]{2,1,0:T(8,128)S(1)} %reshape.9) | data formatting | bytes 8192 | tf_op jit(solution)/shard_map/transpose | solution.py:46
  2.7 6.7 %shard_map.64 = (f32[2,16,64,128]{3,2,1,0:T(8,128)}, f32[8,2,64,128]{3,2,1,0:T(8,128)}, f32[8,2,64,128]{3,2,1,0:T(8,128)}, f32[8,32,128]{2,1,0:T(8,128)}, f32[8,32,128]{2,1,0:T(8,128)}) custom-call(f32[2,16,64,128]{3,2,1,0:T(8,128)} %traj_ref.1, f32[8,16,64,128]{3,2,1,0:T(8,128)} %cot_hbm.1, s32[16,64,128]{2,1,0:T(8,128)} %kind_ref.1, f32[2,64,8]{2,1,0:T(8,128)} %bitcast.3, ...), custom_call_target="tpu_custom_call" | custom-call | tf_op jit(solution)/shard_map/pallas_call | solution.py:98
  9.3 0.0 collective-permute-start
  9.4 8.0 %collective-permute-start.1 = (f32[8,2,64,128]{3,2,1,0:T(8,128)}, f32[8,2,64,128]{3,2,1,0:T(8,128)S(1)}, u32[]{:S(2)}, u32[]{:S(2)}) collective-permute-start(f32[8,2,64,128]{3,2,1,0:T(8,128)} %get-tuple-element.11), channel_id=1, source_target_pairs={{8,0},{16,8},{24,16},{32,24},{40,32},{48,40},{56,48},{64,56},{72,6... | collective-permute-start | bytes 1572872 | tf_op jit(solution)/shard_map/ppermute | solution.py:265
  17.4 2.6 %collective-permute-start.2 = (f32[8,32,128]{2,1,0:T(8,128)}, f32[8,32,128]{2,1,0:T(8,128)S(1)}, u32[]{:S(2)}, u32[]{:S(2)}) collective-permute-start(f32[8,32,128]{2,1,0:T(8,128)} %get-tuple-element.12), channel_id=1, source_target_pairs={{0,1},{1,2},{2,3},{3,4},{4,5},{5,6},{6,7},{8,9},{9,10},{10,11},{11... | collective-permute-start | bytes 393224 | tf_op jit(solution)/shard_map/ppermute | solution.py:267
  20.0 4.2 %collective-permute-start.3 = (f32[8,32,128]{2,1,0:T(8,128)}, f32[8,32,128]{2,1,0:T(8,128)S(1)}, u32[]{:S(2)}, u32[]{:S(2)}) collective-permute-start(f32[8,32,128]{2,1,0:T(8,128)} %get-tuple-element.13), channel_id=1, source_target_pairs={{1,0},{2,1},{3,2},{4,3},{5,4},{6,5},{7,6},{9,8},{10,9},{11,10},{12... | collective-permute-start | bytes 393224 | tf_op jit(solution)/shard_map/ppermute | solution.py:268
  24.1 5.2 %shard_map.65.out_hbm = f32[8,16,64,128]{3,2,1,0:T(8,128)} custom-call(f32[2,16,64,128]{3,2,1,0:T(8,128)} %get-tuple-element.14.first_hbm, f32[8,16,64,128]{3,2,1,0:T(8,128)} %cot_hbm.1, f32[2,16,64,128]{3,2,1,0:T(8,128)} %cour_hbm.1), custom_call_target="tpu_custom_call" | custom-call | flops 12582912 | bytes 12582912 | tf_op jit(solution)/shard_map/pallas_call | solution.py:158
  29.3 0.0 collective-permute-done.2.lat_low_hbm
  29.3 0.0 copy-start.2
  29.3 0.0 collective-permute-done.3.lat_high_hbm
  29.3 0.0 copy-start.3
  29.3 0.0 collective-permute-done.lon_low_hbm
  29.4 0.0 copy-start
  29.4 0.0 collective-permute-done.1.lon_high_hbm
  29.4 0.6 %copy-done.2 = f32[8,32,128]{2,1,0:T(8,128)} copy-done((f32[8,32,128]{2,1,0:T(8,128)}, f32[8,32,128]{2,1,0:T(8,128)S(1)}, u32[]{:S(2)}) %copy-start.2) | copy-done | bytes 131096
  30.0 0.1 copy-done.3
  30.0 0.2 copy-done
  30.2 0.0 copy-start.1
  30.2 0.8 %copy-done.1 = f32[8,2,64,128]{3,2,1,0:T(8,128)} copy-done((f32[8,2,64,128]{3,2,1,0:T(8,128)}, f32[8,2,64,128]{3,2,1,0:T(8,128)S(1)}, u32[]{:S(2)}) %copy-start.1) | copy-done | bytes 524312
  31.0 3.3 %shard_map.66 = f32[8,16,64,128]{3,2,1,0:T(8,128)} custom-call(f32[8,2,64,128]{3,2,1,0:T(8,128)} %copy-done, f32[8,2,64,128]{3,2,1,0:T(8,128)} %copy-done.1, f32[8,32,128]{2,1,0:T(8,128)} %copy-done.2, f32[8,32,128]{2,1,0:T(8,128)} %copy-done.3, f32[8,16,64,128]{3,2,1,0:T(8,128)} %shard_map.65.out_hbm), custom_call_target="tpu_custom_call", output_to_operand_aliasing={{}: (4, {})} | custom-call | tf_op jit(solution)/shard_map/pallas_call | solution.py:229
  (2 shorter events, 0.0 us)
Async XLA Ops:
  9.3 20.0 %collective-permute-start = (f32[8,2,64,128]{3,2,1,0:T(8,128)}, f32[8,2,64,128]{3,2,1,0:T(8,128)S(1)}, u32[]{:S(2)}, u32[]{:S(2)}) collective-permute-start(f32[8,2,64,128]{3,2,1,0:T(8,128)} %get-tuple-element.10), channel_id=1, source_target_pairs={{0,8},{8,16},{16,24},{24,32},{32,40},{40,48},{48,56},{56,64},{64,7... | collective-permute-start | bytes 1572872 | tf_op jit(solution)/shard_map/ppermute | solution.py:264
  9.4 20.0 %collective-permute-start.1 = (f32[8,2,64,128]{3,2,1,0:T(8,128)}, f32[8,2,64,128]{3,2,1,0:T(8,128)S(1)}, u32[]{:S(2)}, u32[]{:S(2)}) collective-permute-start(f32[8,2,64,128]{3,2,1,0:T(8,128)} %get-tuple-element.11), channel_id=1, source_target_pairs={{8,0},{16,8},{24,16},{32,24},{40,32},{48,40},{56,48},{64,56},{72,6... | collective-permute-start | bytes 1572872 | tf_op jit(solution)/shard_map/ppermute | solution.py:265
  17.4 11.9 %collective-permute-start.2 = (f32[8,32,128]{2,1,0:T(8,128)}, f32[8,32,128]{2,1,0:T(8,128)S(1)}, u32[]{:S(2)}, u32[]{:S(2)}) collective-permute-start(f32[8,32,128]{2,1,0:T(8,128)} %get-tuple-element.12), channel_id=1, source_target_pairs={{0,1},{1,2},{2,3},{3,4},{4,5},{5,6},{6,7},{8,9},{9,10},{10,11},{11... | collective-permute-start | bytes 393224 | tf_op jit(solution)/shard_map/ppermute | solution.py:267
  20.0 9.4 %collective-permute-start.3 = (f32[8,32,128]{2,1,0:T(8,128)}, f32[8,32,128]{2,1,0:T(8,128)S(1)}, u32[]{:S(2)}, u32[]{:S(2)}) collective-permute-start(f32[8,32,128]{2,1,0:T(8,128)} %get-tuple-element.13), channel_id=1, source_target_pairs={{1,0},{2,1},{3,2},{4,3},{5,4},{6,5},{7,6},{9,8},{10,9},{11,10},{12... | collective-permute-start | bytes 393224 | tf_op jit(solution)/shard_map/ppermute | solution.py:268
  29.3 0.6 %copy-start.2 = (f32[8,32,128]{2,1,0:T(8,128)}, f32[8,32,128]{2,1,0:T(8,128)S(1)}, u32[]{:S(2)}) copy-start(f32[8,32,128]{2,1,0:T(8,128)S(1)} %collective-permute-done.2.lat_low_hbm) | copy-start | bytes 393220
  29.3 0.7 %copy-start.3 = (f32[8,32,128]{2,1,0:T(8,128)}, f32[8,32,128]{2,1,0:T(8,128)S(1)}, u32[]{:S(2)}) copy-start(f32[8,32,128]{2,1,0:T(8,128)S(1)} %collective-permute-done.3.lat_high_hbm) | copy-start | bytes 393220
  29.4 0.9 %copy-start = (f32[8,2,64,128]{3,2,1,0:T(8,128)}, f32[8,2,64,128]{3,2,1,0:T(8,128)S(1)}, u32[]{:S(2)}) copy-start(f32[8,2,64,128]{3,2,1,0:T(8,128)S(1)} %collective-permute-done.lon_low_hbm) | copy-start | bytes 1572868
  30.2 0.8 %copy-start.1 = (f32[8,2,64,128]{3,2,1,0:T(8,128)}, f32[8,2,64,128]{3,2,1,0:T(8,128)S(1)}, u32[]{:S(2)}) copy-start(f32[8,2,64,128]{3,2,1,0:T(8,128)S(1)} %collective-permute-done.1.lon_high_hbm) | copy-start | bytes 1572868

commit v7 on v6

--- a/solution.py
+++ b/solution.py
@@ -46,74 +46,84 @@
     return jnp.transpose(cloudy.reshape(nlon // rows, rows, nlat), (0, 2, 1))
 
 
-def sat_kernel(traj_ref, cot_ref, kind_ref, mask_ref, cour_ref,
-               out_ref, lon_bottom, lon_top, lat_bottom, lat_top):
-    fields, rows, nlat, lev = cot_ref.shape
-    step = pl.program_id(0)
-    last = pl.num_programs(0) - 1
+def sat_kernel(traj_hbm, cot_hbm, kind_hbm, cour_hbm, mask_ref,
+               first_hbm, lon_bottom, lon_top, lat_bottom, lat_top,
+               traj_v, cot_v, kind_v, cour_v, first_v, in_sems, out_sems):
+    fields, nlon, nlat, lev = cot_hbm.shape
+    rows = mask_ref.shape[2]
+    group = 4
     chunk = 32
     parts = nlat // chunk
-    for r in range(rows):
-        after = [[None] * parts for _ in range(fields)]
-        for j in range(parts):
-            lat = pl.ds(j * chunk, chunk)
-            cot = [cot_ref[k, r, lat, :] for k in range(4)]
-            new_heat, new_vapour = sat_adjoint(
-                traj_ref[0, r, lat, :], traj_ref[1, r, lat, :], kind_ref[r, lat, :], *cot
-            )
-            cloudy = jnp.broadcast_to(mask_ref[0, lat, r:r + 1], (chunk, lev)) > 0.0
-            heat = jnp.where(cloudy, new_heat, cot[0])
-            vapour = jnp.where(cloudy, new_vapour, cot[1])
-            out_ref[0, r, lat, :] = heat
-            out_ref[1, r, lat, :] = vapour
-            after[0][j] = heat
-            after[1][j] = vapour
-            for f in range(2, fields):
-                after[f][j] = cot_ref[f, r, lat, :]
-        low_weight = cour_ref[1, r, 0:2, :]
-        high_weight = cour_ref[1, r, nlat - 2:nlat, :]
-        for f in range(fields):
-            lat_bottom[f, 2 * r:2 * r + 2, :] = low_weight * after[f][0][0:2]
-            lat_top[f, 2 * r:2 * r + 2, :] = high_weight * after[f][parts - 1][chunk - 2:chunk]
-        if r < 2:
-            @pl.when(step == 0)
-            def _():
+    groups = []
+    for g in range(nlon // group):
+        span = slice(g * group, (g + 1) * group)
+        pairs = [(traj_hbm.at[:, span], traj_v.at[:, span]), (cot_hbm.at[:, span], cot_v.at[:, span]),
+                 (kind_hbm.at[span], kind_v.at[span]), (cour_hbm.at[:, span], cour_v.at[:, span])]
+        copies = [pltpu.make_async_copy(s, d, in_sems.at[4 * g + k]) for k, (s, d) in enumerate(pairs)]
+        for c in copies:
+            c.start()
+        groups.append(copies)
+    stores = []
+    for g in range(nlon // group):
+        for c in groups[g]:
+            c.wait()
+        for r in range(g * group, (g + 1) * group):
+            after = [[None] * parts for _ in range(fields)]
+            for j in range(parts):
+                lat = pl.ds(j * chunk, chunk)
+                cot = [cot_v[k, r, lat, :] for k in range(4)]
+                new_heat, new_vapour = sat_adjoint(
+                    traj_v[0, r, lat, :], traj_v[1, r, lat, :], kind_v[r, lat, :], *cot
+                )
+                cloudy = jnp.broadcast_to(mask_ref[r // rows, lat, r % rows:r % rows + 1], (chunk, lev)) > 0.0
+                heat = jnp.where(cloudy, new_heat, cot[0])
+                vapour = jnp.where(cloudy, new_vapour, cot[1])
+                first_v[0, r, lat, :] = heat
+                first_v[1, r, lat, :] = vapour
+                after[0][j] = heat
+                after[1][j] = vapour
+                for f in range(2, fields):
+                    after[f][j] = cot_v[f, r, lat, :]
+            low_weight = cour_v[1, r, 0:2, :]
+            high_weight = cour_v[1, r, nlat - 2:nlat, :]
+            for f in range(fields):
+                lat_bottom[f, 2 * r:2 * r + 2, :] = low_weight * after[f][0][0:2]
+                lat_top[f, 2 * r:2 * r + 2, :] = high_weight * after[f][parts - 1][chunk - 2:chunk]
+            if r < 2 or r >= nlon - 2:
+                target, at = (lon_bottom, r) if r < 2 else (lon_top, r - nlon + 2)
                 for f in range(fields):
                     for j in range(parts):
                         lat = pl.ds(j * chunk, chunk)
-                        lon_bottom[f, r, lat, :] = cour_ref[0, r, lat, :] * after[f][j]
-        if r >= rows - 2:
-            @pl.when(step == last)
-            def _():
-                for f in range(fields):
-                    for j in range(parts):
-                        lat = pl.ds(j * chunk, chunk)
-                        lon_top[f, r - rows + 2, lat, :] = cour_ref[0, r, lat, :] * after[f][j]
+                        target[f, at, lat, :] = cour_v[0, r, lat, :] * after[f][j]
+        span = slice(g * group, (g + 1) * group)
+        store = pltpu.make_async_copy(first_v.at[:, span], first_hbm.at[:, span], out_sems.at[g])
+        store.start()
+        stores.append(store)
+    for store in stores:
+        store.wait()
 
 
 def first_pair(trajectory, cotangent, branch, mask, courant, rows):
     fields, nlon, nlat, lev = cotangent.shape
     lon_send = jax.ShapeDtypeStruct((fields, 2, nlat, lev), jnp.float32)
     lat_send = jax.ShapeDtypeStruct((fields, 2 * nlon, lev), jnp.float32)
+    hbm = pl.BlockSpec(memory_space=pltpu.HBM)
+    vmem = pl.BlockSpec(memory_space=pltpu.VMEM)
     return pl.pallas_call(
         sat_kernel,
-        grid=(nlon // rows,),
-        in_specs=[
-            pl.BlockSpec((2, rows, nlat, lev), lambda i: (0, i, 0, 0)),
-            pl.BlockSpec((fields, rows, nlat, lev), lambda i: (0, i, 0, 0)),
-            pl.BlockSpec((rows, nlat, lev), lambda i: (i, 0, 0)),
-            pl.BlockSpec((1, nlat, rows), lambda i: (i, 0, 0)),
-            pl.BlockSpec((2, rows, nlat, lev), lambda i: (0, i, 0, 0)),
+        in_specs=[hbm, hbm, hbm, hbm, vmem],
+        out_specs=[hbm, vmem, vmem, vmem, vmem],
+        out_shape=[jax.ShapeDtypeStruct((2, nlon, nlat, lev), jnp.float32), lon_send, lon_send, lat_send, lat_send],
+        scratch_shapes=[
+            pltpu.VMEM(trajectory.shape, jnp.float32),
+            pltpu.VMEM(cotangent.shape, jnp.float32),
+            pltpu.VMEM(branch.shape, jnp.int32),
+            pltpu.VMEM(courant.shape, jnp.float32),
+            pltpu.VMEM((2, nlon, nlat, lev), jnp.float32),
+            pltpu.SemaphoreType.DMA((4 * nlon // 4,)),
+            pltpu.SemaphoreType.DMA((nlon // 4,)),
         ],
-        out_specs=[
-            pl.BlockSpec((2, rows, nlat, lev), lambda i: (0, i, 0, 0)),
-            pl.BlockSpec((fields, 2, nlat, lev), lambda i: (0, 0, 0, 0)),
-            pl.BlockSpec((fields, 2, nlat, lev), lambda i: (0, 0, 0, 0)),
-            pl.BlockSpec((fields, 2 * rows, lev), lambda i: (0, i, 0)),
-            pl.BlockSpec((fields, 2 * rows, lev), lambda i: (0, i, 0)),
-        ],
-        out_shape=[jax.ShapeDtypeStruct((2, nlon, nlat, lev), jnp.float32), lon_send, lon_send, lat_send, lat_send],
-    )(trajectory, cotangent, branch, mask, courant)
+    )(trajectory, cotangent, branch, courant, mask)
 
 
 def stencil_kernel(first_hbm, cot_hbm, cour_hbm, out_hbm, field_v, cour_v, out_v, lon_pad, lat_pad, in_sems, out_sems):
@@ -173,17 +183,16 @@
     )(first, cotangent, courant)
 
 
-def halo_kernel(lon_low_hbm, lon_high_hbm, lat_low_hbm, lat_high_hbm, out_hbm, out_ref,
-                lon_low, lon_high, lat_low, lat_high, lon_lo_buf, lon_hi_buf, lat_lo_buf, lat_hi_buf, sems):
+def halo_kernel(lon_low, lon_high, lat_low, lat_high, out_hbm, out_ref,
+                lon_lo_buf, lon_hi_buf, lat_lo_buf, lat_hi_buf, sems):
     fields, nlon, nlat, lev = out_hbm.shape
-    halos = [(lon_low_hbm, lon_low), (lon_high_hbm, lon_high), (lat_low_hbm, lat_low), (lat_high_hbm, lat_high)]
     regions = [
         (out_hbm.at[:, 0:2], lon_lo_buf),
         (out_hbm.at[:, nlon - 2:nlon], lon_hi_buf),
         (out_hbm.at[:, 2:nlon - 2, 0:8], lat_lo_buf),
         (out_hbm.at[:, 2:nlon - 2, nlat - 8:nlat], lat_hi_buf),
     ]
-    copies = [pltpu.make_async_copy(s, d, sems.at[i]) for i, (s, d) in enumerate(halos + regions)]
+    copies = [pltpu.make_async_copy(s, d, sems.at[i]) for i, (s, d) in enumerate(regions)]
     for c in copies:
         c.start()
     for c in copies:
@@ -225,17 +234,14 @@
 
 def add_halos(out, lon_low, lon_high, lat_low, lat_high):
     fields, nlon, nlat, lev = out.shape
-    hbm = pl.BlockSpec(memory_space=pl.ANY)
+    hbm = pl.BlockSpec(memory_space=pltpu.HBM)
+    vmem = pl.BlockSpec(memory_space=pltpu.VMEM)
     return pl.pallas_call(
         halo_kernel,
-        in_specs=[hbm] * 5,
+        in_specs=[vmem, vmem, vmem, vmem, hbm],
         out_specs=hbm,
         out_shape=jax.ShapeDtypeStruct(out.shape, jnp.float32),
         scratch_shapes=[
-            pltpu.VMEM(lon_low.shape, jnp.float32),
-            pltpu.VMEM(lon_high.shape, jnp.float32),
-            pltpu.VMEM(lat_low.shape, jnp.float32),
-            pltpu.VMEM(lat_high.shape, jnp.float32),
             pltpu.VMEM((fields, 2, nlat, lev), jnp.float32),
             pltpu.VMEM((fields, 2, nlat, lev), jnp.float32),
             pltpu.VMEM((fields, nlon - 4, 8, lev), jnp.float32),

time: 34.4 us -> 36.4 us (1.058)
  Pallas kernels: 15.1 us -> 16.9 us
    pallas_call x2, Pallas kernels: 9.93 us -> 11.7 us  [the longest x1 7.61 us: first_pair(): pl.pallas_call(sat_kernel, in_specs=[hbm, hbm, hbm, hbm, vmem], out_specs...]
  transfers between devices with their start and end apart: 4 -> 4, of which waited for: 0 -> 0; matrix products, arithmetic and copies ran while one was open for 0% -> 0% of each run, Pallas kernels for 15% -> 14%
where the time goes in v7:
time: 36.4 us; the launch traced here: 36.1 us
  Pallas kernels  16.9 us (46%)
  starting transfers between devices  14.8 us (41%)
  local copies, waits for them, and re-layouts  2.43 us (7%)
  other arithmetic  1.2 us (3%)
  between operations  0.77 us (2%)
    ppermute x1, starting transfers between devices, on_device(): lon_high = lax.ppermute(lon_bottom, 'lon', backward)  8 us
    pallas_call x1, Pallas kernels, first_pair(): pl.pallas_call(sat_kernel, in_specs=[hbm, hbm, hbm, hbm, vmem], out_specs...  7.61 us
    pallas_call x1, Pallas kernels, advect(): pl.pallas_call(stencil_kernel, in_specs=[hbm, hbm, hbm], out_specs=hbm, o...  5.18 us
    ppermute x1, starting transfers between devices, on_device(): lat_high = lax.ppermute(lat_bottom, 'lat', backward)  4.16 us
    pallas_call x1, Pallas kernels, add_halos(): pl.pallas_call(halo_kernel, in_specs=[vmem, vmem, vmem, vmem, hbm], out_s...  4.14 us
    ppermute x1, starting transfers between devices, on_device(): lat_low = lax.ppermute(lat_top, 'lat', forward)  2.57 us
    unnamed x8, local copies, waits for them, and re-layouts  1.63 us
    transpose x2, local copies, waits for them, and re-layouts, cloudy_columns(): return jnp.transpose(cloudy.reshape(nlon // rows, rows, nlat), (0, 2, 1))  0.8 us
  transfers between devices with their start and end apart: 4, of which 0 were waited for; matrix products, arithmetic and copies ran while one was open for 0% of the time, Pallas kernels for 14%

profile of v7, /device:TPU:2, one launch (start us, length us, event | category | flops | bytes accessed | tf_op | source)
XLA Modules:
  0.0 36.1 jit_solution(11521700816968571363)
XLA Ops:
  0.7 0.7 %reduce = s32[768]{0:T(1024)S(1)} reduce(s32[1,1,768]{2,1,0:T(1,128)} %param.10, s32[]{:T(128)} %constant.8), dimensions={0,1}, to_apply=%param.10.reduce_sub_computation | reduce | bytes 6148 | tf_op args[4]
  1.4 0.5 %fusion.1 = pred[1024]{0:T(1024)(128)(4,1)S(1)} fusion(s32[768]{0:T(1024)S(1)} %reduce, pred[768]{0:T(1024)(128)(4,1)S(1)} %iota_compare_fusion.1), kind=kLoop, calls=%fused_computation.2 | loop fusion | flops 2358272 | bytes 4864 | tf_op jit(solution)/shard_map/reduce_or | solution.py:45
  1.9 0.1 reshape.9
  1.9 0.7 %copy.9 = f32[2,8,64]{1,2,0:T(8,128)} copy(f32[2,8,64]{2,1,0:T(8,128)S(1)} %reshape.9) | data formatting | bytes 8192 | tf_op jit(solution)/shard_map/transpose | solution.py:46
  2.7 7.6 %shard_map.64 = (f32[2,16,64,128]{3,2,1,0:T(8,128)}, f32[8,2,64,128]{3,2,1,0:T(8,128)}, f32[8,2,64,128]{3,2,1,0:T(8,128)}, f32[8,32,128]{2,1,0:T(8,128)}, f32[8,32,128]{2,1,0:T(8,128)}) custom-call(f32[2,16,64,128]{3,2,1,0:T(8,128)} %traj_hbm.1, f32[8,16,64,128]{3,2,1,0:T(8,128)} %cot_hbm.3, s32[16,64,128]{2,1,0:T(8,128)} %kind_hbm.1, ...), custom_call_target="tpu_custom_call" | custom-call | tf_op jit(solution)/shard_map/pallas_call | solution.py:112
  10.3 0.1 collective-permute-start
  10.4 8.0 %collective-permute-start.1 = (f32[8,2,64,128]{3,2,1,0:T(8,128)}, f32[8,2,64,128]{3,2,1,0:T(8,128)S(1)}, u32[]{:S(2)}, u32[]{:S(2)}) collective-permute-start(f32[8,2,64,128]{3,2,1,0:T(8,128)} %get-tuple-element.11), channel_id=1, source_target_pairs={{8,0},{16,8},{24,16},{32,24},{40,32},{48,40},{56,48},{64,56},{72,6... | collective-permute-start | bytes 1572872 | tf_op jit(solution)/shard_map/ppermute | solution.py:271
  18.4 2.6 %collective-permute-start.2 = (f32[8,32,128]{2,1,0:T(8,128)}, f32[8,32,128]{2,1,0:T(8,128)S(1)}, u32[]{:S(2)}, u32[]{:S(2)}) collective-permute-start(f32[8,32,128]{2,1,0:T(8,128)} %get-tuple-element.12), channel_id=1, source_target_pairs={{0,1},{1,2},{2,3},{3,4},{4,5},{5,6},{6,7},{8,9},{9,10},{10,11},{11... | collective-permute-start | bytes 393224 | tf_op jit(solution)/shard_map/ppermute | solution.py:273
  21.0 4.2 %collective-permute-start.3 = (f32[8,32,128]{2,1,0:T(8,128)}, f32[8,32,128]{2,1,0:T(8,128)S(1)}, u32[]{:S(2)}, u32[]{:S(2)}) collective-permute-start(f32[8,32,128]{2,1,0:T(8,128)} %get-tuple-element.13), channel_id=1, source_target_pairs={{1,0},{2,1},{3,2},{4,3},{5,4},{6,5},{7,6},{9,8},{10,9},{11,10},{12... | collective-permute-start | bytes 393224 | tf_op jit(solution)/shard_map/ppermute | solution.py:274
  25.1 5.2 %shard_map.65.out_hbm = f32[8,16,64,128]{3,2,1,0:T(8,128)} custom-call(f32[2,16,64,128]{3,2,1,0:T(8,128)} %get-tuple-element.14.first_hbm, f32[8,16,64,128]{3,2,1,0:T(8,128)} %cot_hbm.3, f32[2,16,64,128]{3,2,1,0:T(8,128)} %cour_hbm.3), custom_call_target="tpu_custom_call" | custom-call | flops 12582912 | bytes 12582912 | tf_op jit(solution)/shard_map/pallas_call | solution.py:168
  30.3 0.0 collective-permute-done.2.lat_low
  30.3 0.0 copy-start.2
  30.3 0.0 collective-permute-done.3.lat_high
  30.3 0.0 copy-start.3
  30.4 0.0 collective-permute-done.lon_low
  30.4 0.0 copy-start
  30.4 0.0 collective-permute-done.1.lon_high
  30.4 0.6 %copy-done.2 = f32[8,32,128]{2,1,0:T(8,128)} copy-done((f32[8,32,128]{2,1,0:T(8,128)}, f32[8,32,128]{2,1,0:T(8,128)S(1)}, u32[]{:S(2)}) %copy-start.2) | copy-done | bytes 131096
  31.0 0.1 copy-done.3
  31.0 0.2 copy-done
  31.2 0.0 copy-start.1
  31.2 0.8 %copy-done.1 = f32[8,2,64,128]{3,2,1,0:T(8,128)} copy-done((f32[8,2,64,128]{3,2,1,0:T(8,128)}, f32[8,2,64,128]{3,2,1,0:T(8,128)S(1)}, u32[]{:S(2)}) %copy-start.1) | copy-done | bytes 524312
  32.0 4.1 %shard_map.66 = f32[8,16,64,128]{3,2,1,0:T(8,128)} custom-call(f32[8,2,64,128]{3,2,1,0:T(8,128)} %copy-done, f32[8,2,64,128]{3,2,1,0:T(8,128)} %copy-done.1, f32[8,32,128]{2,1,0:T(8,128)} %copy-done.2, f32[8,32,128]{2,1,0:T(8,128)} %copy-done.3, f32[8,16,64,128]{3,2,1,0:T(8,128)} %shard_map.65.out_hbm), custom_call_target="tpu_custom_call", output_to_operand_aliasing={{}: (4, {})} | custom-call | tf_op jit(solution)/shard_map/pallas_call | solution.py:239
  (2 shorter events, 0.0 us)
Async XLA Ops:
  10.3 20.1 %collective-permute-start = (f32[8,2,64,128]{3,2,1,0:T(8,128)}, f32[8,2,64,128]{3,2,1,0:T(8,128)S(1)}, u32[]{:S(2)}, u32[]{:S(2)}) collective-permute-start(f32[8,2,64,128]{3,2,1,0:T(8,128)} %get-tuple-element.10), channel_id=1, source_target_pairs={{0,8},{8,16},{16,24},{24,32},{32,40},{40,48},{48,56},{56,64},{64,7... | collective-permute-start | bytes 1572872 | tf_op jit(solution)/shard_map/ppermute | solution.py:270
  10.4 20.0 %collective-permute-start.1 = (f32[8,2,64,128]{3,2,1,0:T(8,128)}, f32[8,2,64,128]{3,2,1,0:T(8,128)S(1)}, u32[]{:S(2)}, u32[]{:S(2)}) collective-permute-start(f32[8,2,64,128]{3,2,1,0:T(8,128)} %get-tuple-element.11), channel_id=1, source_target_pairs={{8,0},{16,8},{24,16},{32,24},{40,32},{48,40},{56,48},{64,56},{72,6... | collective-permute-start | bytes 1572872 | tf_op jit(solution)/shard_map/ppermute | solution.py:271
  18.4 11.9 %collective-permute-start.2 = (f32[8,32,128]{2,1,0:T(8,128)}, f32[8,32,128]{2,1,0:T(8,128)S(1)}, u32[]{:S(2)}, u32[]{:S(2)}) collective-permute-start(f32[8,32,128]{2,1,0:T(8,128)} %get-tuple-element.12), channel_id=1, source_target_pairs={{0,1},{1,2},{2,3},{3,4},{4,5},{5,6},{6,7},{8,9},{9,10},{10,11},{11... | collective-permute-start | bytes 393224 | tf_op jit(solution)/shard_map/ppermute | solution.py:273
  21.0 9.4 %collective-permute-start.3 = (f32[8,32,128]{2,1,0:T(8,128)}, f32[8,32,128]{2,1,0:T(8,128)S(1)}, u32[]{:S(2)}, u32[]{:S(2)}) collective-permute-start(f32[8,32,128]{2,1,0:T(8,128)} %get-tuple-element.13), channel_id=1, source_target_pairs={{1,0},{2,1},{3,2},{4,3},{5,4},{6,5},{7,6},{9,8},{10,9},{11,10},{12... | collective-permute-start | bytes 393224 | tf_op jit(solution)/shard_map/ppermute | solution.py:274
  30.3 0.6 %copy-start.2 = (f32[8,32,128]{2,1,0:T(8,128)}, f32[8,32,128]{2,1,0:T(8,128)S(1)}, u32[]{:S(2)}) copy-start(f32[8,32,128]{2,1,0:T(8,128)S(1)} %collective-permute-done.2.lat_low) | copy-start | bytes 393220
  30.3 0.7 %copy-start.3 = (f32[8,32,128]{2,1,0:T(8,128)}, f32[8,32,128]{2,1,0:T(8,128)S(1)}, u32[]{:S(2)}) copy-start(f32[8,32,128]{2,1,0:T(8,128)S(1)} %collective-permute-done.3.lat_high) | copy-start | bytes 393220
  30.4 0.9 %copy-start = (f32[8,2,64,128]{3,2,1,0:T(8,128)}, f32[8,2,64,128]{3,2,1,0:T(8,128)S(1)}, u32[]{:S(2)}) copy-start(f32[8,2,64,128]{3,2,1,0:T(8,128)S(1)} %collective-permute-done.lon_low) | copy-start | bytes 1572868
  31.2 0.8 %copy-start.1 = (f32[8,2,64,128]{3,2,1,0:T(8,128)}, f32[8,2,64,128]{3,2,1,0:T(8,128)S(1)}, u32[]{:S(2)}) copy-start(f32[8,2,64,128]{3,2,1,0:T(8,128)S(1)} %collective-permute-done.1.lon_high) | copy-start | bytes 1572868

commit v8 on v6

--- a/solution.py
+++ b/solution.py
@@ -174,19 +174,28 @@
 
 
 def halo_kernel(lon_low_hbm, lon_high_hbm, lat_low_hbm, lat_high_hbm, out_hbm, out_ref,
-                lon_low, lon_high, lat_low, lat_high, lon_lo_buf, lon_hi_buf, lat_lo_buf, lat_hi_buf, sems):
+                lon_low, lon_high, lat_low, lat_high, lon_lo_buf, lon_hi_buf, lat_lo_buf, lat_hi_buf, sems, in_sems, out_sems):
     fields, nlon, nlat, lev = out_hbm.shape
     halos = [(lon_low_hbm, lon_low), (lon_high_hbm, lon_high), (lat_low_hbm, lat_low), (lat_high_hbm, lat_high)]
-    regions = [
-        (out_hbm.at[:, 0:2], lon_lo_buf),
-        (out_hbm.at[:, nlon - 2:nlon], lon_hi_buf),
-        (out_hbm.at[:, 2:nlon - 2, 0:8], lat_lo_buf),
-        (out_hbm.at[:, 2:nlon - 2, nlat - 8:nlat], lat_hi_buf),
-    ]
-    copies = [pltpu.make_async_copy(s, d, sems.at[i]) for i, (s, d) in enumerate(halos + regions)]
-    for c in copies:
+    halo_copies = [pltpu.make_async_copy(s, d, sems.at[i]) for i, (s, d) in enumerate(halos)]
+    for c in halo_copies:
         c.start()
-    for c in copies:
+
+    def regions(f):
+        return [
+            (out_hbm.at[f, 0:2], lon_lo_buf.at[f]),
+            (out_hbm.at[f, nlon - 2:nlon], lon_hi_buf.at[f]),
+            (out_hbm.at[f, 2:nlon - 2, 0:8], lat_lo_buf.at[f]),
+            (out_hbm.at[f, 2:nlon - 2, nlat - 8:nlat], lat_hi_buf.at[f]),
+        ]
+
+    loads = []
+    for f in range(fields):
+        copies = [pltpu.make_async_copy(s, d, in_sems.at[4 * f + i]) for i, (s, d) in enumerate(regions(f))]
+        for c in copies:
+            c.start()
+        loads.append(copies)
+    for c in halo_copies:
         c.wait()
     sub = lax.broadcasted_iota(jnp.int32, (8, lev), 0)
 
@@ -199,7 +208,10 @@
         row7 = (8.0 * high_rows[0:1] - high_rows[1:2]) / 12.0
         return tile + jnp.where(sub == 6, row6, jnp.where(sub == 7, row7, 0.0))
 
+    stores = []
     for f in range(fields):
+        for c in loads[f]:
+            c.wait()
         lo = lon_low[f]
         hi = lon_high[f]
         edge_terms = [(lo[0] - 8.0 * lo[1]) / 12.0, lo[1] / 12.0, -hi[0] / 12.0, (8.0 * hi[0] - hi[1]) / 12.0]
@@ -216,10 +228,11 @@
             high_rows = lat_high[f, 2 * r:2 * r + 2]
             lat_lo_buf[f, r - 2] = lat_fix(lat_lo_buf[f, r - 2], low_rows, high_rows, True)
             lat_hi_buf[f, r - 2] = lat_fix(lat_hi_buf[f, r - 2], low_rows, high_rows, False)
-    copies = [pltpu.make_async_copy(d, s, sems.at[4 + i]) for i, (s, d) in enumerate(regions)]
-    for c in copies:
-        c.start()
-    for c in copies:
+        copies = [pltpu.make_async_copy(d, s, out_sems.at[4 * f + i]) for i, (s, d) in enumerate(regions(f))]
+        for c in copies:
+            c.start()
+        stores += copies
+    for c in stores:
         c.wait()
 
 
@@ -240,7 +253,9 @@
             pltpu.VMEM((fields, 2, nlat, lev), jnp.float32),
             pltpu.VMEM((fields, nlon - 4, 8, lev), jnp.float32),
             pltpu.VMEM((fields, nlon - 4, 8, lev), jnp.float32),
-            pltpu.SemaphoreType.DMA((8,)),
+            pltpu.SemaphoreType.DMA((4,)),
+            pltpu.SemaphoreType.DMA((4 * fields,)),
+            pltpu.SemaphoreType.DMA((4 * fields,)),
         ],
         input_output_aliases={4: 0},
     )(lon_low, lon_high, lat_low, lat_high, out)
@@ -260,12 +275,12 @@
     rows = 8
     mask = cloudy_columns(cloud_list, cloud_count, nlon, nlat, rows)
     first, lon_bottom, lon_top, lat_bottom, lat_top = first_pair(trajectory, cotangent, branch, mask, courant, rows)
-    forward, backward = neighbours("lon", True)
-    lon_low = lax.ppermute(lon_top, "lon", forward)
-    lon_high = lax.ppermute(lon_bottom, "lon", backward)
     forward, backward = neighbours("lat", False)
     lat_low = lax.ppermute(lat_top, "lat", forward)
     lat_high = lax.ppermute(lat_bottom, "lat", backward)
+    forward, backward = neighbours("lon", True)
+    lon_high = lax.ppermute(lon_bottom, "lon", backward)
+    lon_low = lax.ppermute(lon_top, "lon", forward)
     out = advect(first, cotangent, courant)
     return add_halos(out, lon_low, lon_high, lat_low, lat_high)
 

time: 34.4 us -> 34.9 us (1.015)
  Pallas kernels: 15.1 us -> 15.6 us
    pallas_call x1, Pallas kernels: 3.27 us -> 3.75 us  [add_halos(): pl.pallas_call(halo_kernel, in_specs=[hbm] * 5, out_specs=hbm, out_shape=...]
where the time goes in v8:
time: 34.9 us; the launch traced here: 34.7 us
  Pallas kernels  15.6 us (45%)
  starting transfers between devices  14.8 us (42%)
  local copies, waits for them, and re-layouts  2.43 us (7%)
  other arithmetic  1.2 us (3%)
  between operations  0.76 us (2%)
    ppermute x1, starting transfers between devices, on_device(): lon_high = lax.ppermute(lon_bottom, 'lon', backward)  8 us
    pallas_call x1, Pallas kernels, first_pair(): pl.pallas_call(sat_kernel, grid=(nlon // rows,), in_specs=[pl.BlockSpec((...  6.65 us
    pallas_call x1, Pallas kernels, advect(): pl.pallas_call(stencil_kernel, in_specs=[hbm, hbm, hbm], out_specs=hbm, o...  5.18 us
    ppermute x1, starting transfers between devices, on_device(): lat_high = lax.ppermute(lat_bottom, 'lat', backward)  4.16 us
    pallas_call x1, Pallas kernels, add_halos(): pl.pallas_call(halo_kernel, in_specs=[hbm] * 5, out_specs=hbm, out_shape=...  3.75 us
    ppermute x1, starting transfers between devices, on_device(): lat_low = lax.ppermute(lat_top, 'lat', forward)  2.57 us
    unnamed x8, local copies, waits for them, and re-layouts  1.63 us
    transpose x2, local copies, waits for them, and re-layouts, cloudy_columns(): return jnp.transpose(cloudy.reshape(nlon // rows, rows, nlat), (0, 2, 1))  0.8 us
  transfers between devices with their start and end apart: 4, of which 0 were waited for; matrix products, arithmetic and copies ran while one was open for 0% of the time, Pallas kernels for 15%

profile of v8, /device:TPU:2, one launch (start us, length us, event | category | flops | bytes accessed | tf_op | source)
XLA Modules:
  0.0 34.7 jit_solution(7783422308588031576)
XLA Ops:
  0.7 0.7 %reduce = s32[768]{0:T(1024)S(1)} reduce(s32[1,1,768]{2,1,0:T(1,128)} %param.10, s32[]{:T(128)} %constant.8), dimensions={0,1}, to_apply=%param.10.reduce_sub_computation | reduce | bytes 6148 | tf_op args[4]
  1.4 0.5 %fusion.1 = pred[1024]{0:T(1024)(128)(4,1)S(1)} fusion(s32[768]{0:T(1024)S(1)} %reduce, pred[768]{0:T(1024)(128)(4,1)S(1)} %iota_compare_fusion.1), kind=kLoop, calls=%fused_computation.2 | loop fusion | flops 2358272 | bytes 4864 | tf_op jit(solution)/shard_map/reduce_or | solution.py:45
  1.9 0.1 reshape.9
  1.9 0.7 %copy.9 = f32[2,8,64]{1,2,0:T(8,128)} copy(f32[2,8,64]{2,1,0:T(8,128)S(1)} %reshape.9) | data formatting | bytes 8192 | tf_op jit(solution)/shard_map/transpose | solution.py:46
  2.7 6.7 %shard_map.64 = (f32[2,16,64,128]{3,2,1,0:T(8,128)}, f32[8,2,64,128]{3,2,1,0:T(8,128)}, f32[8,2,64,128]{3,2,1,0:T(8,128)}, f32[8,32,128]{2,1,0:T(8,128)}, f32[8,32,128]{2,1,0:T(8,128)}) custom-call(f32[2,16,64,128]{3,2,1,0:T(8,128)} %traj_ref.1, f32[8,16,64,128]{3,2,1,0:T(8,128)} %cot_hbm.1, s32[16,64,128]{2,1,0:T(8,128)} %kind_ref.1, f32[2,64,8]{2,1,0:T(8,128)} %bitcast.3, ...), custom_call_target="tpu_custom_call" | custom-call | tf_op jit(solution)/shard_map/pallas_call | solution.py:98
  9.3 0.0 collective-permute-start
  9.4 8.0 %collective-permute-start.1 = (f32[8,2,64,128]{3,2,1,0:T(8,128)}, f32[8,2,64,128]{3,2,1,0:T(8,128)S(1)}, u32[]{:S(2)}, u32[]{:S(2)}) collective-permute-start(f32[8,2,64,128]{3,2,1,0:T(8,128)} %get-tuple-element.11), channel_id=1, source_target_pairs={{8,0},{16,8},{24,16},{32,24},{40,32},{48,40},{56,48},{64,56},{72,6... | collective-permute-start | bytes 1572872 | tf_op jit(solution)/shard_map/ppermute | solution.py:282
  17.4 2.6 %collective-permute-start.2 = (f32[8,32,128]{2,1,0:T(8,128)}, f32[8,32,128]{2,1,0:T(8,128)S(1)}, u32[]{:S(2)}, u32[]{:S(2)}) collective-permute-start(f32[8,32,128]{2,1,0:T(8,128)} %get-tuple-element.12), channel_id=1, source_target_pairs={{0,1},{1,2},{2,3},{3,4},{4,5},{5,6},{6,7},{8,9},{9,10},{10,11},{11... | collective-permute-start | bytes 393224 | tf_op jit(solution)/shard_map/ppermute | solution.py:279
  20.0 4.2 %collective-permute-start.3 = (f32[8,32,128]{2,1,0:T(8,128)}, f32[8,32,128]{2,1,0:T(8,128)S(1)}, u32[]{:S(2)}, u32[]{:S(2)}) collective-permute-start(f32[8,32,128]{2,1,0:T(8,128)} %get-tuple-element.13), channel_id=1, source_target_pairs={{1,0},{2,1},{3,2},{4,3},{5,4},{6,5},{7,6},{9,8},{10,9},{11,10},{12... | collective-permute-start | bytes 393224 | tf_op jit(solution)/shard_map/ppermute | solution.py:280
  24.1 5.2 %shard_map.65.out_hbm = f32[8,16,64,128]{3,2,1,0:T(8,128)} custom-call(f32[2,16,64,128]{3,2,1,0:T(8,128)} %get-tuple-element.14.first_hbm, f32[8,16,64,128]{3,2,1,0:T(8,128)} %cot_hbm.1, f32[2,16,64,128]{3,2,1,0:T(8,128)} %cour_hbm.1), custom_call_target="tpu_custom_call" | custom-call | flops 12582912 | bytes 12582912 | tf_op jit(solution)/shard_map/pallas_call | solution.py:158
  29.3 0.0 collective-permute-done.2.lat_low_hbm
  29.3 0.0 copy-start.2
  29.3 0.0 collective-permute-done.3.lat_high_hbm
  29.3 0.0 copy-start.3
  29.3 0.0 collective-permute-done.lon_low_hbm
  29.4 0.0 copy-start
  29.4 0.0 collective-permute-done.1.lon_high_hbm
  29.4 0.6 %copy-done.2 = f32[8,32,128]{2,1,0:T(8,128)} copy-done((f32[8,32,128]{2,1,0:T(8,128)}, f32[8,32,128]{2,1,0:T(8,128)S(1)}, u32[]{:S(2)}) %copy-start.2) | copy-done | bytes 131096
  30.0 0.1 copy-done.3
  30.0 0.2 copy-done
  30.2 0.0 copy-start.1
  30.2 0.8 %copy-done.1 = f32[8,2,64,128]{3,2,1,0:T(8,128)} copy-done((f32[8,2,64,128]{3,2,1,0:T(8,128)}, f32[8,2,64,128]{3,2,1,0:T(8,128)S(1)}, u32[]{:S(2)}) %copy-start.1) | copy-done | bytes 524312
  31.0 3.7 %shard_map.66 = f32[8,16,64,128]{3,2,1,0:T(8,128)} custom-call(f32[8,2,64,128]{3,2,1,0:T(8,128)} %copy-done, f32[8,2,64,128]{3,2,1,0:T(8,128)} %copy-done.1, f32[8,32,128]{2,1,0:T(8,128)} %copy-done.2, f32[8,32,128]{2,1,0:T(8,128)} %copy-done.3, f32[8,16,64,128]{3,2,1,0:T(8,128)} %shard_map.65.out_hbm), custom_call_target="tpu_custom_call", output_to_operand_aliasing={{}: (4, {})} | custom-call | tf_op jit(solution)/shard_map/pallas_call | solution.py:242
  (2 shorter events, 0.0 us)
Async XLA Ops:
  9.3 20.0 %collective-permute-start = (f32[8,2,64,128]{3,2,1,0:T(8,128)}, f32[8,2,64,128]{3,2,1,0:T(8,128)S(1)}, u32[]{:S(2)}, u32[]{:S(2)}) collective-permute-start(f32[8,2,64,128]{3,2,1,0:T(8,128)} %get-tuple-element.10), channel_id=1, source_target_pairs={{0,8},{8,16},{16,24},{24,32},{32,40},{40,48},{48,56},{56,64},{64,7... | collective-permute-start | bytes 1572872 | tf_op jit(solution)/shard_map/ppermute | solution.py:283
  9.4 20.0 %collective-permute-start.1 = (f32[8,2,64,128]{3,2,1,0:T(8,128)}, f32[8,2,64,128]{3,2,1,0:T(8,128)S(1)}, u32[]{:S(2)}, u32[]{:S(2)}) collective-permute-start(f32[8,2,64,128]{3,2,1,0:T(8,128)} %get-tuple-element.11), channel_id=1, source_target_pairs={{8,0},{16,8},{24,16},{32,24},{40,32},{48,40},{56,48},{64,56},{72,6... | collective-permute-start | bytes 1572872 | tf_op jit(solution)/shard_map/ppermute | solution.py:282
  17.4 11.9 %collective-permute-start.2 = (f32[8,32,128]{2,1,0:T(8,128)}, f32[8,32,128]{2,1,0:T(8,128)S(1)}, u32[]{:S(2)}, u32[]{:S(2)}) collective-permute-start(f32[8,32,128]{2,1,0:T(8,128)} %get-tuple-element.12), channel_id=1, source_target_pairs={{0,1},{1,2},{2,3},{3,4},{4,5},{5,6},{6,7},{8,9},{9,10},{10,11},{11... | collective-permute-start | bytes 393224 | tf_op jit(solution)/shard_map/ppermute | solution.py:279
  20.0 9.4 %collective-permute-start.3 = (f32[8,32,128]{2,1,0:T(8,128)}, f32[8,32,128]{2,1,0:T(8,128)S(1)}, u32[]{:S(2)}, u32[]{:S(2)}) collective-permute-start(f32[8,32,128]{2,1,0:T(8,128)} %get-tuple-element.13), channel_id=1, source_target_pairs={{1,0},{2,1},{3,2},{4,3},{5,4},{6,5},{7,6},{9,8},{10,9},{11,10},{12... | collective-permute-start | bytes 393224 | tf_op jit(solution)/shard_map/ppermute | solution.py:280
  29.3 0.6 %copy-start.2 = (f32[8,32,128]{2,1,0:T(8,128)}, f32[8,32,128]{2,1,0:T(8,128)S(1)}, u32[]{:S(2)}) copy-start(f32[8,32,128]{2,1,0:T(8,128)S(1)} %collective-permute-done.2.lat_low_hbm) | copy-start | bytes 393220
  29.3 0.7 %copy-start.3 = (f32[8,32,128]{2,1,0:T(8,128)}, f32[8,32,128]{2,1,0:T(8,128)S(1)}, u32[]{:S(2)}) copy-start(f32[8,32,128]{2,1,0:T(8,128)S(1)} %collective-permute-done.3.lat_high_hbm) | copy-start | bytes 393220
  29.4 0.9 %copy-start = (f32[8,2,64,128]{3,2,1,0:T(8,128)}, f32[8,2,64,128]{3,2,1,0:T(8,128)S(1)}, u32[]{:S(2)}) copy-start(f32[8,2,64,128]{3,2,1,0:T(8,128)S(1)} %collective-permute-done.lon_low_hbm) | copy-start | bytes 1572868
  30.2 0.8 %copy-start.1 = (f32[8,2,64,128]{3,2,1,0:T(8,128)}, f32[8,2,64,128]{3,2,1,0:T(8,128)S(1)}, u32[]{:S(2)}) copy-start(f32[8,2,64,128]{3,2,1,0:T(8,128)S(1)} %collective-permute-done.1.lon_high_hbm) | copy-start | bytes 1572868

commit v9 on v6

--- a/solution.py
+++ b/solution.py
@@ -13,27 +13,38 @@
 latent_ice = 1.3
 
 
-def increments(warmth, vapour, kinds):
+def sat_adjoint(warmth, vapour, kinds, cot_heat, cot_vapour, cot_liquid, cot_ice):
     mixed = jax.nn.sigmoid(2.0 * warmth)
     liquid_share = jnp.where(kinds == 1, 1.0, jnp.where(kinds == 2, 0.0, mixed))
     latent = latent_liquid * liquid_share + latent_ice * (1.0 - liquid_share)
     active = (kinds > 0).astype(warmth.dtype)
+    half_latent = growth * latent
     amount = jnp.zeros_like(warmth)
+    saved = []
     for newton_step in range(NEWT):
         saturated = jnp.exp(growth * (warmth + latent * amount))
+        inverse = 1.0 / (1.0 + half_latent * saturated)
         excess = vapour - amount - saturated
-        amount = amount + excess / (1.0 + growth * latent * saturated)
+        saved.append((amount, saturated, inverse, excess))
+        amount = amount + excess * inverse
     amount = active * amount
-    return (latent * amount, -amount, liquid_share * amount, (1.0 - liquid_share) * amount)
-
-
-def sat_adjoint(warmth, vapour, kinds, cot_heat, cot_vapour, cot_liquid, cot_ice):
-
-    def forward(first_in, second_in):
-        return increments(first_in, second_in, kinds)
-
-    unused, pullback = jax.vjp(forward, warmth, vapour)
-    grad_heat, grad_vapour = pullback((cot_heat, cot_vapour, cot_liquid, cot_ice))
+    grad_amount = latent * cot_heat - cot_vapour + liquid_share * cot_liquid + (1.0 - liquid_share) * cot_ice
+    grad_share = amount * (cot_liquid - cot_ice)
+    grad_latent = amount * cot_heat
+    grad = active * grad_amount
+    grad_heat = jnp.zeros_like(warmth)
+    grad_vapour = jnp.zeros_like(warmth)
+    for amount, saturated, inverse, excess in reversed(saved):
+        slope = excess * inverse * inverse
+        grad_sat = -grad * (inverse + half_latent * slope)
+        half_sat = growth * saturated
+        grad_heat = grad_heat + grad_sat * half_sat
+        grad_latent = grad_latent + grad_sat * half_sat * amount - grad * slope * half_sat
+        grad_vapour = grad_vapour + grad * inverse
+        grad = grad * (1.0 - inverse) + grad_sat * half_latent * saturated
+    grad_share = grad_share + (latent_liquid - latent_ice) * grad_latent
+    mixed_kind = (kinds == 0) | (kinds == 3)
+    grad_heat = grad_heat + jnp.where(mixed_kind, grad_share * 2.0 * mixed * (1.0 - mixed), 0.0)
     return (cot_heat + grad_heat, cot_vapour + grad_vapour)
 
 

time: 34.4 us -> 34.4 us (level)
  no operation moved by 1% of the time
where the time goes in v9:
time: 34.4 us; the launch traced here: 34.2 us
  Pallas kernels  15 us (44%)
  starting transfers between devices  14.8 us (43%)
  local copies, waits for them, and re-layouts  2.43 us (7%)
  other arithmetic  1.2 us (3%)
  between operations  0.76 us (2%)
    ppermute x1, starting transfers between devices, on_device(): lon_high = lax.ppermute(lon_bottom, 'lon', backward)  8 us
    pallas_call x1, Pallas kernels, first_pair(): pl.pallas_call(sat_kernel, grid=(nlon // rows,), in_specs=[pl.BlockSpec((...  6.59 us
    pallas_call x1, Pallas kernels, advect(): pl.pallas_call(stencil_kernel, in_specs=[hbm, hbm, hbm], out_specs=hbm, o...  5.18 us
    ppermute x1, starting transfers between devices, on_device(): lat_high = lax.ppermute(lat_bottom, 'lat', backward)  4.16 us
    pallas_call x1, Pallas kernels, add_halos(): pl.pallas_call(halo_kernel, in_specs=[hbm] * 5, out_specs=hbm, out_shape=...  3.27 us
    ppermute x1, starting transfers between devices, on_device(): lat_low = lax.ppermute(lat_top, 'lat', forward)  2.57 us
    unnamed x8, local copies, waits for them, and re-layouts  1.63 us
    transpose x2, local copies, waits for them, and re-layouts, cloudy_columns(): return jnp.transpose(cloudy.reshape(nlon // rows, rows, nlat), (0, 2, 1))  0.8 us
  transfers between devices with their start and end apart: 4, of which 0 were waited for; matrix products, arithmetic and copies ran while one was open for 0% of the time, Pallas kernels for 15%

profile of v9, /device:TPU:2, one launch (start us, length us, event | category | flops | bytes accessed | tf_op | source)
XLA Modules:
  0.0 34.2 jit_solution(9702892243780848701)
XLA Ops:
  0.7 0.7 %reduce = s32[768]{0:T(1024)S(1)} reduce(s32[1,1,768]{2,1,0:T(1,128)} %param.10, s32[]{:T(128)} %constant.8), dimensions={0,1}, to_apply=%param.10.reduce_sub_computation | reduce | bytes 6148 | tf_op args[4]
  1.4 0.5 %fusion.1 = pred[1024]{0:T(1024)(128)(4,1)S(1)} fusion(s32[768]{0:T(1024)S(1)} %reduce, pred[768]{0:T(1024)(128)(4,1)S(1)} %iota_compare_fusion.1), kind=kLoop, calls=%fused_computation.2 | loop fusion | flops 2358272 | bytes 4864 | tf_op jit(solution)/shard_map/reduce_or | solution.py:56
  1.9 0.1 reshape.9
  1.9 0.7 %copy.9 = f32[2,8,64]{1,2,0:T(8,128)} copy(f32[2,8,64]{2,1,0:T(8,128)S(1)} %reshape.9) | data formatting | bytes 8192 | tf_op jit(solution)/shard_map/transpose | solution.py:57
  2.7 6.6 %shard_map.64 = (f32[2,16,64,128]{3,2,1,0:T(8,128)}, f32[8,2,64,128]{3,2,1,0:T(8,128)}, f32[8,2,64,128]{3,2,1,0:T(8,128)}, f32[8,32,128]{2,1,0:T(8,128)}, f32[8,32,128]{2,1,0:T(8,128)}) custom-call(f32[2,16,64,128]{3,2,1,0:T(8,128)} %traj_ref.1, f32[8,16,64,128]{3,2,1,0:T(8,128)} %cot_hbm.1, s32[16,64,128]{2,1,0:T(8,128)} %kind_ref.1, f32[2,64,8]{2,1,0:T(8,128)} %bitcast.3, ...), custom_call_target="tpu_custom_call" | custom-call | tf_op jit(solution)/shard_map/pallas_call | solution.py:109
  9.3 0.0 collective-permute-start
  9.3 8.0 %collective-permute-start.1 = (f32[8,2,64,128]{3,2,1,0:T(8,128)}, f32[8,2,64,128]{3,2,1,0:T(8,128)S(1)}, u32[]{:S(2)}, u32[]{:S(2)}) collective-permute-start(f32[8,2,64,128]{3,2,1,0:T(8,128)} %get-tuple-element.11), channel_id=1, source_target_pairs={{8,0},{16,8},{24,16},{32,24},{40,32},{48,40},{56,48},{64,56},{72,6... | collective-permute-start | bytes 1572872 | tf_op jit(solution)/shard_map/ppermute | solution.py:276
  17.3 2.6 %collective-permute-start.2 = (f32[8,32,128]{2,1,0:T(8,128)}, f32[8,32,128]{2,1,0:T(8,128)S(1)}, u32[]{:S(2)}, u32[]{:S(2)}) collective-permute-start(f32[8,32,128]{2,1,0:T(8,128)} %get-tuple-element.12), channel_id=1, source_target_pairs={{0,1},{1,2},{2,3},{3,4},{4,5},{5,6},{6,7},{8,9},{9,10},{10,11},{11... | collective-permute-start | bytes 393224 | tf_op jit(solution)/shard_map/ppermute | solution.py:278
  19.9 4.2 %collective-permute-start.3 = (f32[8,32,128]{2,1,0:T(8,128)}, f32[8,32,128]{2,1,0:T(8,128)S(1)}, u32[]{:S(2)}, u32[]{:S(2)}) collective-permute-start(f32[8,32,128]{2,1,0:T(8,128)} %get-tuple-element.13), channel_id=1, source_target_pairs={{1,0},{2,1},{3,2},{4,3},{5,4},{6,5},{7,6},{9,8},{10,9},{11,10},{12... | collective-permute-start | bytes 393224 | tf_op jit(solution)/shard_map/ppermute | solution.py:279
  24.0 5.2 %shard_map.65.out_hbm = f32[8,16,64,128]{3,2,1,0:T(8,128)} custom-call(f32[2,16,64,128]{3,2,1,0:T(8,128)} %get-tuple-element.14.first_hbm, f32[8,16,64,128]{3,2,1,0:T(8,128)} %cot_hbm.1, f32[2,16,64,128]{3,2,1,0:T(8,128)} %cour_hbm.1), custom_call_target="tpu_custom_call" | custom-call | flops 12582912 | bytes 12582912 | tf_op jit(solution)/shard_map/pallas_call | solution.py:169
  29.2 0.0 collective-permute-done.2.lat_low_hbm
  29.2 0.0 copy-start.2
  29.3 0.0 collective-permute-done.3.lat_high_hbm
  29.3 0.0 copy-start.3
  29.3 0.0 collective-permute-done.lon_low_hbm
  29.3 0.0 copy-start
  29.3 0.0 collective-permute-done.1.lon_high_hbm
  29.3 0.6 %copy-done.2 = f32[8,32,128]{2,1,0:T(8,128)} copy-done((f32[8,32,128]{2,1,0:T(8,128)}, f32[8,32,128]{2,1,0:T(8,128)S(1)}, u32[]{:S(2)}) %copy-start.2) | copy-done | bytes 131096
  29.9 0.1 copy-done.3
  30.0 0.2 copy-done
  30.1 0.0 copy-start.1
  30.1 0.8 %copy-done.1 = f32[8,2,64,128]{3,2,1,0:T(8,128)} copy-done((f32[8,2,64,128]{3,2,1,0:T(8,128)}, f32[8,2,64,128]{3,2,1,0:T(8,128)S(1)}, u32[]{:S(2)}) %copy-start.1) | copy-done | bytes 524312
  30.9 3.3 %shard_map.66 = f32[8,16,64,128]{3,2,1,0:T(8,128)} custom-call(f32[8,2,64,128]{3,2,1,0:T(8,128)} %copy-done, f32[8,2,64,128]{3,2,1,0:T(8,128)} %copy-done.1, f32[8,32,128]{2,1,0:T(8,128)} %copy-done.2, f32[8,32,128]{2,1,0:T(8,128)} %copy-done.3, f32[8,16,64,128]{3,2,1,0:T(8,128)} %shard_map.65.out_hbm), custom_call_target="tpu_custom_call", output_to_operand_aliasing={{}: (4, {})} | custom-call | tf_op jit(solution)/shard_map/pallas_call | solution.py:240
  (2 shorter events, 0.0 us)
Async XLA Ops:
  9.3 20.0 %collective-permute-start = (f32[8,2,64,128]{3,2,1,0:T(8,128)}, f32[8,2,64,128]{3,2,1,0:T(8,128)S(1)}, u32[]{:S(2)}, u32[]{:S(2)}) collective-permute-start(f32[8,2,64,128]{3,2,1,0:T(8,128)} %get-tuple-element.10), channel_id=1, source_target_pairs={{0,8},{8,16},{16,24},{24,32},{32,40},{40,48},{48,56},{56,64},{64,7... | collective-permute-start | bytes 1572872 | tf_op jit(solution)/shard_map/ppermute | solution.py:275
  9.3 20.0 %collective-permute-start.1 = (f32[8,2,64,128]{3,2,1,0:T(8,128)}, f32[8,2,64,128]{3,2,1,0:T(8,128)S(1)}, u32[]{:S(2)}, u32[]{:S(2)}) collective-permute-start(f32[8,2,64,128]{3,2,1,0:T(8,128)} %get-tuple-element.11), channel_id=1, source_target_pairs={{8,0},{16,8},{24,16},{32,24},{40,32},{48,40},{56,48},{64,56},{72,6... | collective-permute-start | bytes 1572872 | tf_op jit(solution)/shard_map/ppermute | solution.py:276
  17.3 11.9 %collective-permute-start.2 = (f32[8,32,128]{2,1,0:T(8,128)}, f32[8,32,128]{2,1,0:T(8,128)S(1)}, u32[]{:S(2)}, u32[]{:S(2)}) collective-permute-start(f32[8,32,128]{2,1,0:T(8,128)} %get-tuple-element.12), channel_id=1, source_target_pairs={{0,1},{1,2},{2,3},{3,4},{4,5},{5,6},{6,7},{8,9},{9,10},{10,11},{11... | collective-permute-start | bytes 393224 | tf_op jit(solution)/shard_map/ppermute | solution.py:278
  19.9 9.4 %collective-permute-start.3 = (f32[8,32,128]{2,1,0:T(8,128)}, f32[8,32,128]{2,1,0:T(8,128)S(1)}, u32[]{:S(2)}, u32[]{:S(2)}) collective-permute-start(f32[8,32,128]{2,1,0:T(8,128)} %get-tuple-element.13), channel_id=1, source_target_pairs={{1,0},{2,1},{3,2},{4,3},{5,4},{6,5},{7,6},{9,8},{10,9},{11,10},{12... | collective-permute-start | bytes 393224 | tf_op jit(solution)/shard_map/ppermute | solution.py:279
  29.2 0.6 %copy-start.2 = (f32[8,32,128]{2,1,0:T(8,128)}, f32[8,32,128]{2,1,0:T(8,128)S(1)}, u32[]{:S(2)}) copy-start(f32[8,32,128]{2,1,0:T(8,128)S(1)} %collective-permute-done.2.lat_low_hbm) | copy-start | bytes 393220
  29.3 0.7 %copy-start.3 = (f32[8,32,128]{2,1,0:T(8,128)}, f32[8,32,128]{2,1,0:T(8,128)S(1)}, u32[]{:S(2)}) copy-start(f32[8,32,128]{2,1,0:T(8,128)S(1)} %collective-permute-done.3.lat_high_hbm) | copy-start | bytes 393220
  29.3 0.9 %copy-start = (f32[8,2,64,128]{3,2,1,0:T(8,128)}, f32[8,2,64,128]{3,2,1,0:T(8,128)S(1)}, u32[]{:S(2)}) copy-start(f32[8,2,64,128]{3,2,1,0:T(8,128)S(1)} %collective-permute-done.lon_low_hbm) | copy-start | bytes 1572868
  30.1 0.8 %copy-start.1 = (f32[8,2,64,128]{3,2,1,0:T(8,128)}, f32[8,2,64,128]{3,2,1,0:T(8,128)S(1)}, u32[]{:S(2)}) copy-start(f32[8,2,64,128]{3,2,1,0:T(8,128)S(1)} %collective-permute-done.1.lon_high_hbm) | copy-start | bytes 1572868

commit v10 on v9

--- a/solution.py
+++ b/solution.py
@@ -57,8 +57,8 @@
     return jnp.transpose(cloudy.reshape(nlon // rows, rows, nlat), (0, 2, 1))
 
 
-def sat_kernel(traj_ref, cot_ref, kind_ref, mask_ref, cour_ref,
-               out_ref, lon_bottom, lon_top, lat_bottom, lat_top):
+def sat_kernel(parity_ref, traj_ref, cot_ref, kind_ref, mask_ref, cour_ref,
+               out_ref, lon_mate, lon_far, lat_mate, lat_far):
     fields, rows, nlat, lev = cot_ref.shape
     step = pl.program_id(0)
     last = pl.num_programs(0) - 1
@@ -83,26 +83,27 @@
                 after[f][j] = cot_ref[f, r, lat, :]
         low_weight = cour_ref[1, r, 0:2, :]
         high_weight = cour_ref[1, r, nlat - 2:nlat, :]
+        lat_even = parity_ref[1] == 0
         for f in range(fields):
-            lat_bottom[f, 2 * r:2 * r + 2, :] = low_weight * after[f][0][0:2]
-            lat_top[f, 2 * r:2 * r + 2, :] = high_weight * after[f][parts - 1][chunk - 2:chunk]
-        if r < 2:
-            @pl.when(step == 0)
-            def _():
-                for f in range(fields):
-                    for j in range(parts):
-                        lat = pl.ds(j * chunk, chunk)
-                        lon_bottom[f, r, lat, :] = cour_ref[0, r, lat, :] * after[f][j]
-        if r >= rows - 2:
-            @pl.when(step == last)
-            def _():
-                for f in range(fields):
-                    for j in range(parts):
-                        lat = pl.ds(j * chunk, chunk)
-                        lon_top[f, r - rows + 2, lat, :] = cour_ref[0, r, lat, :] * after[f][j]
-
-
-def first_pair(trajectory, cotangent, branch, mask, courant, rows):
+            bottom = low_weight * after[f][0][0:2]
+            top = high_weight * after[f][parts - 1][chunk - 2:chunk]
+            lat_mate[f, 2 * r:2 * r + 2, :] = jnp.where(lat_even, top, bottom)
+            lat_far[f, 2 * r:2 * r + 2, :] = jnp.where(lat_even, bottom, top)
+        lon_even = parity_ref[0] == 0
+        for edge_step, edge_rows, mate_when in ((0, range(2), jnp.logical_not(lon_even)), (last, range(rows - 2, rows), lon_even)):
+            if r not in edge_rows:
+                continue
+            at = r - edge_rows[0]
+            for target, flag in ((lon_mate, mate_when), (lon_far, jnp.logical_not(mate_when))):
+                @pl.when((step == edge_step) & flag)
+                def _():
+                    for f in range(fields):
+                        for j in range(parts):
+                            lat = pl.ds(j * chunk, chunk)
+                            target[f, at, lat, :] = cour_ref[0, r, lat, :] * after[f][j]
+
+
+def first_pair(parity, trajectory, cotangent, branch, mask, courant, rows):
     fields, nlon, nlat, lev = cotangent.shape
     lon_send = jax.ShapeDtypeStruct((fields, 2, nlat, lev), jnp.float32)
     lat_send = jax.ShapeDtypeStruct((fields, 2 * nlon, lev), jnp.float32)
@@ -110,6 +111,7 @@
         sat_kernel,
         grid=(nlon // rows,),
         in_specs=[
+            pl.BlockSpec(memory_space=pltpu.SMEM),
             pl.BlockSpec((2, rows, nlat, lev), lambda i: (0, i, 0, 0)),
             pl.BlockSpec((fields, rows, nlat, lev), lambda i: (0, i, 0, 0)),
             pl.BlockSpec((rows, nlat, lev), lambda i: (i, 0, 0)),
@@ -124,7 +126,7 @@
             pl.BlockSpec((fields, 2 * rows, lev), lambda i: (0, i, 0)),
         ],
         out_shape=[jax.ShapeDtypeStruct((2, nlon, nlat, lev), jnp.float32), lon_send, lon_send, lat_send, lat_send],
-    )(trajectory, cotangent, branch, mask, courant)
+    )(parity, trajectory, cotangent, branch, mask, courant)
 
 
 def stencil_kernel(first_hbm, cot_hbm, cour_hbm, out_hbm, field_v, cour_v, out_v, lon_pad, lat_pad, in_sems, out_sems):
@@ -184,10 +186,12 @@
     )(first, cotangent, courant)
 
 
-def halo_kernel(lon_low_hbm, lon_high_hbm, lat_low_hbm, lat_high_hbm, out_hbm, out_ref,
-                lon_low, lon_high, lat_low, lat_high, lon_lo_buf, lon_hi_buf, lat_lo_buf, lat_hi_buf, sems):
+def halo_kernel(parity_ref, lon_mate_hbm, lon_far_hbm, lat_mate_hbm, lat_far_hbm, out_hbm, out_ref,
+                lon_mate, lon_far, lat_mate, lat_far, lon_lo_buf, lon_hi_buf, lat_lo_buf, lat_hi_buf, sems):
     fields, nlon, nlat, lev = out_hbm.shape
-    halos = [(lon_low_hbm, lon_low), (lon_high_hbm, lon_high), (lat_low_hbm, lat_low), (lat_high_hbm, lat_high)]
+    halos = [(lon_mate_hbm, lon_mate), (lon_far_hbm, lon_far), (lat_mate_hbm, lat_mate), (lat_far_hbm, lat_far)]
+    lon_even = parity_ref[0] == 0
+    lat_even = parity_ref[1] == 0
     regions = [
         (out_hbm.at[:, 0:2], lon_lo_buf),
         (out_hbm.at[:, nlon - 2:nlon], lon_hi_buf),
@@ -211,20 +215,20 @@
         return tile + jnp.where(sub == 6, row6, jnp.where(sub == 7, row7, 0.0))
 
     for f in range(fields):
-        lo = lon_low[f]
-        hi = lon_high[f]
+        lo = jnp.where(lon_even, lon_far[f], lon_mate[f])
+        hi = jnp.where(lon_even, lon_mate[f], lon_far[f])
         edge_terms = [(lo[0] - 8.0 * lo[1]) / 12.0, lo[1] / 12.0, -hi[0] / 12.0, (8.0 * hi[0] - hi[1]) / 12.0]
         for k, r in enumerate((0, 1, nlon - 2, nlon - 1)):
             buf = lon_lo_buf if k < 2 else lon_hi_buf
             block = buf[f, k % 2] + edge_terms[k]
-            low_rows = lat_low[f, 2 * r:2 * r + 2]
-            high_rows = lat_high[f, 2 * r:2 * r + 2]
+            low_rows = jnp.where(lat_even, lat_far[f, 2 * r:2 * r + 2], lat_mate[f, 2 * r:2 * r + 2])
+            high_rows = jnp.where(lat_even, lat_mate[f, 2 * r:2 * r + 2], lat_far[f, 2 * r:2 * r + 2])
             buf[f, k % 2] = block
             buf[f, k % 2, 0:8] = lat_fix(block[0:8], low_rows, high_rows, True)
             buf[f, k % 2, nlat - 8:nlat] = lat_fix(block[nlat - 8:nlat], low_rows, high_rows, False)
         for r in range(2, nlon - 2):
-            low_rows = lat_low[f, 2 * r:2 * r + 2]
-            high_rows = lat_high[f, 2 * r:2 * r + 2]
+            low_rows = jnp.where(lat_even, lat_far[f, 2 * r:2 * r + 2], lat_mate[f, 2 * r:2 * r + 2])
+            high_rows = jnp.where(lat_even, lat_mate[f, 2 * r:2 * r + 2], lat_far[f, 2 * r:2 * r + 2])
             lat_lo_buf[f, r - 2] = lat_fix(lat_lo_buf[f, r - 2], low_rows, high_rows, True)
             lat_hi_buf[f, r - 2] = lat_fix(lat_hi_buf[f, r - 2], low_rows, high_rows, False)
     copies = [pltpu.make_async_copy(d, s, sems.at[4 + i]) for i, (s, d) in enumerate(regions)]
@@ -234,12 +238,12 @@
         c.wait()
 
 
-def add_halos(out, lon_low, lon_high, lat_low, lat_high):
+def add_halos(parity, out, lon_low, lon_high, lat_low, lat_high):
     fields, nlon, nlat, lev = out.shape
     hbm = pl.BlockSpec(memory_space=pl.ANY)
     return pl.pallas_call(
         halo_kernel,
-        in_specs=[hbm] * 5,
+        in_specs=[pl.BlockSpec(memory_space=pltpu.SMEM)] + [hbm] * 5,
         out_specs=hbm,
         out_shape=jax.ShapeDtypeStruct(out.shape, jnp.float32),
         scratch_shapes=[
@@ -253,32 +257,38 @@
             pltpu.VMEM((fields, nlon - 4, 8, lev), jnp.float32),
             pltpu.SemaphoreType.DMA((8,)),
         ],
-        input_output_aliases={4: 0},
-    )(lon_low, lon_high, lat_low, lat_high, out)
-
-
-def neighbours(axis, periodic):
+        input_output_aliases={5: 0},
+    )(parity, lon_low, lon_high, lat_low, lat_high, out)
+
+
+def pairings(axis, periodic):
     count = lax.axis_size(axis)
-    forward = [(i, i + 1) for i in range(count - 1)]
-    if periodic:
-        forward.append((count - 1, 0))
-    backward = [(target, source) for source, target in forward]
-    return forward, backward
+    mate = [(i, i ^ 1) for i in range(count)]
+    far = []
+    for i in range(1, count, 2):
+        j = i + 1
+        if j == count:
+            if not periodic:
+                continue
+            j = 0
+        far += [(i, j), (j, i)]
+    return mate, far
 
 
 def on_device(trajectory, cotangent, courant, branch, cloud_list, cloud_count):
     fields, nlon, nlat, lev = cotangent.shape
     rows = 8
+    parity = jnp.stack([lax.axis_index("lon") % 2, lax.axis_index("lat") % 2]).astype(jnp.int32)
     mask = cloudy_columns(cloud_list, cloud_count, nlon, nlat, rows)
-    first, lon_bottom, lon_top, lat_bottom, lat_top = first_pair(trajectory, cotangent, branch, mask, courant, rows)
-    forward, backward = neighbours("lon", True)
-    lon_low = lax.ppermute(lon_top, "lon", forward)
-    lon_high = lax.ppermute(lon_bottom, "lon", backward)
-    forward, backward = neighbours("lat", False)
-    lat_low = lax.ppermute(lat_top, "lat", forward)
-    lat_high = lax.ppermute(lat_bottom, "lat", backward)
+    first, lon_mate, lon_far, lat_mate, lat_far = first_pair(parity, trajectory, cotangent, branch, mask, courant, rows)
+    mate, far = pairings("lon", True)
+    lon_mate = lax.ppermute(lon_mate, "lon", mate)
+    lon_far = lax.ppermute(lon_far, "lon", far)
+    mate, far = pairings("lat", False)
+    lat_mate = lax.ppermute(lat_mate, "lat", mate)
+    lat_far = lax.ppermute(lat_far, "lat", far)
     out = advect(first, cotangent, courant)
-    return add_halos(out, lon_low, lon_high, lat_low, lat_high)
+    return add_halos(parity, out, lon_mate, lon_far, lat_mate, lat_far)
 
 
 def solution(mesh):

time: 34.4 us -> 34.2 us (level)
  starting transfers between devices: 14.8 us -> 12.5 us
  Pallas kernels: 15 us -> 15.9 us
  other arithmetic: 1.2 us -> 1.85 us
  waiting for transfers between devices: 0.01 us -> 0.63 us
    ppermute x4, starting transfers between devices: 14.8 us -> 12.5 us  [the longest x1 8.59 us: on_device(): lon_far = lax.ppermute(lon_far, 'lon', far)]
    pallas_call x2, Pallas kernels: 9.86 us -> 10.7 us  [the longest x1 6.68 us: first_pair(): pl.pallas_call(sat_kernel, grid=(nlon // rows,), in_specs=[pl.BlockSpec(m...]
    another operation x0 -> x1, other arithmetic: none -> 0.66 us  [on_device(): jnp.stack([lax.axis_index('lon') % 2, lax.axis_index('lat') % 2])]
    ppermute x4, waiting for transfers between devices: 0.01 us -> 0.63 us  [the longest x1 0.58 us: on_device(): lat_mate = lax.ppermute(lat_mate, 'lat', mate)]
  transfers between devices with their start and end apart: 4 -> 4, of which waited for: 0 -> 1; matrix products, arithmetic and copies ran while one was open for 0% -> 0% of each run, Pallas kernels for 15% -> 15%
where the time goes in v10:
time: 34.2 us; the launch traced here: 34 us
  Pallas kernels  15.9 us (46%)
  starting transfers between devices  12.5 us (37%)
  local copies, waits for them, and re-layouts  2.42 us (7%)
  other arithmetic  1.85 us (5%)
  between operations  0.71 us (2%)
  waiting for transfers between devices  0.63 us (2%)
    ppermute x1, starting transfers between devices, on_device(): lon_far = lax.ppermute(lon_far, 'lon', far)  8.59 us
    pallas_call x1, Pallas kernels, first_pair(): pl.pallas_call(sat_kernel, grid=(nlon // rows,), in_specs=[pl.BlockSpec(m...  6.68 us
    pallas_call x1, Pallas kernels, advect(): pl.pallas_call(stencil_kernel, in_specs=[hbm, hbm, hbm], out_specs=hbm, o...  5.18 us
    pallas_call x1, Pallas kernels, add_halos(): pl.pallas_call(halo_kernel, in_specs=[pl.BlockSpec(memory_space=pltpu.SME...  4 us
    ppermute x1, starting transfers between devices, on_device(): lat_far = lax.ppermute(lat_far, 'lat', far)  3.22 us
    unnamed x8, local copies, waits for them, and re-layouts  1.62 us
    transpose x2, local copies, waits for them, and re-layouts, cloudy_columns(): return jnp.transpose(cloudy.reshape(nlon // rows, rows, nlat), (0, 2, 1))  0.8 us
    unnamed x1, other arithmetic  0.7 us
  transfers between devices with their start and end apart: 4, of which 1 were waited for; matrix products, arithmetic and copies ran while one was open for 0% of the time, Pallas kernels for 15%

profile of v10, /device:TPU:2, one launch (start us, length us, event | category | flops | bytes accessed | tf_op | source)
XLA Modules:
  0.0 34.0 jit_solution(7625600785179131561)
XLA Ops:
  0.7 0.7 %reduce = s32[768]{0:T(1024)S(1)} reduce(s32[1,1,768]{2,1,0:T(1,128)} %param.10, s32[]{:T(128)} %constant.23.clone.1), dimensions={0,1}, to_apply=%param.10.reduce_sub_computation | reduce | bytes 6148 | tf_op args[4]
  1.4 0.5 %fusion.1 = pred[1024]{0:T(1024)(128)(4,1)S(1)} fusion(s32[768]{0:T(1024)S(1)} %reduce, pred[768]{0:T(1024)(128)(4,1)S(1)} %iota_compare_fusion.1), kind=kLoop, calls=%fused_computation.2 | loop fusion | flops 2358272 | bytes 4864 | tf_op jit(solution)/shard_map/reduce_or | solution.py:56
  1.9 0.1 reshape.9
  1.9 0.7 %copy.9 = f32[2,8,64]{1,2,0:T(8,128)} copy(f32[2,8,64]{2,1,0:T(8,128)S(1)} %reshape.9) | data formatting | bytes 8192 | tf_op jit(solution)/shard_map/transpose | solution.py:57
  2.7 0.7 %pad_add_fusion.parity_ref = s32[2]{0:T(128)} fusion(s32[1]{0:T(128)} %bitcast.1, s32[1]{0:T(128)} %bitcast), kind=kLoop, calls=%fused_computation.4 | loop fusion | flops 2 | bytes 16 | tf_op jit(solution)/shard_map/stack | solution.py:281
  3.3 6.7 %shard_map.64 = (f32[2,16,64,128]{3,2,1,0:T(8,128)}, f32[8,2,64,128]{3,2,1,0:T(8,128)}, f32[8,2,64,128]{3,2,1,0:T(8,128)}, f32[8,32,128]{2,1,0:T(8,128)}, f32[8,32,128]{2,1,0:T(8,128)}) custom-call(s32[2]{0:T(128)} %pad_add_fusion.parity_ref, f32[2,16,64,128]{3,2,1,0:T(8,128)} %traj_ref.1, f32[8,16,64,128]{3,2,1,0:T(8,128)} %cot_hbm.1, ...), custom_call_target="tpu_custom_call" | custom-call | tf_op jit(solution)/shard_map/pallas_call | solution.py:110
  10.0 0.1 collective-permute-start
  10.1 8.6 %collective-permute-start.1 = (f32[8,2,64,128]{3,2,1,0:T(8,128)}, f32[8,2,64,128]{3,2,1,0:T(8,128)S(1)}, u32[]{:S(2)}, u32[]{:S(2)}) collective-permute-start(f32[8,2,64,128]{3,2,1,0:T(8,128)} %get-tuple-element.11), channel_id=1, source_target_pairs={{8,16},{16,8},{24,32},{32,24},{40,48},{48,40},{56,64},{64,56},{72,... | collective-permute-start | bytes 1572872 | tf_op jit(solution)/shard_map/ppermute | solution.py:286
  18.7 0.7 %collective-permute-start.2 = (f32[8,32,128]{2,1,0:T(8,128)}, f32[8,32,128]{2,1,0:T(8,128)S(1)}, u32[]{:S(2)}, u32[]{:S(2)}) collective-permute-start(f32[8,32,128]{2,1,0:T(8,128)} %get-tuple-element.12), channel_id=1, source_target_pairs={{0,1},{1,0},{2,3},{3,2},{4,5},{5,4},{6,7},{7,6},{8,9},{9,8},{10,11... | collective-permute-start | bytes 393224 | tf_op jit(solution)/shard_map/ppermute | solution.py:288
  19.3 3.2 %collective-permute-start.3 = (f32[8,32,128]{2,1,0:T(8,128)}, f32[8,32,128]{2,1,0:T(8,128)S(1)}, u32[]{:S(2)}, u32[]{:S(2)}) collective-permute-start(f32[8,32,128]{2,1,0:T(8,128)} %get-tuple-element.13), channel_id=1, source_target_pairs={{1,2},{2,1},{3,4},{4,3},{5,6},{6,5},{9,10},{10,9},{11,12},{12,11},... | collective-permute-start | bytes 393224 | tf_op jit(solution)/shard_map/ppermute | solution.py:289
  22.6 5.2 %shard_map.65.out_hbm = f32[8,16,64,128]{3,2,1,0:T(8,128)} custom-call(f32[2,16,64,128]{3,2,1,0:T(8,128)} %get-tuple-element.14.first_hbm, f32[8,16,64,128]{3,2,1,0:T(8,128)} %cot_hbm.1, f32[2,16,64,128]{3,2,1,0:T(8,128)} %cour_hbm.1), custom_call_target="tpu_custom_call" | custom-call | flops 12582912 | bytes 12582912 | tf_op jit(solution)/shard_map/pallas_call | solution.py:171
  27.7 0.6 %collective-permute-done.2.lat_mate_hbm = f32[8,32,128]{2,1,0:T(8,128)S(1)} collective-permute-done((f32[8,32,128]{2,1,0:T(8,128)}, f32[8,32,128]{2,1,0:T(8,128)S(1)}, u32[]{:S(2)}, u32[]{:S(2)}) %collective-permute-start.2) | collective-permute-done | bytes 131104 | tf_op jit(solution)/shard_map/ppermute | solution.py:288
  28.3 0.0 copy-start.2
  28.3 0.0 collective-permute-done.3.lat_far_hbm
  28.3 0.0 copy-start.3
  28.3 0.0 collective-permute-done.lon_mate_hbm
  28.3 0.0 copy-start
  28.4 0.0 collective-permute-done.1.lon_far_hbm
  28.4 0.6 %copy-done.2 = f32[8,32,128]{2,1,0:T(8,128)} copy-done((f32[8,32,128]{2,1,0:T(8,128)}, f32[8,32,128]{2,1,0:T(8,128)S(1)}, u32[]{:S(2)}) %copy-start.2) | copy-done | bytes 131096
  29.0 0.1 copy-done.3
  29.1 0.2 copy-done
  29.2 0.0 copy-start.1
  29.2 0.8 %copy-done.1 = f32[8,2,64,128]{3,2,1,0:T(8,128)} copy-done((f32[8,2,64,128]{3,2,1,0:T(8,128)}, f32[8,2,64,128]{3,2,1,0:T(8,128)S(1)}, u32[]{:S(2)}) %copy-start.1) | copy-done | bytes 524312
  30.0 4.0 %shard_map.66 = f32[8,16,64,128]{3,2,1,0:T(8,128)} custom-call(s32[2]{0:T(128)} %pad_add_fusion.parity_ref, f32[8,2,64,128]{3,2,1,0:T(8,128)} %copy-done, f32[8,2,64,128]{3,2,1,0:T(8,128)} %copy-done.1, f32[8,32,128]{2,1,0:T(8,128)} %copy-done.2, f32[8,32,128]{2,1,0:T(8,128)} %copy-done.3, ...), custom_call_target="tpu_custom_call", output_to_operand_aliasing={{}: (5, {})} | custom-call | tf_op jit(solution)/shard_map/pallas_call | solution.py:244
  (2 shorter events, 0.0 us)
Async XLA Ops:
  10.0 18.3 %collective-permute-start = (f32[8,2,64,128]{3,2,1,0:T(8,128)}, f32[8,2,64,128]{3,2,1,0:T(8,128)S(1)}, u32[]{:S(2)}, u32[]{:S(2)}) collective-permute-start(f32[8,2,64,128]{3,2,1,0:T(8,128)} %get-tuple-element.10), channel_id=1, source_target_pairs={{0,8},{8,0},{16,24},{24,16},{32,40},{40,32},{48,56},{56,48},{64,72... | collective-permute-start | bytes 1572872 | tf_op jit(solution)/shard_map/ppermute | solution.py:285
  10.1 18.3 %collective-permute-start.1 = (f32[8,2,64,128]{3,2,1,0:T(8,128)}, f32[8,2,64,128]{3,2,1,0:T(8,128)S(1)}, u32[]{:S(2)}, u32[]{:S(2)}) collective-permute-start(f32[8,2,64,128]{3,2,1,0:T(8,128)} %get-tuple-element.11), channel_id=1, source_target_pairs={{8,16},{16,8},{24,32},{32,24},{40,48},{48,40},{56,64},{64,56},{72,... | collective-permute-start | bytes 1572872 | tf_op jit(solution)/shard_map/ppermute | solution.py:286
  18.7 9.7 %collective-permute-start.2 = (f32[8,32,128]{2,1,0:T(8,128)}, f32[8,32,128]{2,1,0:T(8,128)S(1)}, u32[]{:S(2)}, u32[]{:S(2)}) collective-permute-start(f32[8,32,128]{2,1,0:T(8,128)} %get-tuple-element.12), channel_id=1, source_target_pairs={{0,1},{1,0},{2,3},{3,2},{4,5},{5,4},{6,7},{7,6},{8,9},{9,8},{10,11... | collective-permute-start | bytes 393224 | tf_op jit(solution)/shard_map/ppermute | solution.py:288
  19.3 9.0 %collective-permute-start.3 = (f32[8,32,128]{2,1,0:T(8,128)}, f32[8,32,128]{2,1,0:T(8,128)S(1)}, u32[]{:S(2)}, u32[]{:S(2)}) collective-permute-start(f32[8,32,128]{2,1,0:T(8,128)} %get-tuple-element.13), channel_id=1, source_target_pairs={{1,2},{2,1},{3,4},{4,3},{5,6},{6,5},{9,10},{10,9},{11,12},{12,11},... | collective-permute-start | bytes 393224 | tf_op jit(solution)/shard_map/ppermute | solution.py:289
  28.3 0.6 %copy-start.2 = (f32[8,32,128]{2,1,0:T(8,128)}, f32[8,32,128]{2,1,0:T(8,128)S(1)}, u32[]{:S(2)}) copy-start(f32[8,32,128]{2,1,0:T(8,128)S(1)} %collective-permute-done.2.lat_mate_hbm) | copy-start | bytes 393220
  28.3 0.7 %copy-start.3 = (f32[8,32,128]{2,1,0:T(8,128)}, f32[8,32,128]{2,1,0:T(8,128)S(1)}, u32[]{:S(2)}) copy-start(f32[8,32,128]{2,1,0:T(8,128)S(1)} %collective-permute-done.3.lat_far_hbm) | copy-start | bytes 393220
  28.3 0.9 %copy-start = (f32[8,2,64,128]{3,2,1,0:T(8,128)}, f32[8,2,64,128]{3,2,1,0:T(8,128)S(1)}, u32[]{:S(2)}) copy-start(f32[8,2,64,128]{3,2,1,0:T(8,128)S(1)} %collective-permute-done.lon_mate_hbm) | copy-start | bytes 1572868
  29.2 0.8 %copy-start.1 = (f32[8,2,64,128]{3,2,1,0:T(8,128)}, f32[8,2,64,128]{3,2,1,0:T(8,128)S(1)}, u32[]{:S(2)}) copy-start(f32[8,2,64,128]{3,2,1,0:T(8,128)S(1)} %collective-permute-done.1.lon_far_hbm) | copy-start | bytes 1572868

commit v11 on v10

--- a/solution.py
+++ b/solution.py
@@ -57,7 +57,7 @@
     return jnp.transpose(cloudy.reshape(nlon // rows, rows, nlat), (0, 2, 1))
 
 
-def sat_kernel(parity_ref, traj_ref, cot_ref, kind_ref, mask_ref, cour_ref,
+def sat_kernel(traj_ref, cot_ref, kind_ref, mask_ref, cour_ref,
                out_ref, lon_mate, lon_far, lat_mate, lat_far):
     fields, rows, nlat, lev = cot_ref.shape
     step = pl.program_id(0)
@@ -83,13 +83,13 @@
                 after[f][j] = cot_ref[f, r, lat, :]
         low_weight = cour_ref[1, r, 0:2, :]
         high_weight = cour_ref[1, r, nlat - 2:nlat, :]
-        lat_even = parity_ref[1] == 0
+        lat_even = lax.axis_index("lat") % 2 == 0
         for f in range(fields):
             bottom = low_weight * after[f][0][0:2]
             top = high_weight * after[f][parts - 1][chunk - 2:chunk]
             lat_mate[f, 2 * r:2 * r + 2, :] = jnp.where(lat_even, top, bottom)
             lat_far[f, 2 * r:2 * r + 2, :] = jnp.where(lat_even, bottom, top)
-        lon_even = parity_ref[0] == 0
+        lon_even = lax.axis_index("lon") % 2 == 0
         for edge_step, edge_rows, mate_when in ((0, range(2), jnp.logical_not(lon_even)), (last, range(rows - 2, rows), lon_even)):
             if r not in edge_rows:
                 continue
@@ -103,7 +103,7 @@
                             target[f, at, lat, :] = cour_ref[0, r, lat, :] * after[f][j]
 
 
-def first_pair(parity, trajectory, cotangent, branch, mask, courant, rows):
+def first_pair(trajectory, cotangent, branch, mask, courant, rows):
     fields, nlon, nlat, lev = cotangent.shape
     lon_send = jax.ShapeDtypeStruct((fields, 2, nlat, lev), jnp.float32)
     lat_send = jax.ShapeDtypeStruct((fields, 2 * nlon, lev), jnp.float32)
@@ -111,7 +111,6 @@
         sat_kernel,
         grid=(nlon // rows,),
         in_specs=[
-            pl.BlockSpec(memory_space=pltpu.SMEM),
             pl.BlockSpec((2, rows, nlat, lev), lambda i: (0, i, 0, 0)),
             pl.BlockSpec((fields, rows, nlat, lev), lambda i: (0, i, 0, 0)),
             pl.BlockSpec((rows, nlat, lev), lambda i: (i, 0, 0)),
@@ -126,7 +125,7 @@
             pl.BlockSpec((fields, 2 * rows, lev), lambda i: (0, i, 0)),
         ],
         out_shape=[jax.ShapeDtypeStruct((2, nlon, nlat, lev), jnp.float32), lon_send, lon_send, lat_send, lat_send],
-    )(parity, trajectory, cotangent, branch, mask, courant)
+    )(trajectory, cotangent, branch, mask, courant)
 
 
 def stencil_kernel(first_hbm, cot_hbm, cour_hbm, out_hbm, field_v, cour_v, out_v, lon_pad, lat_pad, in_sems, out_sems):
@@ -186,12 +185,12 @@
     )(first, cotangent, courant)
 
 
-def halo_kernel(parity_ref, lon_mate_hbm, lon_far_hbm, lat_mate_hbm, lat_far_hbm, out_hbm, out_ref,
+def halo_kernel(lon_mate_hbm, lon_far_hbm, lat_mate_hbm, lat_far_hbm, out_hbm, out_ref,
                 lon_mate, lon_far, lat_mate, lat_far, lon_lo_buf, lon_hi_buf, lat_lo_buf, lat_hi_buf, sems):
     fields, nlon, nlat, lev = out_hbm.shape
     halos = [(lon_mate_hbm, lon_mate), (lon_far_hbm, lon_far), (lat_mate_hbm, lat_mate), (lat_far_hbm, lat_far)]
-    lon_even = parity_ref[0] == 0
-    lat_even = parity_ref[1] == 0
+    lon_even = lax.axis_index("lon") % 2 == 0
+    lat_even = lax.axis_index("lat") % 2 == 0
     regions = [
         (out_hbm.at[:, 0:2], lon_lo_buf),
         (out_hbm.at[:, nlon - 2:nlon], lon_hi_buf),
@@ -238,12 +237,12 @@
         c.wait()
 
 
-def add_halos(parity, out, lon_low, lon_high, lat_low, lat_high):
+def add_halos(out, lon_low, lon_high, lat_low, lat_high):
     fields, nlon, nlat, lev = out.shape
     hbm = pl.BlockSpec(memory_space=pl.ANY)
     return pl.pallas_call(
         halo_kernel,
-        in_specs=[pl.BlockSpec(memory_space=pltpu.SMEM)] + [hbm] * 5,
+        in_specs=[hbm] * 5,
         out_specs=hbm,
         out_shape=jax.ShapeDtypeStruct(out.shape, jnp.float32),
         scratch_shapes=[
@@ -257,8 +256,8 @@
             pltpu.VMEM((fields, nlon - 4, 8, lev), jnp.float32),
             pltpu.SemaphoreType.DMA((8,)),
         ],
-        input_output_aliases={5: 0},
-    )(parity, lon_low, lon_high, lat_low, lat_high, out)
+        input_output_aliases={4: 0},
+    )(lon_low, lon_high, lat_low, lat_high, out)
 
 
 def pairings(axis, periodic):
@@ -278,9 +277,8 @@
 def on_device(trajectory, cotangent, courant, branch, cloud_list, cloud_count):
     fields, nlon, nlat, lev = cotangent.shape
     rows = 8
-    parity = jnp.stack([lax.axis_index("lon") % 2, lax.axis_index("lat") % 2]).astype(jnp.int32)
     mask = cloudy_columns(cloud_list, cloud_count, nlon, nlat, rows)
-    first, lon_mate, lon_far, lat_mate, lat_far = first_pair(parity, trajectory, cotangent, branch, mask, courant, rows)
+    first, lon_mate, lon_far, lat_mate, lat_far = first_pair(trajectory, cotangent, branch, mask, courant, rows)
     mate, far = pairings("lon", True)
     lon_mate = lax.ppermute(lon_mate, "lon", mate)
     lon_far = lax.ppermute(lon_far, "lon", far)
@@ -288,7 +286,7 @@
     lat_mate = lax.ppermute(lat_mate, "lat", mate)
     lat_far = lax.ppermute(lat_far, "lat", far)
     out = advect(first, cotangent, courant)
-    return add_halos(parity, out, lon_mate, lon_far, lat_mate, lat_far)
+    return add_halos(out, lon_mate, lon_far, lat_mate, lat_far)
 
 
 def solution(mesh):

time: 34.2 us -> 32.8 us (0.959)
  Pallas kernels: 15.9 us -> 15.2 us
  other arithmetic: 1.85 us -> 1.2 us
    pallas_call x2, Pallas kernels: 10.7 us -> 9.99 us  [the longest x1 6.66 us: first_pair(): pl.pallas_call(sat_kernel, grid=(nlon // rows,), in_specs=[pl.BlockSpec((...]
    another operation x1 -> x0, other arithmetic: 0.66 us -> none  [on_device(): jnp.stack([lax.axis_index('lon') % 2, lax.axis_index('lat') % 2])]
  transfers between devices with their start and end apart: 4 -> 4, of which waited for: 1 -> 1; matrix products, arithmetic and copies ran while one was open for 0% -> 0% of each run, Pallas kernels for 15% -> 16%
where the time goes in v11:
time: 32.8 us; the launch traced here: 32.7 us
  Pallas kernels  15.2 us (46%)
  starting transfers between devices  12.5 us (38%)
  local copies, waits for them, and re-layouts  2.42 us (7%)
  other arithmetic  1.2 us (4%)
  between operations  0.71 us (2%)
  waiting for transfers between devices  0.63 us (2%)
    ppermute x1, starting transfers between devices, on_device(): lon_far = lax.ppermute(lon_far, 'lon', far)  8.59 us
    pallas_call x1, Pallas kernels, first_pair(): pl.pallas_call(sat_kernel, grid=(nlon // rows,), in_specs=[pl.BlockSpec((...  6.66 us
    pallas_call x1, Pallas kernels, advect(): pl.pallas_call(stencil_kernel, in_specs=[hbm, hbm, hbm], out_specs=hbm, o...  5.18 us
    pallas_call x1, Pallas kernels, add_halos(): pl.pallas_call(halo_kernel, in_specs=[hbm] * 5, out_specs=hbm, out_shape=...  3.33 us
    ppermute x1, starting transfers between devices, on_device(): lat_far = lax.ppermute(lat_far, 'lat', far)  3.22 us
    unnamed x8, local copies, waits for them, and re-layouts  1.62 us
    transpose x2, local copies, waits for them, and re-layouts, cloudy_columns(): return jnp.transpose(cloudy.reshape(nlon // rows, rows, nlat), (0, 2, 1))  0.8 us
    unnamed x1, other arithmetic  0.7 us
  transfers between devices with their start and end apart: 4, of which 1 were waited for; matrix products, arithmetic and copies ran while one was open for 0% of the time, Pallas kernels for 16%

profile of v11, /device:TPU:2, one launch (start us, length us, event | category | flops | bytes accessed | tf_op | source)
XLA Modules:
  0.0 32.7 jit_solution(13979819667103635890)
XLA Ops:
  0.7 0.7 %reduce = s32[768]{0:T(1024)S(1)} reduce(s32[1,1,768]{2,1,0:T(1,128)} %param.10, s32[]{:T(128)} %constant.8), dimensions={0,1}, to_apply=%param.10.reduce_sub_computation | reduce | bytes 6148 | tf_op args[4]
  1.4 0.5 %fusion.1 = pred[1024]{0:T(1024)(128)(4,1)S(1)} fusion(s32[768]{0:T(1024)S(1)} %reduce, pred[768]{0:T(1024)(128)(4,1)S(1)} %iota_compare_fusion.1), kind=kLoop, calls=%fused_computation.2 | loop fusion | flops 2358272 | bytes 4864 | tf_op jit(solution)/shard_map/reduce_or | solution.py:56
  1.9 0.1 reshape.9
  1.9 0.7 %copy.9 = f32[2,8,64]{1,2,0:T(8,128)} copy(f32[2,8,64]{2,1,0:T(8,128)S(1)} %reshape.9) | data formatting | bytes 8192 | tf_op jit(solution)/shard_map/transpose | solution.py:57
  2.7 6.7 %shard_map.64 = (f32[2,16,64,128]{3,2,1,0:T(8,128)}, f32[8,2,64,128]{3,2,1,0:T(8,128)}, f32[8,2,64,128]{3,2,1,0:T(8,128)}, f32[8,32,128]{2,1,0:T(8,128)}, f32[8,32,128]{2,1,0:T(8,128)}) custom-call(f32[2,16,64,128]{3,2,1,0:T(8,128)} %traj_ref.1, f32[8,16,64,128]{3,2,1,0:T(8,128)} %cot_hbm.1, s32[16,64,128]{2,1,0:T(8,128)} %kind_ref.1, f32[2,64,8]{2,1,0:T(8,128)} %bitcast.3, ...), custom_call_target="tpu_custom_call" | custom-call | tf_op jit(solution)/shard_map/pallas_call | solution.py:110
  9.3 0.0 collective-permute-start
  9.4 8.6 %collective-permute-start.1 = (f32[8,2,64,128]{3,2,1,0:T(8,128)}, f32[8,2,64,128]{3,2,1,0:T(8,128)S(1)}, u32[]{:S(2)}, u32[]{:S(2)}) collective-permute-start(f32[8,2,64,128]{3,2,1,0:T(8,128)} %get-tuple-element.11), channel_id=1, source_target_pairs={{8,16},{16,8},{24,32},{32,24},{40,48},{48,40},{56,64},{64,56},{72,... | collective-permute-start | bytes 1572872 | tf_op jit(solution)/shard_map/ppermute | solution.py:284
  18.0 0.7 %collective-permute-start.2 = (f32[8,32,128]{2,1,0:T(8,128)}, f32[8,32,128]{2,1,0:T(8,128)S(1)}, u32[]{:S(2)}, u32[]{:S(2)}) collective-permute-start(f32[8,32,128]{2,1,0:T(8,128)} %get-tuple-element.12), channel_id=1, source_target_pairs={{0,1},{1,0},{2,3},{3,2},{4,5},{5,4},{6,7},{7,6},{8,9},{9,8},{10,11... | collective-permute-start | bytes 393224 | tf_op jit(solution)/shard_map/ppermute | solution.py:286
  18.6 3.2 %collective-permute-start.3 = (f32[8,32,128]{2,1,0:T(8,128)}, f32[8,32,128]{2,1,0:T(8,128)S(1)}, u32[]{:S(2)}, u32[]{:S(2)}) collective-permute-start(f32[8,32,128]{2,1,0:T(8,128)} %get-tuple-element.13), channel_id=1, source_target_pairs={{1,2},{2,1},{3,4},{4,3},{5,6},{6,5},{9,10},{10,9},{11,12},{12,11},... | collective-permute-start | bytes 393224 | tf_op jit(solution)/shard_map/ppermute | solution.py:287
  21.9 5.2 %shard_map.65.out_hbm = f32[8,16,64,128]{3,2,1,0:T(8,128)} custom-call(f32[2,16,64,128]{3,2,1,0:T(8,128)} %get-tuple-element.14.first_hbm, f32[8,16,64,128]{3,2,1,0:T(8,128)} %cot_hbm.1, f32[2,16,64,128]{3,2,1,0:T(8,128)} %cour_hbm.1), custom_call_target="tpu_custom_call" | custom-call | flops 12582912 | bytes 12582912 | tf_op jit(solution)/shard_map/pallas_call | solution.py:170
  27.1 0.6 %collective-permute-done.2.lat_mate_hbm = f32[8,32,128]{2,1,0:T(8,128)S(1)} collective-permute-done((f32[8,32,128]{2,1,0:T(8,128)}, f32[8,32,128]{2,1,0:T(8,128)S(1)}, u32[]{:S(2)}, u32[]{:S(2)}) %collective-permute-start.2) | collective-permute-done | bytes 131104 | tf_op jit(solution)/shard_map/ppermute | solution.py:286
  27.6 0.0 copy-start.2
  27.6 0.0 collective-permute-done.3.lat_far_hbm
  27.6 0.0 copy-start.3
  27.6 0.0 collective-permute-done.lon_mate_hbm
  27.6 0.0 copy-start
  27.7 0.0 collective-permute-done.1.lon_far_hbm
  27.7 0.6 %copy-done.2 = f32[8,32,128]{2,1,0:T(8,128)} copy-done((f32[8,32,128]{2,1,0:T(8,128)}, f32[8,32,128]{2,1,0:T(8,128)S(1)}, u32[]{:S(2)}) %copy-start.2) | copy-done | bytes 131096
  28.3 0.1 copy-done.3
  28.4 0.2 copy-done
  28.5 0.0 copy-start.1
  28.5 0.8 %copy-done.1 = f32[8,2,64,128]{3,2,1,0:T(8,128)} copy-done((f32[8,2,64,128]{3,2,1,0:T(8,128)}, f32[8,2,64,128]{3,2,1,0:T(8,128)S(1)}, u32[]{:S(2)}) %copy-start.1) | copy-done | bytes 524312
  29.3 3.3 %shard_map.66 = f32[8,16,64,128]{3,2,1,0:T(8,128)} custom-call(f32[8,2,64,128]{3,2,1,0:T(8,128)} %copy-done, f32[8,2,64,128]{3,2,1,0:T(8,128)} %copy-done.1, f32[8,32,128]{2,1,0:T(8,128)} %copy-done.2, f32[8,32,128]{2,1,0:T(8,128)} %copy-done.3, f32[8,16,64,128]{3,2,1,0:T(8,128)} %shard_map.65.out_hbm), custom_call_target="tpu_custom_call", output_to_operand_aliasing={{}: (4, {})} | custom-call | tf_op jit(solution)/shard_map/pallas_call | solution.py:243
  (2 shorter events, 0.0 us)
Async XLA Ops:
  9.3 18.3 %collective-permute-start = (f32[8,2,64,128]{3,2,1,0:T(8,128)}, f32[8,2,64,128]{3,2,1,0:T(8,128)S(1)}, u32[]{:S(2)}, u32[]{:S(2)}) collective-permute-start(f32[8,2,64,128]{3,2,1,0:T(8,128)} %get-tuple-element.10), channel_id=1, source_target_pairs={{0,8},{8,0},{16,24},{24,16},{32,40},{40,32},{48,56},{56,48},{64,72... | collective-permute-start | bytes 1572872 | tf_op jit(solution)/shard_map/ppermute | solution.py:283
  9.4 18.3 %collective-permute-start.1 = (f32[8,2,64,128]{3,2,1,0:T(8,128)}, f32[8,2,64,128]{3,2,1,0:T(8,128)S(1)}, u32[]{:S(2)}, u32[]{:S(2)}) collective-permute-start(f32[8,2,64,128]{3,2,1,0:T(8,128)} %get-tuple-element.11), channel_id=1, source_target_pairs={{8,16},{16,8},{24,32},{32,24},{40,48},{48,40},{56,64},{64,56},{72,... | collective-permute-start | bytes 1572872 | tf_op jit(solution)/shard_map/ppermute | solution.py:284
  18.0 9.7 %collective-permute-start.2 = (f32[8,32,128]{2,1,0:T(8,128)}, f32[8,32,128]{2,1,0:T(8,128)S(1)}, u32[]{:S(2)}, u32[]{:S(2)}) collective-permute-start(f32[8,32,128]{2,1,0:T(8,128)} %get-tuple-element.12), channel_id=1, source_target_pairs={{0,1},{1,0},{2,3},{3,2},{4,5},{5,4},{6,7},{7,6},{8,9},{9,8},{10,11... | collective-permute-start | bytes 393224 | tf_op jit(solution)/shard_map/ppermute | solution.py:286
  18.6 9.0 %collective-permute-start.3 = (f32[8,32,128]{2,1,0:T(8,128)}, f32[8,32,128]{2,1,0:T(8,128)S(1)}, u32[]{:S(2)}, u32[]{:S(2)}) collective-permute-start(f32[8,32,128]{2,1,0:T(8,128)} %get-tuple-element.13), channel_id=1, source_target_pairs={{1,2},{2,1},{3,4},{4,3},{5,6},{6,5},{9,10},{10,9},{11,12},{12,11},... | collective-permute-start | bytes 393224 | tf_op jit(solution)/shard_map/ppermute | solution.py:287
  27.6 0.6 %copy-start.2 = (f32[8,32,128]{2,1,0:T(8,128)}, f32[8,32,128]{2,1,0:T(8,128)S(1)}, u32[]{:S(2)}) copy-start(f32[8,32,128]{2,1,0:T(8,128)S(1)} %collective-permute-done.2.lat_mate_hbm) | copy-start | bytes 393220
  27.6 0.7 %copy-start.3 = (f32[8,32,128]{2,1,0:T(8,128)}, f32[8,32,128]{2,1,0:T(8,128)S(1)}, u32[]{:S(2)}) copy-start(f32[8,32,128]{2,1,0:T(8,128)S(1)} %collective-permute-done.3.lat_far_hbm) | copy-start | bytes 393220
  27.6 0.9 %copy-start = (f32[8,2,64,128]{3,2,1,0:T(8,128)}, f32[8,2,64,128]{3,2,1,0:T(8,128)S(1)}, u32[]{:S(2)}) copy-start(f32[8,2,64,128]{3,2,1,0:T(8,128)S(1)} %collective-permute-done.lon_mate_hbm) | copy-start | bytes 1572868
  28.5 0.8 %copy-start.1 = (f32[8,2,64,128]{3,2,1,0:T(8,128)}, f32[8,2,64,128]{3,2,1,0:T(8,128)S(1)}, u32[]{:S(2)}) copy-start(f32[8,2,64,128]{3,2,1,0:T(8,128)S(1)} %collective-permute-done.1.lon_far_hbm) | copy-start | bytes 1572868

commit v12 on v11

--- a/solution.py
+++ b/solution.py
@@ -53,7 +53,7 @@
     count = cloud_count[0, 0]
     slot = jnp.arange(index.shape[0], dtype=jnp.int32)
     hit = (index[:, None] == jnp.arange(nlon * nlat, dtype=jnp.int32)[None, :]) & (slot < count)[:, None]
-    cloudy = jnp.any(hit, axis=0).astype(jnp.float32)
+    cloudy = jnp.max(jnp.where(hit, 1.0, 0.0), axis=0)
     return jnp.transpose(cloudy.reshape(nlon // rows, rows, nlat), (0, 2, 1))
 
 

time: 32.8 us -> 33 us (level)
    transpose x2 -> x0, local copies, waits for them, and re-layouts: 0.8 us -> none  [cloudy_columns(): return jnp.transpose(cloudy.reshape(nlon // rows, rows, nlat), (0, 2, 1))]
    reshape x0 -> x2, local copies, waits for them, and re-layouts: none -> 0.8 us  [cloudy_columns(): return jnp.transpose(cloudy.reshape(nlon // rows, rows, nlat), (0, 2, 1))]
    reduce_max x0 -> x1, other arithmetic: none -> 0.68 us  [cloudy_columns(): cloudy = jnp.max(jnp.where(hit, 1.0, 0.0), axis=0)]
    reduce_or x1 -> x0, other arithmetic: 0.49 us -> none  [cloudy_columns(): cloudy = jnp.any(hit, axis=0).astype(jnp.float32)]
where the time goes in v12:
time: 33 us; the launch traced here: 32.8 us
  Pallas kernels  15.2 us (46%)
  starting transfers between devices  12.5 us (38%)
  local copies, waits for them, and re-layouts  2.42 us (7%)
  other arithmetic  1.39 us (4%)
  between operations  0.71 us (2%)
  waiting for transfers between devices  0.63 us (2%)
    ppermute x1, starting transfers between devices, on_device(): lon_far = lax.ppermute(lon_far, 'lon', far)  8.59 us
    pallas_call x1, Pallas kernels, first_pair(): pl.pallas_call(sat_kernel, grid=(nlon // rows,), in_specs=[pl.BlockSpec((...  6.66 us
    pallas_call x1, Pallas kernels, advect(): pl.pallas_call(stencil_kernel, in_specs=[hbm, hbm, hbm], out_specs=hbm, o...  5.18 us
    pallas_call x1, Pallas kernels, add_halos(): pl.pallas_call(halo_kernel, in_specs=[hbm] * 5, out_specs=hbm, out_shape=...  3.33 us
    ppermute x1, starting transfers between devices, on_device(): lat_far = lax.ppermute(lat_far, 'lat', far)  3.22 us
    unnamed x8, local copies, waits for them, and re-layouts  1.62 us
    reshape x2, local copies, waits for them, and re-layouts, cloudy_columns(): return jnp.transpose(cloudy.reshape(nlon // rows, rows, nlat), (0, 2, 1))  0.8 us
    unnamed x1, other arithmetic  0.7 us
  transfers between devices with their start and end apart: 4, of which 1 were waited for; matrix products, arithmetic and copies ran while one was open for 0% of the time, Pallas kernels for 16%

profile of v12, /device:TPU:2, one launch (start us, length us, event | category | flops | bytes accessed | tf_op | source)
XLA Modules:
  0.0 32.8 jit_solution(5218714089641173015)
XLA Ops:
  0.7 0.7 %reduce = s32[768]{0:T(1024)S(1)} reduce(s32[1,1,768]{2,1,0:T(1,128)} %param.10, s32[]{:T(128)} %constant.12), dimensions={0,1}, to_apply=%param.10.reduce_sub_computation | reduce | bytes 6148 | tf_op args[4]
  1.4 0.7 %select_reduce_fusion = f32[1024]{0:T(1024)S(1)} fusion(s32[768]{0:T(1024)S(1)} %reduce, pred[768]{0:T(1024)(128)(4,1)S(1)} %iota_compare_fusion.1), kind=kLoop, calls=%fused_computation | loop fusion | flops 3144704 | bytes 7936 | tf_op jit(solution)/shard_map/reduce_max | solution.py:56
  2.1 0.1 reshape.8
  2.1 0.7 %copy.9 = f32[2,8,64]{1,2,0:T(8,128)} copy(f32[2,8,64]{2,1,0:T(8,128)S(1)} %reshape.8) | data formatting | bytes 8192 | tf_op jit(solution)/shard_map/reshape | solution.py:57
  2.9 6.7 %shard_map.64 = (f32[2,16,64,128]{3,2,1,0:T(8,128)}, f32[8,2,64,128]{3,2,1,0:T(8,128)}, f32[8,2,64,128]{3,2,1,0:T(8,128)}, f32[8,32,128]{2,1,0:T(8,128)}, f32[8,32,128]{2,1,0:T(8,128)}) custom-call(f32[2,16,64,128]{3,2,1,0:T(8,128)} %traj_ref.1, f32[8,16,64,128]{3,2,1,0:T(8,128)} %cot_hbm.1, s32[16,64,128]{2,1,0:T(8,128)} %kind_ref.1, f32[2,64,8]{2,1,0:T(8,128)} %bitcast.3, ...), custom_call_target="tpu_custom_call" | custom-call | tf_op jit(solution)/shard_map/pallas_call | solution.py:110
  9.5 0.0 collective-permute-start
  9.6 8.6 %collective-permute-start.1 = (f32[8,2,64,128]{3,2,1,0:T(8,128)}, f32[8,2,64,128]{3,2,1,0:T(8,128)S(1)}, u32[]{:S(2)}, u32[]{:S(2)}) collective-permute-start(f32[8,2,64,128]{3,2,1,0:T(8,128)} %get-tuple-element.11), channel_id=1, source_target_pairs={{8,16},{16,8},{24,32},{32,24},{40,48},{48,40},{56,64},{64,56},{72,... | collective-permute-start | bytes 1572872 | tf_op jit(solution)/shard_map/ppermute | solution.py:284
  18.2 0.7 %collective-permute-start.2 = (f32[8,32,128]{2,1,0:T(8,128)}, f32[8,32,128]{2,1,0:T(8,128)S(1)}, u32[]{:S(2)}, u32[]{:S(2)}) collective-permute-start(f32[8,32,128]{2,1,0:T(8,128)} %get-tuple-element.12), channel_id=1, source_target_pairs={{0,1},{1,0},{2,3},{3,2},{4,5},{5,4},{6,7},{7,6},{8,9},{9,8},{10,11... | collective-permute-start | bytes 393224 | tf_op jit(solution)/shard_map/ppermute | solution.py:286
  18.8 3.2 %collective-permute-start.3 = (f32[8,32,128]{2,1,0:T(8,128)}, f32[8,32,128]{2,1,0:T(8,128)S(1)}, u32[]{:S(2)}, u32[]{:S(2)}) collective-permute-start(f32[8,32,128]{2,1,0:T(8,128)} %get-tuple-element.13), channel_id=1, source_target_pairs={{1,2},{2,1},{3,4},{4,3},{5,6},{6,5},{9,10},{10,9},{11,12},{12,11},... | collective-permute-start | bytes 393224 | tf_op jit(solution)/shard_map/ppermute | solution.py:287
  22.1 5.2 %shard_map.65.out_hbm = f32[8,16,64,128]{3,2,1,0:T(8,128)} custom-call(f32[2,16,64,128]{3,2,1,0:T(8,128)} %get-tuple-element.14.first_hbm, f32[8,16,64,128]{3,2,1,0:T(8,128)} %cot_hbm.1, f32[2,16,64,128]{3,2,1,0:T(8,128)} %cour_hbm.1), custom_call_target="tpu_custom_call" | custom-call | flops 12582912 | bytes 12582912 | tf_op jit(solution)/shard_map/pallas_call | solution.py:170
  27.2 0.6 %collective-permute-done.2.lat_mate_hbm = f32[8,32,128]{2,1,0:T(8,128)S(1)} collective-permute-done((f32[8,32,128]{2,1,0:T(8,128)}, f32[8,32,128]{2,1,0:T(8,128)S(1)}, u32[]{:S(2)}, u32[]{:S(2)}) %collective-permute-start.2) | collective-permute-done | bytes 131104 | tf_op jit(solution)/shard_map/ppermute | solution.py:286
  27.8 0.0 copy-start.2
  27.8 0.0 collective-permute-done.3.lat_far_hbm
  27.8 0.0 copy-start.3
  27.8 0.0 collective-permute-done.lon_mate_hbm
  27.8 0.0 copy-start
  27.8 0.0 collective-permute-done.1.lon_far_hbm
  27.9 0.6 %copy-done.2 = f32[8,32,128]{2,1,0:T(8,128)} copy-done((f32[8,32,128]{2,1,0:T(8,128)}, f32[8,32,128]{2,1,0:T(8,128)S(1)}, u32[]{:S(2)}) %copy-start.2) | copy-done | bytes 131096
  28.5 0.1 copy-done.3
  28.5 0.2 copy-done
  28.7 0.0 copy-start.1
  28.7 0.8 %copy-done.1 = f32[8,2,64,128]{3,2,1,0:T(8,128)} copy-done((f32[8,2,64,128]{3,2,1,0:T(8,128)}, f32[8,2,64,128]{3,2,1,0:T(8,128)S(1)}, u32[]{:S(2)}) %copy-start.1) | copy-done | bytes 524312
  29.5 3.3 %shard_map.66 = f32[8,16,64,128]{3,2,1,0:T(8,128)} custom-call(f32[8,2,64,128]{3,2,1,0:T(8,128)} %copy-done, f32[8,2,64,128]{3,2,1,0:T(8,128)} %copy-done.1, f32[8,32,128]{2,1,0:T(8,128)} %copy-done.2, f32[8,32,128]{2,1,0:T(8,128)} %copy-done.3, f32[8,16,64,128]{3,2,1,0:T(8,128)} %shard_map.65.out_hbm), custom_call_target="tpu_custom_call", output_to_operand_aliasing={{}: (4, {})} | custom-call | tf_op jit(solution)/shard_map/pallas_call | solution.py:243
  (1 shorter events, 0.0 us)
Async XLA Ops:
  9.5 18.3 %collective-permute-start = (f32[8,2,64,128]{3,2,1,0:T(8,128)}, f32[8,2,64,128]{3,2,1,0:T(8,128)S(1)}, u32[]{:S(2)}, u32[]{:S(2)}) collective-permute-start(f32[8,2,64,128]{3,2,1,0:T(8,128)} %get-tuple-element.10), channel_id=1, source_target_pairs={{0,8},{8,0},{16,24},{24,16},{32,40},{40,32},{48,56},{56,48},{64,72... | collective-permute-start | bytes 1572872 | tf_op jit(solution)/shard_map/ppermute | solution.py:283
  9.6 18.3 %collective-permute-start.1 = (f32[8,2,64,128]{3,2,1,0:T(8,128)}, f32[8,2,64,128]{3,2,1,0:T(8,128)S(1)}, u32[]{:S(2)}, u32[]{:S(2)}) collective-permute-start(f32[8,2,64,128]{3,2,1,0:T(8,128)} %get-tuple-element.11), channel_id=1, source_target_pairs={{8,16},{16,8},{24,32},{32,24},{40,48},{48,40},{56,64},{64,56},{72,... | collective-permute-start | bytes 1572872 | tf_op jit(solution)/shard_map/ppermute | solution.py:284
  18.2 9.7 %collective-permute-start.2 = (f32[8,32,128]{2,1,0:T(8,128)}, f32[8,32,128]{2,1,0:T(8,128)S(1)}, u32[]{:S(2)}, u32[]{:S(2)}) collective-permute-start(f32[8,32,128]{2,1,0:T(8,128)} %get-tuple-element.12), channel_id=1, source_target_pairs={{0,1},{1,0},{2,3},{3,2},{4,5},{5,4},{6,7},{7,6},{8,9},{9,8},{10,11... | collective-permute-start | bytes 393224 | tf_op jit(solution)/shard_map/ppermute | solution.py:286
  18.8 9.0 %collective-permute-start.3 = (f32[8,32,128]{2,1,0:T(8,128)}, f32[8,32,128]{2,1,0:T(8,128)S(1)}, u32[]{:S(2)}, u32[]{:S(2)}) collective-permute-start(f32[8,32,128]{2,1,0:T(8,128)} %get-tuple-element.13), channel_id=1, source_target_pairs={{1,2},{2,1},{3,4},{4,3},{5,6},{6,5},{9,10},{10,9},{11,12},{12,11},... | collective-permute-start | bytes 393224 | tf_op jit(solution)/shard_map/ppermute | solution.py:287
  27.8 0.6 %copy-start.2 = (f32[8,32,128]{2,1,0:T(8,128)}, f32[8,32,128]{2,1,0:T(8,128)S(1)}, u32[]{:S(2)}) copy-start(f32[8,32,128]{2,1,0:T(8,128)S(1)} %collective-permute-done.2.lat_mate_hbm) | copy-start | bytes 393220
  27.8 0.7 %copy-start.3 = (f32[8,32,128]{2,1,0:T(8,128)}, f32[8,32,128]{2,1,0:T(8,128)S(1)}, u32[]{:S(2)}) copy-start(f32[8,32,128]{2,1,0:T(8,128)S(1)} %collective-permute-done.3.lat_far_hbm) | copy-start | bytes 393220
  27.8 0.9 %copy-start = (f32[8,2,64,128]{3,2,1,0:T(8,128)}, f32[8,2,64,128]{3,2,1,0:T(8,128)S(1)}, u32[]{:S(2)}) copy-start(f32[8,2,64,128]{3,2,1,0:T(8,128)S(1)} %collective-permute-done.lon_mate_hbm) | copy-start | bytes 1572868
  28.7 0.8 %copy-start.1 = (f32[8,2,64,128]{3,2,1,0:T(8,128)}, f32[8,2,64,128]{3,2,1,0:T(8,128)S(1)}, u32[]{:S(2)}) copy-start(f32[8,2,64,128]{3,2,1,0:T(8,128)S(1)} %collective-permute-done.1.lon_far_hbm) | copy-start | bytes 1572868

commit v13 on v11

--- a/solution.py
+++ b/solution.py
@@ -206,17 +206,17 @@
 
     def lat_fix(tile, low_rows, high_rows, at_low):
         if at_low:
-            row0 = (low_rows[0:1] - 8.0 * low_rows[1:2]) / 12.0
-            row1 = low_rows[1:2] / 12.0
+            row0 = (low_rows[0:1] - 8.0 * low_rows[1:2]) * (1.0 / 12.0)
+            row1 = low_rows[1:2] * (1.0 / 12.0)
             return tile + jnp.where(sub == 0, row0, jnp.where(sub == 1, row1, 0.0))
-        row6 = -high_rows[0:1] / 12.0
-        row7 = (8.0 * high_rows[0:1] - high_rows[1:2]) / 12.0
+        row6 = -high_rows[0:1] * (1.0 / 12.0)
+        row7 = (8.0 * high_rows[0:1] - high_rows[1:2]) * (1.0 / 12.0)
         return tile + jnp.where(sub == 6, row6, jnp.where(sub == 7, row7, 0.0))
 
     for f in range(fields):
         lo = jnp.where(lon_even, lon_far[f], lon_mate[f])
         hi = jnp.where(lon_even, lon_mate[f], lon_far[f])
-        edge_terms = [(lo[0] - 8.0 * lo[1]) / 12.0, lo[1] / 12.0, -hi[0] / 12.0, (8.0 * hi[0] - hi[1]) / 12.0]
+        edge_terms = [(lo[0] - 8.0 * lo[1]) * (1.0 / 12.0), lo[1] * (1.0 / 12.0), -hi[0] * (1.0 / 12.0), (8.0 * hi[0] - hi[1]) * (1.0 / 12.0)]
         for k, r in enumerate((0, 1, nlon - 2, nlon - 1)):
             buf = lon_lo_buf if k < 2 else lon_hi_buf
             block = buf[f, k % 2] + edge_terms[k]

time: 32.8 us -> 32.8 us (level)
  no operation moved by 1% of the time
where the time goes in v13:
time: 32.8 us; the launch traced here: 32.7 us
  Pallas kernels  15.2 us (46%)
  starting transfers between devices  12.5 us (38%)
  local copies, waits for them, and re-layouts  2.42 us (7%)
  other arithmetic  1.2 us (4%)
  between operations  0.71 us (2%)
  waiting for transfers between devices  0.63 us (2%)
    ppermute x1, starting transfers between devices, on_device(): lon_far = lax.ppermute(lon_far, 'lon', far)  8.59 us
    pallas_call x1, Pallas kernels, first_pair(): pl.pallas_call(sat_kernel, grid=(nlon // rows,), in_specs=[pl.BlockSpec((...  6.66 us
    pallas_call x1, Pallas kernels, advect(): pl.pallas_call(stencil_kernel, in_specs=[hbm, hbm, hbm], out_specs=hbm, o...  5.18 us
    pallas_call x1, Pallas kernels, add_halos(): pl.pallas_call(halo_kernel, in_specs=[hbm] * 5, out_specs=hbm, out_shape=...  3.33 us
    ppermute x1, starting transfers between devices, on_device(): lat_far = lax.ppermute(lat_far, 'lat', far)  3.22 us
    unnamed x8, local copies, waits for them, and re-layouts  1.62 us
    transpose x2, local copies, waits for them, and re-layouts, cloudy_columns(): return jnp.transpose(cloudy.reshape(nlon // rows, rows, nlat), (0, 2, 1))  0.8 us
    unnamed x1, other arithmetic  0.7 us
  transfers between devices with their start and end apart: 4, of which 1 were waited for; matrix products, arithmetic and copies ran while one was open for 0% of the time, Pallas kernels for 16%

profile of v13, /device:TPU:2, one launch (start us, length us, event | category | flops | bytes accessed | tf_op | source)
XLA Modules:
  0.0 32.7 jit_solution(13979819667103635890)
XLA Ops:
  0.7 0.7 %reduce = s32[768]{0:T(1024)S(1)} reduce(s32[1,1,768]{2,1,0:T(1,128)} %param.10, s32[]{:T(128)} %constant.8), dimensions={0,1}, to_apply=%param.10.reduce_sub_computation | reduce | bytes 6148 | tf_op args[4]
  1.4 0.5 %fusion.1 = pred[1024]{0:T(1024)(128)(4,1)S(1)} fusion(s32[768]{0:T(1024)S(1)} %reduce, pred[768]{0:T(1024)(128)(4,1)S(1)} %iota_compare_fusion.1), kind=kLoop, calls=%fused_computation.2 | loop fusion | flops 2358272 | bytes 4864 | tf_op jit(solution)/shard_map/reduce_or | solution.py:56
  1.9 0.1 reshape.9
  1.9 0.7 %copy.9 = f32[2,8,64]{1,2,0:T(8,128)} copy(f32[2,8,64]{2,1,0:T(8,128)S(1)} %reshape.9) | data formatting | bytes 8192 | tf_op jit(solution)/shard_map/transpose | solution.py:57
  2.7 6.7 %shard_map.64 = (f32[2,16,64,128]{3,2,1,0:T(8,128)}, f32[8,2,64,128]{3,2,1,0:T(8,128)}, f32[8,2,64,128]{3,2,1,0:T(8,128)}, f32[8,32,128]{2,1,0:T(8,128)}, f32[8,32,128]{2,1,0:T(8,128)}) custom-call(f32[2,16,64,128]{3,2,1,0:T(8,128)} %traj_ref.1, f32[8,16,64,128]{3,2,1,0:T(8,128)} %cot_hbm.1, s32[16,64,128]{2,1,0:T(8,128)} %kind_ref.1, f32[2,64,8]{2,1,0:T(8,128)} %bitcast.3, ...), custom_call_target="tpu_custom_call" | custom-call | tf_op jit(solution)/shard_map/pallas_call | solution.py:110
  9.3 0.0 collective-permute-start
  9.4 8.6 %collective-permute-start.1 = (f32[8,2,64,128]{3,2,1,0:T(8,128)}, f32[8,2,64,128]{3,2,1,0:T(8,128)S(1)}, u32[]{:S(2)}, u32[]{:S(2)}) collective-permute-start(f32[8,2,64,128]{3,2,1,0:T(8,128)} %get-tuple-element.11), channel_id=1, source_target_pairs={{8,16},{16,8},{24,32},{32,24},{40,48},{48,40},{56,64},{64,56},{72,... | collective-permute-start | bytes 1572872 | tf_op jit(solution)/shard_map/ppermute | solution.py:284
  18.0 0.7 %collective-permute-start.2 = (f32[8,32,128]{2,1,0:T(8,128)}, f32[8,32,128]{2,1,0:T(8,128)S(1)}, u32[]{:S(2)}, u32[]{:S(2)}) collective-permute-start(f32[8,32,128]{2,1,0:T(8,128)} %get-tuple-element.12), channel_id=1, source_target_pairs={{0,1},{1,0},{2,3},{3,2},{4,5},{5,4},{6,7},{7,6},{8,9},{9,8},{10,11... | collective-permute-start | bytes 393224 | tf_op jit(solution)/shard_map/ppermute | solution.py:286
  18.6 3.2 %collective-permute-start.3 = (f32[8,32,128]{2,1,0:T(8,128)}, f32[8,32,128]{2,1,0:T(8,128)S(1)}, u32[]{:S(2)}, u32[]{:S(2)}) collective-permute-start(f32[8,32,128]{2,1,0:T(8,128)} %get-tuple-element.13), channel_id=1, source_target_pairs={{1,2},{2,1},{3,4},{4,3},{5,6},{6,5},{9,10},{10,9},{11,12},{12,11},... | collective-permute-start | bytes 393224 | tf_op jit(solution)/shard_map/ppermute | solution.py:287
  21.9 5.2 %shard_map.65.out_hbm = f32[8,16,64,128]{3,2,1,0:T(8,128)} custom-call(f32[2,16,64,128]{3,2,1,0:T(8,128)} %get-tuple-element.14.first_hbm, f32[8,16,64,128]{3,2,1,0:T(8,128)} %cot_hbm.1, f32[2,16,64,128]{3,2,1,0:T(8,128)} %cour_hbm.1), custom_call_target="tpu_custom_call" | custom-call | flops 12582912 | bytes 12582912 | tf_op jit(solution)/shard_map/pallas_call | solution.py:170
  27.1 0.6 %collective-permute-done.2.lat_mate_hbm = f32[8,32,128]{2,1,0:T(8,128)S(1)} collective-permute-done((f32[8,32,128]{2,1,0:T(8,128)}, f32[8,32,128]{2,1,0:T(8,128)S(1)}, u32[]{:S(2)}, u32[]{:S(2)}) %collective-permute-start.2) | collective-permute-done | bytes 131104 | tf_op jit(solution)/shard_map/ppermute | solution.py:286
  27.6 0.0 copy-start.2
  27.6 0.0 collective-permute-done.3.lat_far_hbm
  27.6 0.0 copy-start.3
  27.6 0.0 collective-permute-done.lon_mate_hbm
  27.6 0.0 copy-start
  27.7 0.0 collective-permute-done.1.lon_far_hbm
  27.7 0.6 %copy-done.2 = f32[8,32,128]{2,1,0:T(8,128)} copy-done((f32[8,32,128]{2,1,0:T(8,128)}, f32[8,32,128]{2,1,0:T(8,128)S(1)}, u32[]{:S(2)}) %copy-start.2) | copy-done | bytes 131096
  28.3 0.1 copy-done.3
  28.4 0.2 copy-done
  28.5 0.0 copy-start.1
  28.5 0.8 %copy-done.1 = f32[8,2,64,128]{3,2,1,0:T(8,128)} copy-done((f32[8,2,64,128]{3,2,1,0:T(8,128)}, f32[8,2,64,128]{3,2,1,0:T(8,128)S(1)}, u32[]{:S(2)}) %copy-start.1) | copy-done | bytes 524312
  29.3 3.3 %shard_map.66 = f32[8,16,64,128]{3,2,1,0:T(8,128)} custom-call(f32[8,2,64,128]{3,2,1,0:T(8,128)} %copy-done, f32[8,2,64,128]{3,2,1,0:T(8,128)} %copy-done.1, f32[8,32,128]{2,1,0:T(8,128)} %copy-done.2, f32[8,32,128]{2,1,0:T(8,128)} %copy-done.3, f32[8,16,64,128]{3,2,1,0:T(8,128)} %shard_map.65.out_hbm), custom_call_target="tpu_custom_call", output_to_operand_aliasing={{}: (4, {})} | custom-call | tf_op jit(solution)/shard_map/pallas_call | solution.py:243
  (2 shorter events, 0.0 us)
Async XLA Ops:
  9.3 18.3 %collective-permute-start = (f32[8,2,64,128]{3,2,1,0:T(8,128)}, f32[8,2,64,128]{3,2,1,0:T(8,128)S(1)}, u32[]{:S(2)}, u32[]{:S(2)}) collective-permute-start(f32[8,2,64,128]{3,2,1,0:T(8,128)} %get-tuple-element.10), channel_id=1, source_target_pairs={{0,8},{8,0},{16,24},{24,16},{32,40},{40,32},{48,56},{56,48},{64,72... | collective-permute-start | bytes 1572872 | tf_op jit(solution)/shard_map/ppermute | solution.py:283
  9.4 18.3 %collective-permute-start.1 = (f32[8,2,64,128]{3,2,1,0:T(8,128)}, f32[8,2,64,128]{3,2,1,0:T(8,128)S(1)}, u32[]{:S(2)}, u32[]{:S(2)}) collective-permute-start(f32[8,2,64,128]{3,2,1,0:T(8,128)} %get-tuple-element.11), channel_id=1, source_target_pairs={{8,16},{16,8},{24,32},{32,24},{40,48},{48,40},{56,64},{64,56},{72,... | collective-permute-start | bytes 1572872 | tf_op jit(solution)/shard_map/ppermute | solution.py:284
  18.0 9.7 %collective-permute-start.2 = (f32[8,32,128]{2,1,0:T(8,128)}, f32[8,32,128]{2,1,0:T(8,128)S(1)}, u32[]{:S(2)}, u32[]{:S(2)}) collective-permute-start(f32[8,32,128]{2,1,0:T(8,128)} %get-tuple-element.12), channel_id=1, source_target_pairs={{0,1},{1,0},{2,3},{3,2},{4,5},{5,4},{6,7},{7,6},{8,9},{9,8},{10,11... | collective-permute-start | bytes 393224 | tf_op jit(solution)/shard_map/ppermute | solution.py:286
  18.6 9.0 %collective-permute-start.3 = (f32[8,32,128]{2,1,0:T(8,128)}, f32[8,32,128]{2,1,0:T(8,128)S(1)}, u32[]{:S(2)}, u32[]{:S(2)}) collective-permute-start(f32[8,32,128]{2,1,0:T(8,128)} %get-tuple-element.13), channel_id=1, source_target_pairs={{1,2},{2,1},{3,4},{4,3},{5,6},{6,5},{9,10},{10,9},{11,12},{12,11},... | collective-permute-start | bytes 393224 | tf_op jit(solution)/shard_map/ppermute | solution.py:287
  27.6 0.6 %copy-start.2 = (f32[8,32,128]{2,1,0:T(8,128)}, f32[8,32,128]{2,1,0:T(8,128)S(1)}, u32[]{:S(2)}) copy-start(f32[8,32,128]{2,1,0:T(8,128)S(1)} %collective-permute-done.2.lat_mate_hbm) | copy-start | bytes 393220
  27.6 0.7 %copy-start.3 = (f32[8,32,128]{2,1,0:T(8,128)}, f32[8,32,128]{2,1,0:T(8,128)S(1)}, u32[]{:S(2)}) copy-start(f32[8,32,128]{2,1,0:T(8,128)S(1)} %collective-permute-done.3.lat_far_hbm) | copy-start | bytes 393220
  27.6 0.9 %copy-start = (f32[8,2,64,128]{3,2,1,0:T(8,128)}, f32[8,2,64,128]{3,2,1,0:T(8,128)S(1)}, u32[]{:S(2)}) copy-start(f32[8,2,64,128]{3,2,1,0:T(8,128)S(1)} %collective-permute-done.lon_mate_hbm) | copy-start | bytes 1572868
  28.5 0.8 %copy-start.1 = (f32[8,2,64,128]{3,2,1,0:T(8,128)}, f32[8,2,64,128]{3,2,1,0:T(8,128)S(1)}, u32[]{:S(2)}) copy-start(f32[8,2,64,128]{3,2,1,0:T(8,128)S(1)} %collective-permute-done.1.lon_far_hbm) | copy-start | bytes 1572868
